TPU v7x, 512 devices: a whole 4x4x16 slice. The times are simulated.
512 devices in a mesh: dp: 32 (over x, y, core), expert: 16 (over z).
Axes of the slice: x: 4, y: 4, z: 16, core: 2. Of those that a mesh axis runs over, the one named last changes fastest.
Arguments:
- tokens: bfloat16 [4096, 2048], P('dp', 'expert'), may hold values from -6 to 6
- route_weight: bfloat16 [4096, 8], P('dp'), may hold values from 0.049804688 to 0.44921875
- expert_ids: int32 [4096, 8], P('dp'), may hold values from 0 to 127, all different within a row; in each aligned block of 128 rows (0 to 127, 128 to 255, ...) at most 16 rows name the same one
- gate_weight: bfloat16 [16, 6144, 2048], P('expert', 'dp'), may hold values from -0.125 to 0.125
- up_weight: bfloat16 [16, 6144, 2048], P('expert', 'dp'), may hold values from -0.125 to 0.125
- down_weight: bfloat16 [16, 6144, 2048], P('expert', 'dp'), may hold values from -0.21875 to 0.21875
- grad_output: bfloat16 [4096, 2048], P('dp', 'expert'), may hold values from -1.75 to 1.75
Outputs:
- mixed: bfloat16 [4096, 2048], P('dp', 'expert')
- grad_tokens: bfloat16 [4096, 2048], P('dp', 'expert')
- grad_route: float32 [4096, 8], P(('dp', 'expert'))
- grad_gate: bfloat16 [16, 6144, 2048], P('expert', 'dp')
- grad_up: bfloat16 [16, 6144, 2048], P('expert', 'dp')
- grad_down: bfloat16 [16, 6144, 2048], P('expert', 'dp')
Inputs may be any that keep to these rules, and one draw needn't show every extreme that they name: `expert_ids`: each token names 8 different experts; among the 128 tokens of one device's aligned block no expert is named more than 16 times, a bound that some block reaches.
All inputs are finite; a program needn't handle non-finite values.
Results may differ from a plain program's by a relative error of at most 0.015.
Values may be sent and summed in bfloat16 or wider, within the bound.
No kernel may reach another device: no remote copies, remote signals or barrier semaphores. Data moves between devices by JAX's collectives and lax.ppermute only.
A program may use at most 64 MiB of HBM per device.

v0:
```python
import jax
import jax.numpy as jnp
from jax import lax
from jax.sharding import PartitionSpec as P

PIECES = 4


def contract_last(left_side, right_side):
    return lax.dot_general(
        left_side, right_side, (((1,), (1,)), ((), ())), preferred_element_type=jnp.float32
    )


def contract_first(left_side, right_side):
    return lax.dot_general(
        left_side, right_side, (((0,), (0,)), ((), ())), preferred_element_type=jnp.float32
    )


def silu_parts(gate_act):
    sigmoid_val = jax.nn.sigmoid(gate_act)
    return (gate_act * sigmoid_val, sigmoid_val * (1.0 + gate_act * (1.0 - sigmoid_val)))


def expert_forward(slot_rows, slot_scale, gate_piece, up_piece, down_piece):
    gate_act = contract_last(slot_rows, gate_piece)
    up_act = contract_last(slot_rows, up_piece)
    active, silu_slope = silu_parts(gate_act)
    hidden = (active * up_act).astype(jnp.bfloat16)
    partial_out = jnp.dot(hidden, down_piece, preferred_element_type=jnp.float32)
    scaled = (slot_scale.astype(jnp.float32)[:, None] * partial_out).astype(jnp.bfloat16)
    return (scaled, gate_act, up_act, hidden)


def on_device(tokens, route_weight, expert_ids, gate_weight, up_weight, down_weight, grad_output):
    groups = lax.axis_size("expert")
    group_index = lax.axis_index("expert")
    data_size = lax.axis_size("dp")
    exp_local = data_size // PIECES
    tok_local, topk_count = expert_ids.shape
    capacity = min(tok_local, 2 * tok_local * topk_count // (exp_local * groups))
    full_tokens, full_grad = (
        lax.all_gather(tokens, "expert", axis=1, tiled=True),
        lax.all_gather(grad_output, "expert", axis=1, tiled=True),
    )
    feature_width = full_tokens.shape[1]
    gate_piece = gate_weight[0]
    up_piece = up_weight[0]
    down_piece = down_weight[0]
    flat_ids = expert_ids.reshape(-1)
    row_count = flat_ids.shape[0]
    owned_rows = flat_ids // exp_local == group_index
    local_ids = flat_ids % exp_local
    chosen = (
        (local_ids[:, None] == jnp.arange(exp_local, dtype=jnp.int32)[None, :])
        & owned_rows[:, None]
    ).astype(jnp.int32)
    slot_ranks = jnp.sum(chosen * (jnp.cumsum(chosen, axis=0) - 1), axis=1)
    slot_count = exp_local * capacity
    slot_pos = jnp.where(owned_rows, local_ids * capacity + slot_ranks, slot_count)
    row_index = jnp.arange(row_count, dtype=jnp.int32)
    row_of = jnp.zeros((slot_count,), jnp.int32).at[slot_pos].set(row_index, mode="drop")
    slot_live = (
        jnp.zeros((slot_count,), jnp.int32).at[slot_pos].set(jnp.ones_like(row_index), mode="drop")
    )
    token_of = row_of // topk_count
    keep_mask = slot_live.astype(tokens.dtype)[:, None]
    slot_weight = route_weight.reshape(-1)[row_of] * slot_live.astype(route_weight.dtype)

    def spread(values):
        trailing = values.shape[1:]
        grouped = values.reshape((exp_local, 1, capacity) + trailing)
        return jnp.broadcast_to(grouped, (exp_local, PIECES, capacity) + trailing).reshape(
            (data_size, capacity) + trailing
        )

    send_rows = spread(full_tokens[token_of] * keep_mask)
    send_weight = spread(slot_weight)
    send_grads = spread(full_grad[token_of] * keep_mask)
    recv_grads = None
    recv_scale = None
    recv_rows, recv_weight = (
        lax.all_to_all(send_rows, "dp", split_axis=0, concat_axis=0, tiled=True),
        lax.all_to_all(send_weight, "dp", split_axis=0, concat_axis=0, tiled=True),
    )
    scaled, gate_act, up_act, hidden = expert_forward(
        recv_rows.reshape(-1, feature_width),
        recv_weight.reshape(-1),
        gate_piece,
        up_piece,
        down_piece,
    )
    returned = lax.all_to_all(
        scaled.reshape(data_size, capacity, feature_width),
        "dp",
        split_axis=0,
        concat_axis=0,
        tiled=True,
    )
    slot_rows = recv_rows.reshape(-1, feature_width)
    wide_token = spread(token_of).reshape(-1)
    wide_live = spread(slot_live).reshape(-1)
    wide_row = spread(row_of).reshape(-1)
    token_place = (
        (wide_token[None, :] == jnp.arange(tok_local, dtype=jnp.int32)[:, None])
        & (wide_live[None, :] > 0)
    ).astype(jnp.bfloat16)
    mixed_sum = jnp.dot(
        token_place, returned.reshape(-1, feature_width), preferred_element_type=jnp.float32
    )
    recv_grads, recv_scale = (
        lax.all_to_all(send_grads, "dp", split_axis=0, concat_axis=0, tiled=True),
        lax.all_to_all(send_weight, "dp", split_axis=0, concat_axis=0, tiled=True),
    )
    active, silu_slope = silu_parts(gate_act)
    slot_grads = recv_grads.reshape(-1, feature_width)
    weight_wide = recv_scale.reshape(-1).astype(jnp.float32)[:, None]
    into_hidden = contract_last(slot_grads, down_piece)
    route_terms = jnp.sum(into_hidden * hidden.astype(jnp.float32), axis=1).astype(jnp.bfloat16)
    hidden_grad = weight_wide * into_hidden
    gate_grad = (hidden_grad * up_act * silu_slope).astype(jnp.bfloat16)
    up_grad = (hidden_grad * active).astype(jnp.bfloat16)
    row_grad = (
        jnp.dot(gate_grad, gate_piece, preferred_element_type=jnp.float32)
        + jnp.dot(up_grad, up_piece, preferred_element_type=jnp.float32)
    ).astype(jnp.bfloat16)
    scaled_grad = (weight_wide * slot_grads.astype(jnp.float32)).astype(jnp.bfloat16)
    grad_gate = contract_first(gate_grad, slot_rows).astype(jnp.bfloat16)[None]
    grad_up = contract_first(up_grad, slot_rows).astype(jnp.bfloat16)[None]
    grad_down = contract_first(hidden, scaled_grad).astype(jnp.bfloat16)[None]
    back_rows, back_terms = (
        lax.all_to_all(
            row_grad.reshape(data_size, capacity, feature_width),
            "dp",
            split_axis=0,
            concat_axis=0,
            tiled=True,
        ),
        lax.all_to_all(
            route_terms.reshape(data_size, capacity), "dp", split_axis=0, concat_axis=0, tiled=True
        ),
    )
    token_sum = jnp.dot(
        token_place, back_rows.reshape(-1, feature_width), preferred_element_type=jnp.float32
    )
    row_place = (
        (wide_row[None, :] == jnp.arange(row_count, dtype=jnp.int32)[:, None])
        & (wide_live[None, :] > 0)
    ).astype(jnp.bfloat16)
    route_sum = jnp.dot(
        row_place, back_terms.reshape(-1), preferred_element_type=jnp.float32
    ).reshape(tok_local, topk_count)
    mixed_part, token_part, route_part = (
        lax.psum_scatter(mixed_sum, "expert", scatter_dimension=1, tiled=True),
        lax.psum_scatter(token_sum, "expert", scatter_dimension=1, tiled=True),
        lax.psum_scatter(route_sum, "expert", scatter_dimension=0, tiled=True),
    )
    return (
        mixed_part.astype(jnp.bfloat16),
        token_part.astype(jnp.bfloat16),
        route_part,
        grad_gate,
        grad_up,
        grad_down,
    )


def solution(mesh):
    return jax.shard_map(
        on_device,
        mesh=mesh,
        in_specs=(
            P("dp", "expert"),
            P("dp", None),
            P("dp", None),
            P("expert", "dp", None),
            P("expert", "dp", None),
            P("expert", "dp", None),
            P("dp", "expert"),
        ),
        out_specs=(
            P("dp", "expert"),
            P("dp", "expert"),
            P(("dp", "expert"), None),
            P("expert", "dp", None),
            P("expert", "dp", None),
            P("expert", "dp", None),
        ),
        check_vma=False,
    )
```

profile of v0, /device:TPU:2, one launch (start us, length us, event | category | flops | bytes accessed | tf_op | source)
XLA Modules:
  0.0 366.5 jit_solution(7416273939957925832)
XLA Ops:
  7.2 0.9 copy.22
  8.2 0.1 reshape.318
  8.4 0.8 copy.25
  9.2 0.1 reshape.322
  9.3 2.3 reduce-window.6
  11.6 0.3 slice_reduce_fusion
  11.9 0.2 reduce-window.9
  12.2 4.3 %scatter_custom_fusion.1 = s32[128]{0:T(128)S(1)} fusion(s32[1024]{0:T(1024)S(1)} %bitcast.84, s32[1024]{0:T(1024)S(1)} %ne.90, s32[]{:T(128)} %constant.53.clone.1), kind=kCustom, calls=%fused_computation.95 | custom fusion | bytes 516 | tf_op jit(solution)/shard_map/scatter | solution.py:65
  16.5 4.3 %scatter_custom_fusion = s32[128]{0:T(128)S(1)} fusion(s32[1024]{0:T(1024)S(1)} %bitcast.85, s32[1024]{0:T(1024)S(1)} %iota.26, s32[]{:T(128)} %constant.53.clone.1), kind=kCustom, calls=%fused_computation.97 | custom fusion | bytes 516 | tf_op jit(solution)/shard_map/scatter | solution.py:63
  20.9 1.3 gather_fusion
  22.2 0.6 copy.26
  22.9 9.4 %all-to-all-start = ((bf16[32,1,16]{2,1,0:T(2,128)(2,1)}), bf16[32,1,16]{2,1,0:T(2,128)(2,1)S(1)}, u32[]{:S(2)}, u32[]{:S(2)}) async-start(bf16[32,1,16]{2,1,0:T(2,128)(2,1)} %copy.26), calls=%async_computation | async-start | bytes 32768 | tf_op jit(solution)/shard_map/all_to_all | solution.py:85
  32.4 37.0 %all_gather.6 = bf16[128,2048]{1,0:T(8,128)(2,1)S(1)} all-gather(bf16[128,128]{1,0:T(8,128)(2,1)} %param.7), channel_id=1, replica_groups=mesh['dp'=32,'expert'=16] {'expert'}, dimensions={1}, use_global_device_ids=true | all-gather | bytes 557056 | tf_op jit(solution)/shard_map/all_gather | solution.py:44
  69.4 29.3 %all_gather.7 = bf16[128,2048]{1,0:T(8,128)(2,1)S(1)} all-gather(bf16[128,128]{1,0:T(8,128)(2,1)} %param.13), channel_id=1, replica_groups=mesh['dp'=32,'expert'=16] {'expert'}, dimensions={1}, use_global_device_ids=true | all-gather | bytes 557056 | tf_op jit(solution)/shard_map/all_gather | solution.py:45
  98.7 0.9 gather_fusion.1
  99.6 0.9 gather_fusion.2
  100.6 0.1 broadcast_multiply_fusion.1
  100.7 0.2 broadcast_in_dim.75
  101.0 32.6 %all_to_all.36 = bf16[32,16,2048]{2,1,0:T(8,128)(2,1)S(1)} all-to-all(bf16[32,16,2048]{2,1,0:T(8,128)(2,1)S(1)} %bitcast.76), channel_id=1, replica_groups=mesh['dp'=32,'expert'=16] {'dp'}, dimensions={0} | all-to-all | bytes 4194304 | tf_op jit(solution)/shard_map/all_to_all | solution.py:84
  133.6 1.6 broadcast_in_dim.76
  135.2 7.0 %all-to-all-start.3 = ((bf16[32,16,2048]{2,1,0:T(8,128)(2,1)}), bf16[32,16,2048]{2,1,0:T(8,128)(2,1)}, u32[]{:S(2)}, u32[]{:S(2)}) async-start(bf16[32,16,2048]{2,1,0:T(8,128)(2,1)} %bitcast.75), calls=%async_computation.4 | async-start | bytes 4194304 | tf_op jit(solution)/shard_map/all_to_all | solution.py:113
  142.3 2.8 fusion.12
  145.1 1.6 fusion.16
  146.7 21.4 %all-to-all-done.3 = bf16[32,16,2048]{2,1,0:T(8,128)(2,1)} async-done(((bf16[32,16,2048]{2,1,0:T(8,128)(2,1)}), bf16[32,16,2048]{2,1,0:T(8,128)(2,1)}, u32[]{:S(2)}, u32[]{:S(2)}) %all-to-all-start.3) | async-done | bytes 2097184 | tf_op jit(solution)/shard_map/all_to_all | solution.py:113
  168.1 2.7 multiply_reduce_fusion
  170.9 0.7 copy-done.3
  171.5 2.0 multiply_convert_fusion.1
  173.6 7.7 %all-to-all-start.2 = ((bf16[32,16,2048]{2,1,0:T(8,128)(2,1)}), bf16[32,16,2048]{2,1,0:T(8,128)(2,1)}, u32[]{:S(2)}, u32[]{:S(2)}) async-start(bf16[32,16,2048]{2,1,0:T(8,128)(2,1)} %bitcast.79), calls=%async_computation.2 | async-start | bytes 4194304 | tf_op jit(solution)/shard_map/all_to_all | solution.py:94
  181.7 2.0 fusion.14
  183.6 2.1 add_convert_fusion
  185.7 21.5 %all-to-all-done.2 = bf16[32,16,2048]{2,1,0:T(8,128)(2,1)} async-done(((bf16[32,16,2048]{2,1,0:T(8,128)(2,1)}), bf16[32,16,2048]{2,1,0:T(8,128)(2,1)}, u32[]{:S(2)}, u32[]{:S(2)}) %all-to-all-start.2) | async-done | bytes 2097184 | tf_op jit(solution)/shard_map/all_to_all | solution.py:94
  207.2 7.7 %all-to-all-start.4 = ((bf16[32,16,2048]{2,1,0:T(8,128)(2,1)}), bf16[32,16,2048]{2,1,0:T(8,128)(2,1)}, u32[]{:S(2)}, u32[]{:S(2)}) async-start(bf16[32,16,2048]{2,1,0:T(8,128)(2,1)} %bitcast.74), calls=%async_computation.5 | async-start | bytes 4194304 | tf_op jit(solution)/shard_map/all_to_all | solution.py:133
  215.0 3.1 fusion.22
  218.1 0.2 reduce-scatter.5.cloned.1.call-start
  218.3 22.6 %all-to-all-done.4 = bf16[32,16,2048]{2,1,0:T(8,128)(2,1)} async-done(((bf16[32,16,2048]{2,1,0:T(8,128)(2,1)}), bf16[32,16,2048]{2,1,0:T(8,128)(2,1)}, u32[]{:S(2)}, u32[]{:S(2)}) %all-to-all-start.4) | async-done | bytes 2097184 | tf_op jit(solution)/shard_map/all_to_all | solution.py:133
  240.9 3.0 fusion.20
  244.1 1.3 dynamic-slice
  246.1 0.7 convert_element_type.95
  246.8 6.8 %all-to-all-start.5 = ((bf16[32,1,16]{2,1,0:T(2,128)(2,1)}), bf16[32,1,16]{2,1,0:T(2,128)(2,1)S(1)}, u32[]{:S(2)}, u32[]{:S(2)}) async-start(bf16[32,1,16]{2,1,0:T(2,128)(2,1)} %convert_element_type.95), calls=%async_computation.7 | async-start | bytes 32768 | tf_op jit(solution)/shard_map/all_to_all | solution.py:140
  253.6 1.5 fusion
  255.1 3.2 fusion.2
  258.3 1.5 fusion.1
  259.9 2.5 fusion.4
  262.4 54.3 %all-reduce = f32[128,8]{1,0:T(8,128)S(1)} all-reduce(f32[128,8]{1,0:T(8,128)S(1)} %bitcast.80), channel_id=4, replica_groups=mesh['dp'=32,'expert'=16] {'expert'}, use_global_device_ids=true, to_apply=%region_8.9.clone | all-reduce | flops 1024 | bytes 8192
  316.7 0.6 constant_dynamic-slice_fusion
  317.3 1.5 convert_element_type.81
  318.7 39.4 %reduce-scatter.5.cloned.1.call-done = f32[128,128]{1,0:T(8,128)} async-done(((f32[128,2048]{1,0:T(8,128)}), f32[128,128]{1,0:T(8,128)}) %reduce-scatter.5.cloned.1.call-update) | async-done | bytes 65552 | tf_op jit(solution)/shard_map/reduce_scatter | solution.py:156
  358.2 1.5 convert_element_type.85
  (50 shorter events, 1.6 us)
Async XLA Ops:
  7.2 161.0 %copy-start = (bf16[1,192,2048]{2,1,0:T(8,128)(2,1)S(1)}, bf16[1,192,2048]{2,1,0:T(8,128)(2,1)}, u32[]{:S(2)}) copy-start(bf16[1,192,2048]{2,1,0:T(8,128)(2,1)} %param.12) | copy-start | bytes 2359300
  22.9 77.9 %all-to-all-start = ((bf16[32,1,16]{2,1,0:T(2,128)(2,1)}), bf16[32,1,16]{2,1,0:T(2,128)(2,1)S(1)}, u32[]{:S(2)}, u32[]{:S(2)}) async-start(bf16[32,1,16]{2,1,0:T(2,128)(2,1)} %copy.26), calls=%async_computation | async-start | bytes 32768 | tf_op jit(solution)/shard_map/all_to_all | solution.py:85
  135.2 33.0 %all-to-all-start.3 = ((bf16[32,16,2048]{2,1,0:T(8,128)(2,1)}), bf16[32,16,2048]{2,1,0:T(8,128)(2,1)}, u32[]{:S(2)}, u32[]{:S(2)}) async-start(bf16[32,16,2048]{2,1,0:T(8,128)(2,1)} %bitcast.75), calls=%async_computation.4 | async-start | bytes 4194304 | tf_op jit(solution)/shard_map/all_to_all | solution.py:113
  142.3 2.8 copy-start.1
  170.9 0.7 copy-start.3
  173.6 33.6 %all-to-all-start.2 = ((bf16[32,16,2048]{2,1,0:T(8,128)(2,1)}), bf16[32,16,2048]{2,1,0:T(8,128)(2,1)}, u32[]{:S(2)}, u32[]{:S(2)}) async-start(bf16[32,16,2048]{2,1,0:T(8,128)(2,1)} %bitcast.79), calls=%async_computation.2 | async-start | bytes 4194304 | tf_op jit(solution)/shard_map/all_to_all | solution.py:94
  181.7 2.0 copy-start.2
  207.2 33.6 %all-to-all-start.4 = ((bf16[32,16,2048]{2,1,0:T(8,128)(2,1)}), bf16[32,16,2048]{2,1,0:T(8,128)(2,1)}, u32[]{:S(2)}, u32[]{:S(2)}) async-start(bf16[32,16,2048]{2,1,0:T(8,128)(2,1)} %bitcast.74), calls=%async_computation.5 | async-start | bytes 4194304 | tf_op jit(solution)/shard_map/all_to_all | solution.py:133
  214.9 102.4 %reduce-scatter.3.cloned.1.call-start = ((), (), s32[]{:S(2)}) async-start(), calls=%async_computation.8 | async-start | bytes 1114112 | tf_op jit(solution)/shard_map/reduce_scatter | solution.py:155
  218.1 140.1 %reduce-scatter.5.cloned.1.call-start = ((), (), s32[]{:S(2)}) async-start(), calls=%async_computation.9 | async-start | bytes 1114112 | tf_op jit(solution)/shard_map/reduce_scatter | solution.py:156
  246.8 13.0 %all-to-all-start.5 = ((bf16[32,1,16]{2,1,0:T(2,128)(2,1)}), bf16[32,1,16]{2,1,0:T(2,128)(2,1)S(1)}, u32[]{:S(2)}, u32[]{:S(2)}) async-start(bf16[32,1,16]{2,1,0:T(2,128)(2,1)} %convert_element_type.95), calls=%async_computation.7 | async-start | bytes 32768 | tf_op jit(solution)/shard_map/all_to_all | solution.py:140
  253.6 1.5 copy-start.4
Sparse Core Ops, SparseCore 0:
  218.5 67.8 reduce-scatter.2
  289.3 68.8 reduce-scatter.4
where the time goes:
time: 367 us; the launch traced here: 366 us
  blocking collectives  153 us (42%)
  waiting for transfers between devices  105 us (29%)
  starting transfers between devices  38.9 us (11%)
  matrix products  27.9 us (8%)
  local copies, waits for them, and re-layouts  20.7 us (6%)
  between operations  15 us (4%)
  other arithmetic  5.84 us (2%)
    unnamed x1, blocking collectives  54.3 us
    reduce_scatter x1, waiting for transfers between devices, on_device(): lax.psum_scatter(token_sum, 'expert', scatter_dimension=1, tiled=True)  39.4 us
    all_gather x1, blocking collectives, on_device(): lax.all_gather(tokens, 'expert', axis=1, tiled=True)  37 us
    all_to_all x1, blocking collectives, on_device(): lax.all_to_all(send_rows, 'dp', split_axis=0, concat_axis=0, tiled=True)  32.6 us
    all_gather x1, blocking collectives, on_device(): lax.all_gather(grad_output, 'expert', axis=1, tiled=True)  29.3 us
    all_to_all x1, waiting for transfers between devices, on_device(): lax.all_to_all(row_grad.reshape(data_size, capacity, feature_width), 'dp'...  22.6 us
    all_to_all x1, waiting for transfers between devices, on_device(): lax.all_to_all(scaled.reshape(data_size, capacity, feature_width), 'dp',...  21.5 us
    all_to_all x1, waiting for transfers between devices, on_device(): lax.all_to_all(send_grads, 'dp', split_axis=0, concat_axis=0, tiled=True)  21.4 us
  transfers between devices with their start and end apart: 7, of which 5 were waited for; matrix products, arithmetic and copies ran while one was open for 8% of the time, Pallas kernels for 0%

commit v1 on v0

v1 whole, which is shorter than its diff:
```python
import jax
import jax.numpy as jnp
from jax import lax
from jax.sharding import PartitionSpec as P

PIECES = 4
PAD = 128


def contract_last(left_side, right_side):
    return lax.dot_general(
        left_side, right_side, (((1,), (1,)), ((), ())), preferred_element_type=jnp.float32
    )


def contract_first(left_side, right_side):
    return lax.dot_general(
        left_side, right_side, (((0,), (0,)), ((), ())), preferred_element_type=jnp.float32
    )


def silu_parts(gate_act):
    sigmoid_val = jax.nn.sigmoid(gate_act)
    return (gate_act * sigmoid_val, sigmoid_val * (1.0 + gate_act * (1.0 - sigmoid_val)))


def column_block(values, dtype):
    lane = jnp.arange(PAD, dtype=jnp.int32)[None, :] == 0
    return jnp.where(lane, values.astype(dtype)[:, None], jnp.zeros((), dtype))


def on_device(tokens, route_weight, expert_ids, gate_weight, up_weight, down_weight, grad_output):
    groups = lax.axis_size("expert")
    group_index = lax.axis_index("expert")
    data_size = lax.axis_size("dp")
    exp_local = data_size // PIECES
    tok_local, topk_count = expert_ids.shape
    capacity = min(tok_local, 2 * tok_local * topk_count // (exp_local * groups))
    part_width = tokens.shape[1]
    both = jnp.concatenate([tokens, grad_output], axis=1)
    gathered = lax.all_gather(both, "expert", axis=0, tiled=False)
    gathered = gathered.reshape(groups, tok_local, 2, part_width)
    full_both = jnp.transpose(gathered, (1, 2, 0, 3)).reshape(tok_local, 2 * groups * part_width)
    feature_width = groups * part_width
    gate_piece = gate_weight[0]
    up_piece = up_weight[0]
    down_piece = down_weight[0]
    flat_ids = expert_ids.reshape(-1)
    row_count = flat_ids.shape[0]
    owned_rows = flat_ids // exp_local == group_index
    local_ids = flat_ids % exp_local
    chosen = (
        (local_ids[:, None] == jnp.arange(exp_local, dtype=jnp.int32)[None, :])
        & owned_rows[:, None]
    ).astype(jnp.int32)
    slot_ranks = jnp.sum(chosen * (jnp.cumsum(chosen, axis=0) - 1), axis=1)
    slot_count = exp_local * capacity
    slot_pos = jnp.where(owned_rows, local_ids * capacity + slot_ranks, slot_count)
    row_index = jnp.arange(row_count, dtype=jnp.int32)
    row_of = jnp.zeros((slot_count,), jnp.int32).at[slot_pos].set(row_index, mode="drop")
    slot_live = (
        jnp.zeros((slot_count,), jnp.int32).at[slot_pos].set(jnp.ones_like(row_index), mode="drop")
    )
    token_of = row_of // topk_count
    keep_mask = slot_live.astype(tokens.dtype)[:, None]
    slot_weight = route_weight.reshape(-1)[row_of] * slot_live.astype(route_weight.dtype)

    def spread(values):
        trailing = values.shape[1:]
        grouped = values.reshape((exp_local, 1, capacity) + trailing)
        return jnp.broadcast_to(grouped, (exp_local, PIECES, capacity) + trailing).reshape(
            (data_size, capacity) + trailing
        )

    send_buf = jnp.concatenate(
        [full_both[token_of] * keep_mask, column_block(slot_weight, tokens.dtype)], axis=1
    )
    recv_buf = lax.all_to_all(spread(send_buf), "dp", split_axis=0, concat_axis=0, tiled=True)
    recv_buf = recv_buf.reshape(-1, 2 * feature_width + PAD)
    slot_rows = recv_buf[:, :feature_width]
    slot_grads = recv_buf[:, feature_width : 2 * feature_width]
    slot_scale = recv_buf[:, 2 * feature_width]
    weight_wide = slot_scale.astype(jnp.float32)[:, None]

    gate_act = contract_last(slot_rows, gate_piece)
    up_act = contract_last(slot_rows, up_piece)
    active, silu_slope = silu_parts(gate_act)
    hidden = (active * up_act).astype(jnp.bfloat16)
    partial_out = jnp.dot(hidden, down_piece, preferred_element_type=jnp.float32)
    scaled = (weight_wide * partial_out).astype(jnp.bfloat16)

    into_hidden = contract_last(slot_grads, down_piece)
    route_terms = jnp.sum(into_hidden * hidden.astype(jnp.float32), axis=1).astype(jnp.bfloat16)
    hidden_grad = weight_wide * into_hidden
    gate_grad = (hidden_grad * up_act * silu_slope).astype(jnp.bfloat16)
    up_grad = (hidden_grad * active).astype(jnp.bfloat16)
    row_grad = (
        jnp.dot(gate_grad, gate_piece, preferred_element_type=jnp.float32)
        + jnp.dot(up_grad, up_piece, preferred_element_type=jnp.float32)
    ).astype(jnp.bfloat16)
    scaled_grad = (weight_wide * slot_grads.astype(jnp.float32)).astype(jnp.bfloat16)
    grad_gate = contract_first(gate_grad, slot_rows).astype(jnp.bfloat16)[None]
    grad_up = contract_first(up_grad, slot_rows).astype(jnp.bfloat16)[None]
    grad_down = contract_first(hidden, scaled_grad).astype(jnp.bfloat16)[None]

    back_buf = jnp.concatenate([scaled, row_grad, column_block(route_terms, jnp.bfloat16)], axis=1)
    back = lax.all_to_all(
        back_buf.reshape(data_size, capacity, 2 * feature_width + PAD),
        "dp",
        split_axis=0,
        concat_axis=0,
        tiled=True,
    ).reshape(-1, 2 * feature_width + PAD)

    wide_token = spread(token_of).reshape(-1)
    wide_live = spread(slot_live).reshape(-1)
    wide_row = spread(row_of).reshape(-1)
    token_place = (
        (wide_token[None, :] == jnp.arange(tok_local, dtype=jnp.int32)[:, None])
        & (wide_live[None, :] > 0)
    ).astype(jnp.bfloat16)
    both_sum = jnp.dot(
        token_place, back[:, : 2 * feature_width], preferred_element_type=jnp.float32
    )
    row_place = (
        (wide_row[None, :] == jnp.arange(row_count, dtype=jnp.int32)[:, None])
        & (wide_live[None, :] > 0)
    ).astype(jnp.bfloat16)
    route_sum = jnp.dot(
        row_place, back[:, 2 * feature_width], preferred_element_type=jnp.float32
    )
    planes = jnp.transpose(
        both_sum.reshape(tok_local, 2, groups, part_width), (0, 2, 1, 3)
    ).reshape(tok_local, groups, 2 * part_width)
    route_row = jnp.pad(route_sum.reshape(groups, -1), ((0, 0), (0, 2 * part_width - row_count // groups)))
    packed = jnp.concatenate([planes, route_row[None]], axis=0).reshape(tok_local + 1, -1)
    reduced = lax.psum_scatter(packed, "expert", scatter_dimension=1, tiled=True)
    mixed_part = reduced[:tok_local, :part_width]
    token_part = reduced[:tok_local, part_width:]
    route_part = reduced[tok_local, : row_count // groups].reshape(-1, topk_count)
    return (
        mixed_part.astype(jnp.bfloat16),
        token_part.astype(jnp.bfloat16),
        route_part,
        grad_gate,
        grad_up,
        grad_down,
    )


def solution(mesh):
    return jax.shard_map(
        on_device,
        mesh=mesh,
        in_specs=(
            P("dp", "expert"),
            P("dp", None),
            P("dp", None),
            P("expert", "dp", None),
            P("expert", "dp", None),
            P("expert", "dp", None),
            P("dp", "expert"),
        ),
        out_specs=(
            P("dp", "expert"),
            P("dp", "expert"),
            P(("dp", "expert"), None),
            P("expert", "dp", None),
            P("expert", "dp", None),
            P("expert", "dp", None),
        ),
        check_vma=False,
    )
```

time: 367 us -> 311 us (0.85)
  blocking collectives: 153 us -> 58.9 us
  waiting for transfers between devices: 105 us -> 177 us
  starting transfers between devices: 38.9 us -> 6.2 us
  matrix products: 27.9 us -> 17.7 us
  local copies, waits for them, and re-layouts: 20.7 us -> 26.8 us
    all_gather x2 -> x0, blocking collectives: 66.3 us -> none  [the longest x1 37 us: on_device(): lax.all_gather(tokens, 'expert', axis=1, tiled=True)]
    all_gather x0 -> x1, waiting for transfers between devices: none -> 61.9 us  [on_device(): gathered = lax.all_gather(both, 'expert', axis=0, tiled=False)]
    unnamed x1 -> x0, blocking collectives: 54.3 us -> none
    all_to_all x5 -> x1, starting transfers between devices: 38.6 us -> 5.93 us  [on_device(): lax.all_to_all(back_buf.reshape(data_size, capacity, 2 * feature_width +...]
    all_to_all x1, blocking collectives: 32.6 us -> 58.9 us  [on_device(): lax.all_to_all(spread(send_buf), 'dp', split_axis=0, concat_axis=0, tiled...]
    reduce_scatter x2 -> x1, waiting for transfers between devices: 39.4 us -> 64.3 us  [on_device(): lax.psum_scatter(packed, 'expert', scatter_dimension=1, tiled=True)]
    all_to_all x5 -> x1, waiting for transfers between devices: 65.6 us -> 50.6 us  [on_device(): lax.all_to_all(back_buf.reshape(data_size, capacity, 2 * feature_width +...]
    dot_general x4 -> x3, matrix products: 10.6 us -> 4.24 us  [the longest x1 2.9 us: on_device(): jnp.dot(token_place, back[:, :2 * feature_width], preferred_element_type=...]
  transfers between devices with their start and end apart: 7 -> 3, of which waited for: 5 -> 3; matrix products, arithmetic and copies ran while one was open for 8% -> 8% of each run, Pallas kernels for 0% -> 0%
where the time goes in v1:
time: 311 us; the launch traced here: 310 us
  waiting for transfers between devices  177 us (57%)
  blocking collectives  58.9 us (19%)
  local copies, waits for them, and re-layouts  26.8 us (9%)
  matrix products  17.7 us (6%)
  between operations  14.4 us (5%)
  other arithmetic  9.39 us (3%)
  starting transfers between devices  6.2 us (2%)
    reduce_scatter x1, waiting for transfers between devices, on_device(): lax.psum_scatter(packed, 'expert', scatter_dimension=1, tiled=True)  64.3 us
    all_gather x1, waiting for transfers between devices, on_device(): gathered = lax.all_gather(both, 'expert', axis=0, tiled=False)  61.9 us
    all_to_all x1, blocking collectives, on_device(): lax.all_to_all(spread(send_buf), 'dp', split_axis=0, concat_axis=0, tiled...  58.9 us
    all_to_all x1, waiting for transfers between devices, on_device(): lax.all_to_all(back_buf.reshape(data_size, capacity, 2 * feature_width +...  50.6 us
    dot_general x3, matrix products, contract_first(): lax.dot_general(left_side, right_side, (((0,), (0,)), ((), ())), preferre...  9.27 us
  transfers between devices with their start and end apart: 3, of which 3 were waited for; matrix products, arithmetic and copies ran while one was open for 8% of the time, Pallas kernels for 0%

profile of v1, /device:TPU:2, one launch (start us, length us, event | category | flops | bytes accessed | tf_op | source)
XLA Modules:
  0.0 310.2 jit_solution(7784164541367940357)
XLA Ops:
  7.2 1.5 pad_maximum_fusion.2
  8.7 0.8 copy.22
  9.7 2.3 reduce-window.6
  11.9 0.3 slice_reduce_fusion.1
  12.3 0.1 reshape.304
  12.4 0.8 copy.26
  13.2 0.1 reshape.310
  13.3 0.2 reduce-window.9
  13.7 4.3 %scatter_custom_fusion.1 = s32[128]{0:T(128)S(1)} fusion(s32[1024]{0:T(1024)S(1)} %bitcast.91, s32[1024]{0:T(1024)S(1)} %ne.90, s32[]{:T(128)} %constant.56.clone.1), kind=kCustom, calls=%fused_computation.108 | custom fusion | bytes 516 | tf_op jit(solution)/shard_map/scatter | solution.py:62
  18.0 4.3 %scatter_custom_fusion = s32[128]{0:T(128)S(1)} fusion(s32[1024]{0:T(1024)S(1)} %bitcast.92, s32[1024]{0:T(1024)S(1)} %iota.34, s32[]{:T(128)} %constant.56.clone.1), kind=kCustom, calls=%fused_computation.110 | custom fusion | bytes 516 | tf_op jit(solution)/shard_map/scatter | solution.py:60
  22.4 1.3 gather_fusion.1
  23.9 61.9 %all-gather.3.cloned.1.call-done = bf16[2048,256]{1,0:T(8,128)(2,1)} async-done(((bf16[128,256]{1,0:T(8,128)(2,1)}), bf16[2048,256]{1,0:T(8,128)(2,1)}) %all-gather.3.cloned.1.call-update) | async-done | bytes 1048592 | tf_op jit(solution)/shard_map/all_gather | solution.py:41
  85.8 1.3 reshape.308
  87.2 1.2 copy.25
  88.4 0.5 copy.35
  88.9 1.2 gather_fusion
  90.1 0.1 broadcast_multiply_fusion
  90.3 0.3 broadcast_in_dim.113
  90.6 58.9 %all_to_all.10 = bf16[32,16,4224]{2,1,0:T(8,128)(2,1)S(1)} all-to-all(bf16[32,16,4224]{2,1,0:T(8,128)(2,1)S(1)} %bitcast.76), channel_id=1, replica_groups=mesh['dp'=32,'expert'=16] {'dp'}, dimensions={0} | all-to-all | bytes 8650752 | tf_op jit(solution)/shard_map/all_to_all | solution.py:78
  149.5 0.1 convert_reduce_fusion
  149.6 0.8 fusion.15
  150.5 0.7 copy-done.2
  151.2 0.8 fusion.17
  152.0 1.0 multiply_reduce_fusion
  153.0 0.1 broadcast_select_fusion
  153.2 0.7 multiply_convert_fusion.1
  153.9 0.8 fusion.26
  154.7 0.8 add_convert_fusion
  155.4 2.2 pad_maximum_fusion
  157.7 5.9 %all-to-all-start.1 = ((bf16[32,16,4224]{2,1,0:T(8,128)(2,1)}), bf16[32,16,4224]{2,1,0:T(8,128)(2,1)}, u32[]{:S(2)}, u32[]{:S(2)}) async-start(bf16[32,16,4224]{2,1,0:T(8,128)(2,1)} %bitcast.75), calls=%async_computation.1 | async-start | bytes 8650752 | tf_op jit(solution)/shard_map/all_to_all | solution.py:107
  163.6 0.2 reduce-scatter.2.cloned.1.call-start
  164.2 0.1 eq.112
  164.4 50.6 %all-to-all-done.1 = bf16[32,16,4224]{2,1,0:T(8,128)(2,1)} async-done(((bf16[32,16,4224]{2,1,0:T(8,128)(2,1)}), bf16[32,16,4224]{2,1,0:T(8,128)(2,1)}, u32[]{:S(2)}, u32[]{:S(2)}) %all-to-all-start.1) | async-done | bytes 4325408 | tf_op jit(solution)/shard_map/all_to_all | solution.py:107
  215.0 1.0 slice_reduce_fusion
  216.0 2.9 fusion.10
  218.9 0.4 copy.31
  219.3 2.4 copy.27
  221.7 2.9 concatenate.21
  224.7 0.6 fusion.6
  225.3 1.6 pad_maximum_fusion.1
  226.9 3.1 fusion.2
  229.9 3.1 fusion.3
  233.0 3.2 %fusion.4 = bf16[1,192,2048]{2,1,0:T(8,128)(2,1)} fusion(bf16[512,192]{0,1:T(8,128)(2,1)S(1)} %get-tuple-element.7, f32[512]{0:T(512)S(1)} %convert_reduce_fusion, bf16[512,4224]{1,0:T(8,128)(2,1)} %bitcast.84), kind=kOutput, calls=%fused_computation.15 | convolution fusion | flops 406192128 | bytes 3082240 | tf_op jit(solution)/shard_map/dot_general | solution.py:17
  236.2 64.3 %reduce-scatter.2.cloned.1.call-done = f32[129,256]{1,0:T(8,128)} async-done(((f32[129,4096]{1,0:T(8,128)}), f32[129,256]{1,0:T(8,128)}) %reduce-scatter.2.cloned.1.call-update) | async-done | bytes 132112 | tf_op jit(solution)/shard_map/reduce_scatter | solution.py:137
  300.4 0.9 convert.5
  301.4 0.6 fusion.51
  302.0 0.7 slice_reduce_fusion.2
  302.7 0.7 reshape_squeeze.3
  (44 shorter events, 1.3 us)
Async XLA Ops:
  7.2 144.9 %copy-start = (bf16[1,192,2048]{2,1,0:T(8,128)(2,1)S(1)}, bf16[1,192,2048]{2,1,0:T(8,128)(2,1)}, u32[]{:S(2)}) copy-start(bf16[1,192,2048]{2,1,0:T(8,128)(2,1)} %param.12) | copy-start | bytes 2359300
  7.2 78.6 %all-gather.3.cloned.1.call-start = ((), (), s32[]{:S(2)}) async-start(), calls=%async_computation.4 | async-start | bytes 1114112 | tf_op jit(solution)/shard_map/all_gather | solution.py:41
  90.6 59.0 %copy-start.3 = (bf16[1,192,2048]{2,1,0:T(8,128)(2,1)S(1)}, bf16[1,192,2048]{2,1,0:T(8,128)(2,1)}, u32[]{:S(2)}) copy-start(bf16[1,192,2048]{2,1,0:T(8,128)(2,1)} %param.11) | copy-start | bytes 2359300
  149.5 2.5 copy-start.1
  149.5 1.7 copy-start.2
  157.7 57.3 %all-to-all-start.1 = ((bf16[32,16,4224]{2,1,0:T(8,128)(2,1)}), bf16[32,16,4224]{2,1,0:T(8,128)(2,1)}, u32[]{:S(2)}, u32[]{:S(2)}) async-start(bf16[32,16,4224]{2,1,0:T(8,128)(2,1)} %bitcast.75), calls=%async_computation.1 | async-start | bytes 8650752 | tf_op jit(solution)/shard_map/all_to_all | solution.py:107
  163.6 136.8 %reduce-scatter.2.cloned.1.call-start = ((), (), s32[]{:S(2)}) async-start(), calls=%async_computation.3 | async-start | bytes 2367488 | tf_op jit(solution)/shard_map/reduce_scatter | solution.py:137
Sparse Core Ops, SparseCore 0:
  10.6 75.1 all-gather.2
  227.0 73.3 reduce-scatter.1

commit v2 on v1

--- a/solution.py
+++ b/solution.py
@@ -1,7 +1,7 @@
 import jax
 import jax.numpy as jnp
 from jax import lax
-from jax.sharding import PartitionSpec as P
+from jax.sharding import Mesh, PartitionSpec as P
 
 PIECES = 4
 PAD = 128
@@ -32,8 +32,11 @@
 def on_device(tokens, route_weight, expert_ids, gate_weight, up_weight, down_weight, grad_output):
     groups = lax.axis_size("expert")
     group_index = lax.axis_index("expert")
-    data_size = lax.axis_size("dp")
+    chips = lax.axis_size("dpc")
+    cores = lax.axis_size("core")
+    data_size = chips * cores
     exp_local = data_size // PIECES
+    chip_share = chips // exp_local
     tok_local, topk_count = expert_ids.shape
     capacity = min(tok_local, 2 * tok_local * topk_count // (exp_local * groups))
     part_width = tokens.shape[1]
@@ -42,6 +45,7 @@
     gathered = gathered.reshape(groups, tok_local, 2, part_width)
     full_both = jnp.transpose(gathered, (1, 2, 0, 3)).reshape(tok_local, 2 * groups * part_width)
     feature_width = groups * part_width
+    row_width = 2 * feature_width + PAD
     gate_piece = gate_weight[0]
     up_piece = up_weight[0]
     down_piece = down_weight[0]
@@ -68,15 +72,21 @@
     def spread(values):
         trailing = values.shape[1:]
         grouped = values.reshape((exp_local, 1, capacity) + trailing)
-        return jnp.broadcast_to(grouped, (exp_local, PIECES, capacity) + trailing).reshape(
-            (data_size, capacity) + trailing
+        return jnp.broadcast_to(grouped, (exp_local, chip_share, capacity) + trailing).reshape(
+            (chips, capacity) + trailing
         )
 
     send_buf = jnp.concatenate(
         [full_both[token_of] * keep_mask, column_block(slot_weight, tokens.dtype)], axis=1
     )
-    recv_buf = lax.all_to_all(spread(send_buf), "dp", split_axis=0, concat_axis=0, tiled=True)
-    recv_buf = recv_buf.reshape(-1, 2 * feature_width + PAD)
+    half_buf = lax.all_to_all(spread(send_buf), "dpc", split_axis=0, concat_axis=0, tiled=True)
+    recv_buf = lax.all_to_all(
+        jnp.broadcast_to(half_buf[None], (cores,) + half_buf.shape),
+        "core",
+        split_axis=0,
+        concat_axis=0,
+        tiled=True,
+    ).reshape(-1, row_width)
     slot_rows = recv_buf[:, :feature_width]
     slot_grads = recv_buf[:, feature_width : 2 * feature_width]
     slot_scale = recv_buf[:, 2 * feature_width]
@@ -103,14 +113,25 @@
     grad_up = contract_first(up_grad, slot_rows).astype(jnp.bfloat16)[None]
     grad_down = contract_first(hidden, scaled_grad).astype(jnp.bfloat16)[None]
 
-    back_buf = jnp.concatenate([scaled, row_grad, column_block(route_terms, jnp.bfloat16)], axis=1)
+    core_index = lax.axis_index("core")
+    piece_buf = jnp.concatenate([scaled, row_grad], axis=1).reshape(cores, -1, 2 * feature_width)
+    pair = lax.all_to_all(piece_buf, "core", split_axis=0, concat_axis=0, tiled=True)
+    pair_terms = lax.all_to_all(
+        route_terms.reshape(cores, -1), "core", split_axis=0, concat_axis=0, tiled=True
+    )
+    pair_sum = jnp.sum(pair.astype(jnp.float32), axis=0).astype(jnp.bfloat16)
+    lane = jnp.arange(PAD, dtype=jnp.int32)[None, :]
+    term_block = jnp.zeros((pair_terms.shape[1], PAD), jnp.bfloat16)
+    for k in range(cores):
+        term_block = jnp.where(lane == k, pair_terms[k][:, None], term_block)
+    back_buf = jnp.concatenate([pair_sum, term_block], axis=1)
     back = lax.all_to_all(
-        back_buf.reshape(data_size, capacity, 2 * feature_width + PAD),
-        "dp",
+        back_buf.reshape(chips, capacity, row_width),
+        "dpc",
         split_axis=0,
         concat_axis=0,
         tiled=True,
-    ).reshape(-1, 2 * feature_width + PAD)
+    ).reshape(-1, row_width)
 
     wide_token = spread(token_of).reshape(-1)
     wide_live = spread(slot_live).reshape(-1)
@@ -127,8 +148,10 @@
         & (wide_live[None, :] > 0)
     ).astype(jnp.bfloat16)
     route_sum = jnp.dot(
-        row_place, back[:, 2 * feature_width], preferred_element_type=jnp.float32
-    )
+        row_place,
+        back[:, 2 * feature_width : 2 * feature_width + cores],
+        preferred_element_type=jnp.float32,
+    ).sum(axis=1)
     planes = jnp.transpose(
         both_sum.reshape(tok_local, 2, groups, part_width), (0, 2, 1, 3)
     ).reshape(tok_local, groups, 2 * part_width)
@@ -149,25 +172,29 @@
 
 
 def solution(mesh):
+    devices = mesh.devices
+    data_size, groups = devices.shape
+    chip_mesh = Mesh(devices.reshape(data_size // 2, 2, groups), ("dpc", "core", "expert"))
+    dp = ("dpc", "core")
     return jax.shard_map(
         on_device,
-        mesh=mesh,
+        mesh=chip_mesh,
         in_specs=(
-            P("dp", "expert"),
-            P("dp", None),
-            P("dp", None),
-            P("expert", "dp", None),
-            P("expert", "dp", None),
-            P("expert", "dp", None),
-            P("dp", "expert"),
+            P(dp, "expert"),
+            P(dp, None),
+            P(dp, None),
+            P("expert", dp, None),
+            P("expert", dp, None),
+            P("expert", dp, None),
+            P(dp, "expert"),
         ),
         out_specs=(
-            P("dp", "expert"),
-            P("dp", "expert"),
-            P(("dp", "expert"), None),
-            P("expert", "dp", None),
-            P("expert", "dp", None),
-            P("expert", "dp", None),
+            P(dp, "expert"),
+            P(dp, "expert"),
+            P(("dpc", "core", "expert"), None),
+            P("expert", dp, None),
+            P("expert", dp, None),
+            P("expert", dp, None),
         ),
         check_vma=False,
     )

time: 311 us -> 279 us (0.90)
  blocking collectives: 58.9 us -> 11 us
  starting transfers between devices: 6.2 us -> 19 us
  other arithmetic: 9.39 us -> 15.1 us
    all_to_all x1 -> x2, blocking collectives: 58.9 us -> 11 us  [the longest x1 7.34 us: on_device(): lax.all_to_all(jnp.broadcast_to(half_buf[None], (cores,) + half_buf.shape...]
    all_to_all x1 -> x3, starting transfers between devices: 5.93 us -> 18.9 us  [the longest x1 7.27 us: on_device(): lax.all_to_all(spread(send_buf), 'dpc', split_axis=0, concat_axis=0, tile...]
    reduce_sum x0 -> x1, other arithmetic: none -> 3.31 us  [on_device(): pair_sum = jnp.sum(pair.astype(jnp.float32), axis=0).astype(jnp.bfloat16)]
    all_to_all x1 -> x3, waiting for transfers between devices: 50.6 us -> 51.3 us  [the longest x1 28.5 us: on_device(): lax.all_to_all(back_buf.reshape(chips, capacity, row_width), 'dpc', split...]
  transfers between devices with their start and end apart: 3 -> 5, of which waited for: 3 -> 5; matrix products, arithmetic and copies ran while one was open for 8% -> 9% of each run, Pallas kernels for 0% -> 0%
where the time goes in v2:
time: 279 us; the launch traced here: 278 us
  waiting for transfers between devices  175 us (63%)
  local copies, waits for them, and re-layouts  28.3 us (10%)
  starting transfers between devices  19 us (7%)
  other arithmetic  15.1 us (5%)
  matrix products  15 us (5%)
  between operations  14.4 us (5%)
  blocking collectives  11 us (4%)
    all_gather x1, waiting for transfers between devices, on_device(): gathered = lax.all_gather(both, 'expert', axis=0, tiled=False)  61.9 us
    reduce_scatter x1, waiting for transfers between devices, on_device(): lax.psum_scatter(packed, 'expert', scatter_dimension=1, tiled=True)  61.9 us
    all_to_all x1, waiting for transfers between devices, on_device(): lax.all_to_all(back_buf.reshape(chips, capacity, row_width), 'dpc', split...  28.5 us
    all_to_all x1, waiting for transfers between devices, on_device(): lax.all_to_all(spread(send_buf), 'dpc', split_axis=0, concat_axis=0, tile...  18.6 us
    dot_general x3, matrix products, contract_first(): lax.dot_general(left_side, right_side, (((0,), (0,)), ((), ())), preferre...  9.33 us
    all_to_all x1, blocking collectives, on_device(): lax.all_to_all(jnp.broadcast_to(half_buf[None], (cores,) + half_buf.shape...  7.34 us
    all_to_all x1, starting transfers between devices, on_device(): lax.all_to_all(spread(send_buf), 'dpc', split_axis=0, concat_axis=0, tile...  7.27 us
    all_to_all x1, starting transfers between devices, on_device(): lax.all_to_all(back_buf.reshape(chips, capacity, row_width), 'dpc', split...  5.83 us
  transfers between devices with their start and end apart: 5, of which 5 were waited for; matrix products, arithmetic and copies ran while one was open for 9% of the time, Pallas kernels for 0%

profile of v2, /device:TPU:2, one launch (start us, length us, event | category | flops | bytes accessed | tf_op | source)
XLA Modules:
  0.0 278.0 jit_solution(7725228497464315505)
XLA Ops:
  7.2 1.5 pad_maximum_fusion.3
  8.7 0.8 copy.21
  9.7 2.3 reduce-window.6
  12.4 0.8 copy.25
  13.7 4.3 %scatter_custom_fusion.1 = s32[128]{0:T(128)S(1)} fusion(s32[1024]{0:T(1024)S(1)} %bitcast.91, s32[1024]{0:T(1024)S(1)} %ne.90, s32[]{:T(128)} %constant.58.clone.1), kind=kCustom, calls=%fused_computation.111 | custom fusion | bytes 516 | tf_op jit(solution)/shard_map/scatter | solution.py:66
  18.0 4.3 %scatter_custom_fusion = s32[128]{0:T(128)S(1)} fusion(s32[1024]{0:T(1024)S(1)} %bitcast.92, s32[1024]{0:T(1024)S(1)} %iota.30, s32[]{:T(128)} %constant.58.clone.1), kind=kCustom, calls=%fused_computation.113 | custom fusion | bytes 516 | tf_op jit(solution)/shard_map/scatter | solution.py:64
  22.4 1.3 gather_fusion.1
  23.9 61.9 %all-gather.3.cloned.1.call-done = bf16[2048,256]{1,0:T(8,128)(2,1)} async-done(((bf16[128,256]{1,0:T(8,128)(2,1)}), bf16[2048,256]{1,0:T(8,128)(2,1)}) %all-gather.3.cloned.1.call-update) | async-done | bytes 1048592 | tf_op jit(solution)/shard_map/all_gather | solution.py:44
  85.8 1.3 reshape.333
  87.2 1.2 copy.24
  88.4 0.5 copy.34
  88.9 1.2 gather_fusion
  90.3 1.5 broadcast_in_dim.131
  91.8 7.3 %all-to-all-start = ((bf16[16,16,4224]{2,1,0:T(8,128)(2,1)}), bf16[16,16,4224]{2,1,0:T(8,128)(2,1)S(1)}, u32[]{:S(2)}, u32[]{:S(2)}) async-start(bf16[16,16,4224]{2,1,0:T(8,128)(2,1)} %bitcast.74), calls=%async_computation | async-start | bytes 4325376 | tf_op jit(solution)/shard_map/all_to_all | solution.py:82
  99.1 18.6 %all-to-all-done = bf16[16,16,4224]{2,1,0:T(8,128)(2,1)S(1)} async-done(((bf16[16,16,4224]{2,1,0:T(8,128)(2,1)}), bf16[16,16,4224]{2,1,0:T(8,128)(2,1)S(1)}, u32[]{:S(2)}, u32[]{:S(2)}) %all-to-all-start) | async-done | bytes 2162720 | tf_op jit(solution)/shard_map/all_to_all | solution.py:82
  117.6 0.3 broadcast_in_dim.132
  117.9 7.3 %all_to_all.26 = bf16[2,16,16,4224]{3,2,1,0:T(8,128)(2,1)S(1)} all-to-all(bf16[2,16,16,4224]{3,2,1,0:T(8,128)(2,1)S(1)} %broadcast_in_dim.132), channel_id=1, replica_groups=mesh['dpc'=16,'core'=2,'expert'=16] {'core'}, dimensions={0} | all-to-all | bytes 8650752 | tf_op jit(solution)/shard_map/all_to_all | solution.py:83
  125.4 0.8 fusion.14
  126.3 0.9 copy-done.2
  127.1 0.8 fusion.16
  128.0 1.0 multiply_reduce_fusion
  129.0 0.5 broadcast.341
  129.5 0.7 reduce.13
  130.2 3.7 %all_to_all.27 = bf16[2,2,128]{2,1,0:T(2,128)(2,1)S(1)} all-to-all(bf16[2,2,128]{2,1,0:T(2,128)(2,1)S(1)} %reshape.394), channel_id=1, replica_groups=mesh['dpc'=16,'core'=2,'expert'=16] {'core'}, dimensions={0} | all-to-all | bytes 2048 | tf_op jit(solution)/shard_map/all_to_all | solution.py:119
  134.1 0.8 multiply_convert_fusion.1
  134.9 0.7 fusion.24
  135.6 0.8 add_convert_fusion
  136.4 2.5 pad_maximum_fusion
  138.9 5.8 %all-to-all-start.2 = ((bf16[2,256,4096]{2,1,0:T(8,128)(2,1)}), bf16[2,256,4096]{2,1,0:T(8,128)(2,1)}, u32[]{:S(2)}, u32[]{:S(2)}) async-start(bf16[2,256,4096]{2,1,0:T(8,128)(2,1)} %bitcast.73), calls=%async_computation.2 | async-start | bytes 8388608 | tf_op jit(solution)/shard_map/all_to_all | solution.py:118
  144.8 4.2 %all-to-all-done.2 = bf16[2,256,4096]{2,1,0:T(8,128)(2,1)} async-done(((bf16[2,256,4096]{2,1,0:T(8,128)(2,1)}), bf16[2,256,4096]{2,1,0:T(8,128)(2,1)}, u32[]{:S(2)}, u32[]{:S(2)}) %all-to-all-start.2) | async-done | bytes 4194336 | tf_op jit(solution)/shard_map/all_to_all | solution.py:118
  149.0 3.3 %reduce_sum.43 = bf16[256,4096]{1,0:T(8,128)(2,1)S(1)} reduce(bf16[2,256,4096]{2,1,0:T(8,128)(2,1)} %all-to-all-done.2, bf16[]{:T(256)} %constant.68.clone.1), dimensions={0}, to_apply=%region_5.6 | reduce | flops 1048576 | bytes 6291458 | tf_op jit(solution)/shard_map/reduce_sum | solution.py:122
  152.3 1.5 pad_maximum_fusion.2
  153.8 5.8 %all-to-all-start.4 = ((bf16[16,16,4224]{2,1,0:T(8,128)(2,1)}), bf16[16,16,4224]{2,1,0:T(8,128)(2,1)S(1)}, u32[]{:S(2)}, u32[]{:S(2)}) async-start(bf16[16,16,4224]{2,1,0:T(8,128)(2,1)} %pad_maximum_fusion.2), calls=%async_computation.4 | async-start | bytes 4325376 | tf_op jit(solution)/shard_map/all_to_all | solution.py:128
  160.2 28.5 %all-to-all-done.4 = bf16[16,16,4224]{2,1,0:T(8,128)(2,1)S(1)} async-done(((bf16[16,16,4224]{2,1,0:T(8,128)(2,1)}), bf16[16,16,4224]{2,1,0:T(8,128)(2,1)S(1)}, u32[]{:S(2)}, u32[]{:S(2)}) %all-to-all-start.4) | async-done | bytes 2162720 | tf_op jit(solution)/shard_map/all_to_all | solution.py:128
  188.8 0.3 convolution_reduce_fusion
  189.1 0.5 fusion.9
  189.6 0.4 copy.30
  189.9 2.4 copy.27
  192.3 2.9 %concatenate.29 = f32[128,4096]{1,0:T(8,128)S(1)} reshape(f32[128,16,2,128]{3,2,1,0:T(2,128)} %copy.27) | data formatting | bytes 4194304 | tf_op jit(solution)/shard_map/concatenate | solution.py:159
  195.4 1.6 pad_maximum_fusion.1
  197.0 3.1 %fusion = bf16[1,192,2048]{2,1,0:T(8,128)(2,1)} fusion(bf16[512,192]{0,1:T(8,128)(2,1)S(1)} %get-tuple-element.12, bf16[512,4224]{1,0:T(8,128)(2,1)} %bitcast.83), kind=kOutput, calls=%fused_computation.11 | convolution fusion | flops 403046400 | bytes 3080192 | tf_op jit(solution)/shard_map/dot_general | solution.py:17
  200.0 3.1 %fusion.1 = bf16[1,192,2048]{2,1,0:T(8,128)(2,1)} fusion(bf16[512,192]{0,1:T(8,128)(2,1)S(1)} %get-tuple-element.13, bf16[512,4224]{1,0:T(8,128)(2,1)} %bitcast.84), kind=kOutput, calls=%fused_computation.12 | convolution fusion | flops 403046400 | bytes 3080192 | tf_op jit(solution)/shard_map/dot_general | solution.py:17
  203.1 3.2 %fusion.2 = bf16[1,192,2048]{2,1,0:T(8,128)(2,1)} fusion(bf16[512,192]{0,1:T(8,128)(2,1)S(1)} %copy-done.5, f32[512]{0:T(512)S(1)} %convert_reduce_fusion, bf16[512,4224]{1,0:T(8,128)(2,1)} %bitcast.85), kind=kOutput, calls=%fused_computation.13 | convolution fusion | flops 406192128 | bytes 3082240 | tf_op jit(solution)/shard_map/dot_general | solution.py:17
  206.3 61.9 %reduce-scatter.2.cloned.1.call-done = f32[129,256]{1,0:T(8,128)} async-done(((f32[129,4096]{1,0:T(8,128)}), f32[129,256]{1,0:T(8,128)}) %reduce-scatter.2.cloned.1.call-update) | async-done | bytes 132112 | tf_op jit(solution)/shard_map/reduce_scatter | solution.py:160
  268.2 0.9 convert.6
  269.1 0.6 fusion.52
  269.7 0.7 slice_reduce_fusion.3
  270.4 0.7 reshape_squeeze.3
  (63 shorter events, 2.8 us)
Async XLA Ops:
  7.2 120.8 %copy-start = (bf16[1,192,2048]{2,1,0:T(8,128)(2,1)S(1)}, bf16[1,192,2048]{2,1,0:T(8,128)(2,1)}, u32[]{:S(2)}) copy-start(bf16[1,192,2048]{2,1,0:T(8,128)(2,1)} %param.12) | copy-start | bytes 2359300
  7.2 78.6 %all-gather.3.cloned.1.call-start = ((), (), s32[]{:S(2)}) async-start(), calls=%async_computation.7 | async-start | bytes 1114112 | tf_op jit(solution)/shard_map/all_gather | solution.py:44
  91.8 25.9 %all-to-all-start = ((bf16[16,16,4224]{2,1,0:T(8,128)(2,1)}), bf16[16,16,4224]{2,1,0:T(8,128)(2,1)S(1)}, u32[]{:S(2)}, u32[]{:S(2)}) async-start(bf16[16,16,4224]{2,1,0:T(8,128)(2,1)} %bitcast.74), calls=%async_computation | async-start | bytes 4325376 | tf_op jit(solution)/shard_map/all_to_all | solution.py:82
  117.9 7.5 %copy-start.3 = (bf16[1,192,2048]{2,1,0:T(8,128)(2,1)S(1)}, bf16[1,192,2048]{2,1,0:T(8,128)(2,1)}, u32[]{:S(2)}) copy-start(bf16[1,192,2048]{2,1,0:T(8,128)(2,1)} %param.11) | copy-start | bytes 2359300
  125.3 2.7 copy-start.1
  125.4 1.7 copy-start.2
  129.0 6.7 %copy-start.4 = (bf16[512,192]{0,1:T(8,128)(2,1)}, bf16[512,192]{0,1:T(8,128)(2,1)S(1)}, u32[]{:S(2)}) copy-start(bf16[512,192]{0,1:T(8,128)(2,1)S(1)} %get-tuple-element.9) | copy-start | bytes 589828
  138.9 10.1 %all-to-all-start.2 = ((bf16[2,256,4096]{2,1,0:T(8,128)(2,1)}), bf16[2,256,4096]{2,1,0:T(8,128)(2,1)}, u32[]{:S(2)}, u32[]{:S(2)}) async-start(bf16[2,256,4096]{2,1,0:T(8,128)(2,1)} %bitcast.73), calls=%async_computation.2 | async-start | bytes 8388608 | tf_op jit(solution)/shard_map/all_to_all | solution.py:118
  153.8 35.0 %all-to-all-start.4 = ((bf16[16,16,4224]{2,1,0:T(8,128)(2,1)}), bf16[16,16,4224]{2,1,0:T(8,128)(2,1)S(1)}, u32[]{:S(2)}, u32[]{:S(2)}) async-start(bf16[16,16,4224]{2,1,0:T(8,128)(2,1)} %pad_maximum_fusion.2), calls=%async_computation.4 | async-start | bytes 4325376 | tf_op jit(solution)/shard_map/all_to_all | solution.py:128
  159.6 108.6 %reduce-scatter.2.cloned.1.call-start = ((), (), s32[]{:S(2)}) async-start(), calls=%async_computation.6 | async-start | bytes 2367488 | tf_op jit(solution)/shard_map/reduce_scatter | solution.py:160
  200.0 3.1 %copy-start.5 = (bf16[512,192]{0,1:T(8,128)(2,1)S(1)}, bf16[512,192]{0,1:T(8,128)(2,1)}, u32[]{:S(2)}) copy-start(bf16[512,192]{0,1:T(8,128)(2,1)} %copy-done.4) | copy-start | bytes 589828
Sparse Core Ops, SparseCore 0:
  10.6 75.1 all-gather.2
  197.1 71.0 reduce-scatter.1

commit v3 on v2

--- a/solution.py
+++ b/solution.py
@@ -41,7 +41,13 @@
     capacity = min(tok_local, 2 * tok_local * topk_count // (exp_local * groups))
     part_width = tokens.shape[1]
     both = jnp.concatenate([tokens, grad_output], axis=1)
-    gathered = lax.all_gather(both, "expert", axis=0, tiled=False)
+    gathered = lax.all_to_all(
+        jnp.broadcast_to(both[None], (groups,) + both.shape),
+        "expert",
+        split_axis=0,
+        concat_axis=0,
+        tiled=True,
+    )
     gathered = gathered.reshape(groups, tok_local, 2, part_width)
     full_both = jnp.transpose(gathered, (1, 2, 0, 3)).reshape(tok_local, 2 * groups * part_width)
     feature_width = groups * part_width

time: 279 us -> 278 us (level)
  the two profiles are of different devices: /device:TPU:2 before, /device:TPU:16 now
where the time goes in v3:
time: 278 us; the launch traced here: 277 us
  waiting for transfers between devices  160 us (58%)
  starting transfers between devices  35.3 us (13%)
  local copies, waits for them, and re-layouts  26.7 us (10%)
  matrix products  15 us (5%)
  other arithmetic  14.5 us (5%)
  between operations  14.4 us (5%)
  blocking collectives  11 us (4%)
    reduce_scatter x1, waiting for transfers between devices, on_device(): lax.psum_scatter(packed, 'expert', scatter_dimension=1, tiled=True)  67.1 us
    all_to_all x1, waiting for transfers between devices, on_device(): lax.all_to_all(jnp.broadcast_to(both[None], (groups,) + both.shape), 'exp...  36.1 us
    all_to_all x1, waiting for transfers between devices, on_device(): lax.all_to_all(back_buf.reshape(chips, capacity, row_width), 'dpc', split...  29.4 us
    all_to_all x1, waiting for transfers between devices, on_device(): lax.all_to_all(spread(send_buf), 'dpc', split_axis=0, concat_axis=0, tile...  23 us
    all_to_all x1, starting transfers between devices, on_device(): lax.all_to_all(jnp.broadcast_to(both[None], (groups,) + both.shape), 'exp...  15.2 us
    dot_general x3, matrix products, contract_first(): lax.dot_general(left_side, right_side, (((0,), (0,)), ((), ())), preferre...  9.33 us
    all_to_all x1, blocking collectives, on_device(): lax.all_to_all(jnp.broadcast_to(half_buf[None], (cores,) + half_buf.shape...  7.34 us
    all_to_all x1, starting transfers between devices, on_device(): lax.all_to_all(spread(send_buf), 'dpc', split_axis=0, concat_axis=0, tile...  7.28 us
  transfers between devices with their start and end apart: 5, of which 5 were waited for; matrix products, arithmetic and copies ran while one was open for 9% of the time, Pallas kernels for 0%

profile of v3, /device:TPU:16, one launch (start us, length us, event | category | flops | bytes accessed | tf_op | source)
XLA Modules:
  0.0 276.8 jit_solution(16323577920544523027)
XLA Ops:
  7.2 0.9 pad_maximum_fusion.3
  8.2 1.2 broadcast_in_dim.130
  9.4 15.2 %all-to-all-start = ((bf16[16,128,256]{1,2,0:T(8,128)(2,1)}), bf16[16,128,256]{1,2,0:T(8,128)(2,1)S(1)}, u32[]{:S(2)}, u32[]{:S(2)}) async-start(bf16[16,128,256]{1,2,0:T(8,128)(2,1)} %broadcast_in_dim.130), calls=%async_computation | async-start | bytes 2097152 | tf_op jit(solution)/shard_map/all_to_all | solution.py:44
  25.3 2.3 reduce-window.6
  27.5 0.3 slice_reduce_fusion
  28.2 4.3 %scatter_custom_fusion.1 = s32[128]{0:T(128)S(1)} fusion(s32[1024]{0:T(1024)S(1)} %bitcast.94, s32[1024]{0:T(1024)S(1)} %ne.90, s32[]{:T(128)} %constant.58.clone.1), kind=kCustom, calls=%fused_computation.111 | custom fusion | bytes 516 | tf_op jit(solution)/shard_map/scatter | solution.py:72
  32.5 4.3 %scatter_custom_fusion = s32[128]{0:T(128)S(1)} fusion(s32[1024]{0:T(1024)S(1)} %bitcast.95, s32[1024]{0:T(1024)S(1)} %iota.30, s32[]{:T(128)} %constant.58.clone.1), kind=kCustom, calls=%fused_computation.113 | custom fusion | bytes 516 | tf_op jit(solution)/shard_map/scatter | solution.py:70
  36.9 1.3 gather_fusion.1
  38.4 36.1 %all-to-all-done = bf16[16,128,256]{1,2,0:T(8,128)(2,1)S(1)} async-done(((bf16[16,128,256]{1,2,0:T(8,128)(2,1)}), bf16[16,128,256]{1,2,0:T(8,128)(2,1)S(1)}, u32[]{:S(2)}, u32[]{:S(2)}) %all-to-all-start) | async-done | bytes 1048608 | tf_op jit(solution)/shard_map/all_to_all | solution.py:44
  74.5 1.0 copy.25
  75.5 0.5 copy.35
  75.9 1.2 gather_fusion
  77.4 1.5 broadcast_in_dim.138
  78.9 7.3 %all-to-all-start.1 = ((bf16[16,16,4224]{2,1,0:T(8,128)(2,1)}), bf16[16,16,4224]{2,1,0:T(8,128)(2,1)S(1)}, u32[]{:S(2)}, u32[]{:S(2)}) async-start(bf16[16,16,4224]{2,1,0:T(8,128)(2,1)} %bitcast.76), calls=%async_computation.1 | async-start | bytes 4325376 | tf_op jit(solution)/shard_map/all_to_all | solution.py:88
  86.2 23.0 %all-to-all-done.1 = bf16[16,16,4224]{2,1,0:T(8,128)(2,1)S(1)} async-done(((bf16[16,16,4224]{2,1,0:T(8,128)(2,1)}), bf16[16,16,4224]{2,1,0:T(8,128)(2,1)S(1)}, u32[]{:S(2)}, u32[]{:S(2)}) %all-to-all-start.1) | async-done | bytes 2162720 | tf_op jit(solution)/shard_map/all_to_all | solution.py:88
  109.2 0.3 broadcast_in_dim.139
  109.5 7.3 %all_to_all.31 = bf16[2,16,16,4224]{3,2,1,0:T(8,128)(2,1)S(1)} all-to-all(bf16[2,16,16,4224]{3,2,1,0:T(8,128)(2,1)S(1)} %broadcast_in_dim.139), channel_id=1, replica_groups=mesh['dpc'=16,'core'=2,'expert'=16] {'core'}, dimensions={0} | all-to-all | bytes 8650752 | tf_op jit(solution)/shard_map/all_to_all | solution.py:89
  117.0 0.8 fusion.14
  117.8 0.9 copy-done.2
  118.6 0.8 fusion.16
  119.5 1.0 multiply_reduce_fusion
  120.5 0.5 broadcast.342
  121.1 0.7 reduce.13
  121.8 3.7 %all_to_all.32 = bf16[2,2,128]{2,1,0:T(2,128)(2,1)S(1)} all-to-all(bf16[2,2,128]{2,1,0:T(2,128)(2,1)S(1)} %reshape.393), channel_id=1, replica_groups=mesh['dpc'=16,'core'=2,'expert'=16] {'core'}, dimensions={0} | all-to-all | bytes 2048 | tf_op jit(solution)/shard_map/all_to_all | solution.py:125
  125.7 0.8 multiply_convert_fusion.1
  126.4 0.7 fusion.24
  127.2 0.8 add_convert_fusion
  128.0 2.5 pad_maximum_fusion
  130.4 5.8 %all-to-all-start.3 = ((bf16[2,256,4096]{2,1,0:T(8,128)(2,1)}), bf16[2,256,4096]{2,1,0:T(8,128)(2,1)}, u32[]{:S(2)}, u32[]{:S(2)}) async-start(bf16[2,256,4096]{2,1,0:T(8,128)(2,1)} %bitcast.75), calls=%async_computation.3 | async-start | bytes 8388608 | tf_op jit(solution)/shard_map/all_to_all | solution.py:124
  136.3 4.2 %all-to-all-done.3 = bf16[2,256,4096]{2,1,0:T(8,128)(2,1)} async-done(((bf16[2,256,4096]{2,1,0:T(8,128)(2,1)}), bf16[2,256,4096]{2,1,0:T(8,128)(2,1)}, u32[]{:S(2)}, u32[]{:S(2)}) %all-to-all-start.3) | async-done | bytes 4194336 | tf_op jit(solution)/shard_map/all_to_all | solution.py:124
  140.5 3.3 %reduce_sum.43 = bf16[256,4096]{1,0:T(8,128)(2,1)S(1)} reduce(bf16[2,256,4096]{2,1,0:T(8,128)(2,1)} %all-to-all-done.3, bf16[]{:T(256)} %constant.68.clone.1), dimensions={0}, to_apply=%region_5.6 | reduce | flops 1048576 | bytes 6291458 | tf_op jit(solution)/shard_map/reduce_sum | solution.py:128
  143.8 1.5 pad_maximum_fusion.2
  145.3 7.1 %all-to-all-start.5 = ((bf16[16,16,4224]{2,1,0:T(8,128)(2,1)}), bf16[16,16,4224]{2,1,0:T(8,128)(2,1)S(1)}, u32[]{:S(2)}, u32[]{:S(2)}) async-start(bf16[16,16,4224]{2,1,0:T(8,128)(2,1)} %pad_maximum_fusion.2), calls=%async_computation.5 | async-start | bytes 4325376 | tf_op jit(solution)/shard_map/all_to_all | solution.py:134
  153.0 29.4 %all-to-all-done.5 = bf16[16,16,4224]{2,1,0:T(8,128)(2,1)S(1)} async-done(((bf16[16,16,4224]{2,1,0:T(8,128)(2,1)}), bf16[16,16,4224]{2,1,0:T(8,128)(2,1)S(1)}, u32[]{:S(2)}, u32[]{:S(2)}) %all-to-all-start.5) | async-done | bytes 2162720 | tf_op jit(solution)/shard_map/all_to_all | solution.py:134
  182.4 0.3 convolution_reduce_fusion
  182.8 0.5 fusion.9
  183.2 0.4 copy.31
  183.6 2.4 copy.28
  186.0 2.9 %concatenate.29 = f32[128,4096]{1,0:T(8,128)S(1)} reshape(f32[128,16,2,128]{3,2,1,0:T(2,128)} %copy.28) | data formatting | bytes 4194304 | tf_op jit(solution)/shard_map/concatenate | solution.py:165
  189.0 1.6 pad_maximum_fusion.1
  190.6 3.1 %fusion = bf16[1,192,2048]{2,1,0:T(8,128)(2,1)} fusion(bf16[512,192]{0,1:T(8,128)(2,1)S(1)} %get-tuple-element.12, bf16[512,4224]{1,0:T(8,128)(2,1)} %bitcast.85), kind=kOutput, calls=%fused_computation.11 | convolution fusion | flops 403046400 | bytes 3080192 | tf_op jit(solution)/shard_map/dot_general | solution.py:17
  193.7 3.1 %fusion.1 = bf16[1,192,2048]{2,1,0:T(8,128)(2,1)} fusion(bf16[512,192]{0,1:T(8,128)(2,1)S(1)} %get-tuple-element.13, bf16[512,4224]{1,0:T(8,128)(2,1)} %bitcast.86), kind=kOutput, calls=%fused_computation.12 | convolution fusion | flops 403046400 | bytes 3080192 | tf_op jit(solution)/shard_map/dot_general | solution.py:17
  196.8 3.2 %fusion.2 = bf16[1,192,2048]{2,1,0:T(8,128)(2,1)} fusion(bf16[512,192]{0,1:T(8,128)(2,1)S(1)} %copy-done.7, f32[512]{0:T(512)S(1)} %convert_reduce_fusion, bf16[512,4224]{1,0:T(8,128)(2,1)} %bitcast.87), kind=kOutput, calls=%fused_computation.13 | convolution fusion | flops 406192128 | bytes 3082240 | tf_op jit(solution)/shard_map/dot_general | solution.py:17
  200.0 67.1 %reduce-scatter.2.cloned.1.call-done = f32[129,256]{1,0:T(8,128)} async-done(((f32[129,4096]{1,0:T(8,128)}), f32[129,256]{1,0:T(8,128)}) %reduce-scatter.2.cloned.1.call-update) | async-done | bytes 132112 | tf_op jit(solution)/shard_map/reduce_scatter | solution.py:166
  267.1 0.9 convert.6
  268.0 0.6 fusion.52
  268.6 0.7 slice_reduce_fusion.3
  269.3 0.7 reshape_squeeze.3
  (67 shorter events, 2.8 us)
Async XLA Ops:
  7.2 112.3 %copy-start = (bf16[1,192,2048]{2,1,0:T(8,128)(2,1)S(1)}, bf16[1,192,2048]{2,1,0:T(8,128)(2,1)}, u32[]{:S(2)}) copy-start(bf16[1,192,2048]{2,1,0:T(8,128)(2,1)} %param.12) | copy-start | bytes 2359300
  7.2 17.4 %copy-start.4 = (s32[128,8]{0,1:T(8,128)S(1)}, s32[128,8]{0,1:T(8,128)}, u32[]{:S(2)}) copy-start(s32[128,8]{0,1:T(8,128)} %param.9) | copy-start | bytes 12292
  7.2 17.8 %copy-start.5 = (bf16[128,8]{0,1:T(8,128)(2,1)S(1)}, bf16[128,8]{0,1:T(8,128)(2,1)}, u32[]{:S(2)}) copy-start(bf16[128,8]{0,1:T(8,128)(2,1)} %param.8) | copy-start | bytes 6148
  9.4 65.1 %all-to-all-start = ((bf16[16,128,256]{1,2,0:T(8,128)(2,1)}), bf16[16,128,256]{1,2,0:T(8,128)(2,1)S(1)}, u32[]{:S(2)}, u32[]{:S(2)}) async-start(bf16[16,128,256]{1,2,0:T(8,128)(2,1)} %broadcast_in_dim.130), calls=%async_computation | async-start | bytes 2097152 | tf_op jit(solution)/shard_map/all_to_all | solution.py:44
  78.9 30.3 %all-to-all-start.1 = ((bf16[16,16,4224]{2,1,0:T(8,128)(2,1)}), bf16[16,16,4224]{2,1,0:T(8,128)(2,1)S(1)}, u32[]{:S(2)}, u32[]{:S(2)}) async-start(bf16[16,16,4224]{2,1,0:T(8,128)(2,1)} %bitcast.76), calls=%async_computation.1 | async-start | bytes 4325376 | tf_op jit(solution)/shard_map/all_to_all | solution.py:88
  109.5 7.5 %copy-start.3 = (bf16[1,192,2048]{2,1,0:T(8,128)(2,1)S(1)}, bf16[1,192,2048]{2,1,0:T(8,128)(2,1)}, u32[]{:S(2)}) copy-start(bf16[1,192,2048]{2,1,0:T(8,128)(2,1)} %param.11) | copy-start | bytes 2359300
  116.8 2.7 copy-start.1
  116.9 1.7 copy-start.2
  120.5 6.7 %copy-start.6 = (bf16[512,192]{0,1:T(8,128)(2,1)}, bf16[512,192]{0,1:T(8,128)(2,1)S(1)}, u32[]{:S(2)}) copy-start(bf16[512,192]{0,1:T(8,128)(2,1)S(1)} %get-tuple-element.9) | copy-start | bytes 589828
  130.4 10.1 %all-to-all-start.3 = ((bf16[2,256,4096]{2,1,0:T(8,128)(2,1)}), bf16[2,256,4096]{2,1,0:T(8,128)(2,1)}, u32[]{:S(2)}, u32[]{:S(2)}) async-start(bf16[2,256,4096]{2,1,0:T(8,128)(2,1)} %bitcast.75), calls=%async_computation.3 | async-start | bytes 8388608 | tf_op jit(solution)/shard_map/all_to_all | solution.py:124
  145.3 37.1 %all-to-all-start.5 = ((bf16[16,16,4224]{2,1,0:T(8,128)(2,1)}), bf16[16,16,4224]{2,1,0:T(8,128)(2,1)S(1)}, u32[]{:S(2)}, u32[]{:S(2)}) async-start(bf16[16,16,4224]{2,1,0:T(8,128)(2,1)} %pad_maximum_fusion.2), calls=%async_computation.5 | async-start | bytes 4325376 | tf_op jit(solution)/shard_map/all_to_all | solution.py:134
  152.4 114.7 %reduce-scatter.2.cloned.1.call-start = ((), (), s32[]{:S(2)}) async-start(), calls=%async_computation.7 | async-start | bytes 2367488 | tf_op jit(solution)/shard_map/reduce_scatter | solution.py:166
  193.7 3.1 %copy-start.7 = (bf16[512,192]{0,1:T(8,128)(2,1)S(1)}, bf16[512,192]{0,1:T(8,128)(2,1)}, u32[]{:S(2)}) copy-start(bf16[512,192]{0,1:T(8,128)(2,1)} %copy-done.6) | copy-start | bytes 589828
Sparse Core Ops, SparseCore 0:
  190.8 76.2 reduce-scatter.1

commit v4 on v3

--- a/solution.py
+++ b/solution.py
@@ -159,11 +159,12 @@
         preferred_element_type=jnp.float32,
     ).sum(axis=1)
     planes = jnp.transpose(
-        both_sum.reshape(tok_local, 2, groups, part_width), (0, 2, 1, 3)
-    ).reshape(tok_local, groups, 2 * part_width)
+        both_sum.reshape(tok_local, 2, groups, part_width), (2, 0, 1, 3)
+    ).reshape(groups, tok_local, 2 * part_width)
     route_row = jnp.pad(route_sum.reshape(groups, -1), ((0, 0), (0, 2 * part_width - row_count // groups)))
-    packed = jnp.concatenate([planes, route_row[None]], axis=0).reshape(tok_local + 1, -1)
-    reduced = lax.psum_scatter(packed, "expert", scatter_dimension=1, tiled=True)
+    packed = jnp.concatenate([planes, route_row[:, None]], axis=1).astype(jnp.bfloat16)
+    received = lax.all_to_all(packed, "expert", split_axis=0, concat_axis=0, tiled=True)
+    reduced = jnp.sum(received.astype(jnp.float32), axis=0)
     mixed_part = reduced[:tok_local, :part_width]
     token_part = reduced[:tok_local, part_width:]
     route_part = reduced[tok_local, : row_count // groups].reshape(-1, topk_count)

time: 278 us -> 253 us (0.910)
  waiting for transfers between devices: 160 us -> 135 us
  starting transfers between devices: 35.3 us -> 48.8 us
  between operations: 14.4 us -> 1.06 us
    reduce_scatter x1 -> x0, waiting for transfers between devices: 67.1 us -> none  [on_device(): lax.psum_scatter(packed, 'expert', scatter_dimension=1, tiled=True)]
    all_to_all x0 -> x1, waiting for transfers between devices: none -> 42.3 us  [on_device(): lax.all_to_all(packed, 'expert', split_axis=0, concat_axis=0, tiled=True)]
    all_to_all x0 -> x1, starting transfers between devices: none -> 13.5 us  [on_device(): lax.all_to_all(packed, 'expert', split_axis=0, concat_axis=0, tiled=True)]
where the time goes in v4:
time: 253 us; the launch traced here: 252 us
  waiting for transfers between devices  135 us (53%)
  starting transfers between devices  48.8 us (19%)
  local copies, waits for them, and re-layouts  26.9 us (11%)
  matrix products  15 us (6%)
  other arithmetic  14.5 us (6%)
  blocking collectives  11 us (4%)
    all_to_all x1, waiting for transfers between devices, on_device(): lax.all_to_all(packed, 'expert', split_axis=0, concat_axis=0, tiled=True)  42.3 us
    all_to_all x1, waiting for transfers between devices, on_device(): lax.all_to_all(jnp.broadcast_to(both[None], (groups,) + both.shape), 'exp...  36.1 us
    all_to_all x1, waiting for transfers between devices, on_device(): lax.all_to_all(back_buf.reshape(chips, capacity, row_width), 'dpc', split...  29.5 us
    all_to_all x1, waiting for transfers between devices, on_device(): lax.all_to_all(spread(send_buf), 'dpc', split_axis=0, concat_axis=0, tile...  23 us
    all_to_all x1, starting transfers between devices, on_device(): lax.all_to_all(jnp.broadcast_to(both[None], (groups,) + both.shape), 'exp...  15.2 us
    all_to_all x1, starting transfers between devices, on_device(): lax.all_to_all(packed, 'expert', split_axis=0, concat_axis=0, tiled=True)  13.5 us
    dot_general x3, matrix products, contract_first(): lax.dot_general(left_side, right_side, (((0,), (0,)), ((), ())), preferre...  9.32 us
    all_to_all x1, blocking collectives, on_device(): lax.all_to_all(jnp.broadcast_to(half_buf[None], (cores,) + half_buf.shape...  7.34 us
  transfers between devices with their start and end apart: 5, of which 5 were waited for; matrix products, arithmetic and copies ran while one was open for 9% of the time, Pallas kernels for 0%

profile of v4, /device:TPU:16, one launch (start us, length us, event | category | flops | bytes accessed | tf_op | source)
XLA Modules:
  0.0 252.5 jit_solution(6600576134154056317)
XLA Ops:
  0.7 0.9 pad_maximum_fusion.3
  1.6 1.2 broadcast_in_dim.133
  2.8 15.2 %all-to-all-start = ((bf16[16,128,256]{1,2,0:T(8,128)(2,1)}), bf16[16,128,256]{1,2,0:T(8,128)(2,1)S(1)}, u32[]{:S(2)}, u32[]{:S(2)}) async-start(bf16[16,128,256]{1,2,0:T(8,128)(2,1)} %broadcast_in_dim.133), calls=%async_computation | async-start | bytes 2097152 | tf_op jit(solution)/shard_map/all_to_all | solution.py:44
  18.7 2.3 reduce-window.6
  21.6 4.3 %scatter_custom_fusion.1 = s32[128]{0:T(128)S(1)} fusion(s32[1024]{0:T(1024)S(1)} %bitcast.93, s32[1024]{0:T(1024)S(1)} %ne.90, s32[]{:T(128)} %constant.59.clone.1), kind=kCustom, calls=%fused_computation.112 | custom fusion | bytes 516 | tf_op jit(solution)/shard_map/scatter | solution.py:72
  26.0 4.3 %scatter_custom_fusion = s32[128]{0:T(128)S(1)} fusion(s32[1024]{0:T(1024)S(1)} %bitcast.94, s32[1024]{0:T(1024)S(1)} %iota.30, s32[]{:T(128)} %constant.59.clone.1), kind=kCustom, calls=%fused_computation.114 | custom fusion | bytes 516 | tf_op jit(solution)/shard_map/scatter | solution.py:70
  30.4 1.3 gather_fusion.1
  31.9 36.1 %all-to-all-done = bf16[16,128,256]{1,2,0:T(8,128)(2,1)S(1)} async-done(((bf16[16,128,256]{1,2,0:T(8,128)(2,1)}), bf16[16,128,256]{1,2,0:T(8,128)(2,1)S(1)}, u32[]{:S(2)}, u32[]{:S(2)}) %all-to-all-start) | async-done | bytes 1048608 | tf_op jit(solution)/shard_map/all_to_all | solution.py:44
  68.0 1.0 copy.51
  69.0 0.5 copy.68
  69.4 1.2 gather_fusion
  70.8 1.5 broadcast_in_dim.141
  72.3 7.3 %all-to-all-start.1 = ((bf16[16,16,4224]{2,1,0:T(8,128)(2,1)}), bf16[16,16,4224]{2,1,0:T(8,128)(2,1)S(1)}, u32[]{:S(2)}, u32[]{:S(2)}) async-start(bf16[16,16,4224]{2,1,0:T(8,128)(2,1)} %bitcast.75), calls=%async_computation.1 | async-start | bytes 4325376 | tf_op jit(solution)/shard_map/all_to_all | solution.py:88
  79.6 23.0 %all-to-all-done.1 = bf16[16,16,4224]{2,1,0:T(8,128)(2,1)S(1)} async-done(((bf16[16,16,4224]{2,1,0:T(8,128)(2,1)}), bf16[16,16,4224]{2,1,0:T(8,128)(2,1)S(1)}, u32[]{:S(2)}, u32[]{:S(2)}) %all-to-all-start.1) | async-done | bytes 2162720 | tf_op jit(solution)/shard_map/all_to_all | solution.py:88
  102.6 0.3 broadcast_in_dim.142
  102.9 7.3 %all_to_all.36 = bf16[2,16,16,4224]{3,2,1,0:T(8,128)(2,1)S(1)} all-to-all(bf16[2,16,16,4224]{3,2,1,0:T(8,128)(2,1)S(1)} %broadcast_in_dim.142), channel_id=1, replica_groups=mesh['dpc'=16,'core'=2,'expert'=16] {'core'}, dimensions={0} | all-to-all | bytes 8650752 | tf_op jit(solution)/shard_map/all_to_all | solution.py:89
  110.4 0.8 fusion.13
  111.3 0.9 copy-done.2
  112.1 0.8 fusion.15
  113.0 1.0 multiply_reduce_fusion
  114.0 0.5 broadcast.340
  114.5 0.7 reduce.11
  115.2 3.7 %all_to_all.37 = bf16[2,2,128]{2,1,0:T(2,128)(2,1)S(1)} all-to-all(bf16[2,2,128]{2,1,0:T(2,128)(2,1)S(1)} %reshape.388), channel_id=1, replica_groups=mesh['dpc'=16,'core'=2,'expert'=16] {'core'}, dimensions={0} | all-to-all | bytes 2048 | tf_op jit(solution)/shard_map/all_to_all | solution.py:125
  119.1 0.8 multiply_convert_fusion.1
  119.9 0.7 fusion.23
  120.6 0.8 add_convert_fusion
  121.4 2.5 pad_maximum_fusion
  123.9 5.8 %all-to-all-start.3 = ((bf16[2,256,4096]{2,1,0:T(8,128)(2,1)}), bf16[2,256,4096]{2,1,0:T(8,128)(2,1)}, u32[]{:S(2)}, u32[]{:S(2)}) async-start(bf16[2,256,4096]{2,1,0:T(8,128)(2,1)} %bitcast.74), calls=%async_computation.3 | async-start | bytes 8388608 | tf_op jit(solution)/shard_map/all_to_all | solution.py:124
  129.8 4.2 %all-to-all-done.3 = bf16[2,256,4096]{2,1,0:T(8,128)(2,1)} async-done(((bf16[2,256,4096]{2,1,0:T(8,128)(2,1)}), bf16[2,256,4096]{2,1,0:T(8,128)(2,1)}, u32[]{:S(2)}, u32[]{:S(2)}) %all-to-all-start.3) | async-done | bytes 4194336 | tf_op jit(solution)/shard_map/all_to_all | solution.py:124
  134.0 3.3 %reduce_sum.52 = bf16[256,4096]{1,0:T(8,128)(2,1)S(1)} reduce(bf16[2,256,4096]{2,1,0:T(8,128)(2,1)} %all-to-all-done.3, bf16[]{:T(256)} %constant.69.clone.1), dimensions={0}, to_apply=%region_5.6 | reduce | flops 1048576 | bytes 6291458 | tf_op jit(solution)/shard_map/reduce_sum | solution.py:128
  137.3 1.5 pad_maximum_fusion.1
  138.8 7.1 %all-to-all-start.5 = ((bf16[16,16,4224]{2,1,0:T(8,128)(2,1)}), bf16[16,16,4224]{2,1,0:T(8,128)(2,1)S(1)}, u32[]{:S(2)}, u32[]{:S(2)}) async-start(bf16[16,16,4224]{2,1,0:T(8,128)(2,1)} %pad_maximum_fusion.1), calls=%async_computation.5 | async-start | bytes 4325376 | tf_op jit(solution)/shard_map/all_to_all | solution.py:134
  146.4 29.5 %all-to-all-done.5 = bf16[16,16,4224]{2,1,0:T(8,128)(2,1)S(1)} async-done(((bf16[16,16,4224]{2,1,0:T(8,128)(2,1)}), bf16[16,16,4224]{2,1,0:T(8,128)(2,1)S(1)}, u32[]{:S(2)}, u32[]{:S(2)}) %all-to-all-start.5) | async-done | bytes 2162720 | tf_op jit(solution)/shard_map/all_to_all | solution.py:134
  175.9 0.3 convolution_reduce_fusion
  176.2 0.5 fusion.8
  176.9 1.8 copy.54
  178.8 1.4 copy.55
  180.2 2.0 pad_maximum_fusion.2
  182.2 2.2 copy.56
  184.4 13.5 %all-to-all-start.6 = ((bf16[16,129,256]{2,1,0:T(8,128)(2,1)}), bf16[16,129,256]{2,1,0:T(8,128)(2,1)S(1)}, u32[]{:S(2)}, u32[]{:S(2)}) async-start(bf16[16,129,256]{2,1,0:T(8,128)(2,1)} %copy.56), calls=%async_computation.6 | async-start | bytes 2228224 | tf_op jit(solution)/shard_map/all_to_all | solution.py:166
  197.9 3.1 %fusion = bf16[1,192,2048]{2,1,0:T(8,128)(2,1)} fusion(bf16[512,192]{0,1:T(8,128)(2,1)S(1)} %get-tuple-element.30, bf16[512,4224]{1,0:T(8,128)(2,1)} %bitcast.83), kind=kOutput, calls=%fused_computation.12 | convolution fusion | flops 403046400 | bytes 3080192 | tf_op jit(solution)/shard_map/dot_general | solution.py:17
  200.9 3.1 %fusion.1 = bf16[1,192,2048]{2,1,0:T(8,128)(2,1)} fusion(bf16[512,192]{0,1:T(8,128)(2,1)S(1)} %get-tuple-element.31, bf16[512,4224]{1,0:T(8,128)(2,1)} %bitcast.84), kind=kOutput, calls=%fused_computation.13 | convolution fusion | flops 403046400 | bytes 3080192 | tf_op jit(solution)/shard_map/dot_general | solution.py:17
  204.0 3.2 %fusion.2 = bf16[1,192,2048]{2,1,0:T(8,128)(2,1)} fusion(bf16[512,192]{0,1:T(8,128)(2,1)S(1)} %copy-done.7, f32[512]{0:T(512)S(1)} %convert_reduce_fusion.1, bf16[512,4224]{1,0:T(8,128)(2,1)} %bitcast.85), kind=kOutput, calls=%fused_computation.14 | convolution fusion | flops 406192128 | bytes 3082240 | tf_op jit(solution)/shard_map/dot_general | solution.py:17
  207.2 42.3 %all-to-all-done.6 = bf16[16,129,256]{2,1,0:T(8,128)(2,1)S(1)} async-done(((bf16[16,129,256]{2,1,0:T(8,128)(2,1)}), bf16[16,129,256]{2,1,0:T(8,128)(2,1)S(1)}, u32[]{:S(2)}, u32[]{:S(2)}) %all-to-all-start.6) | async-done | bytes 1056800 | tf_op jit(solution)/shard_map/all_to_all | solution.py:166
  249.5 0.5 convert_reduce_fusion
  250.3 0.7 copy.60
  251.1 0.7 reshape_squeeze.3
  251.7 0.7 copy.59
  (70 shorter events, 3.5 us)
Async XLA Ops:
  0.6 112.3 %copy-start = (bf16[1,192,2048]{2,1,0:T(8,128)(2,1)S(1)}, bf16[1,192,2048]{2,1,0:T(8,128)(2,1)}, u32[]{:S(2)}) copy-start(bf16[1,192,2048]{2,1,0:T(8,128)(2,1)} %param.12) | copy-start | bytes 2359300
  0.6 17.4 %copy-start.4 = (s32[128,8]{0,1:T(8,128)S(1)}, s32[128,8]{0,1:T(8,128)}, u32[]{:S(2)}) copy-start(s32[128,8]{0,1:T(8,128)} %param.9) | copy-start | bytes 12292
  0.7 17.8 %copy-start.5 = (bf16[128,8]{0,1:T(8,128)(2,1)S(1)}, bf16[128,8]{0,1:T(8,128)(2,1)}, u32[]{:S(2)}) copy-start(bf16[128,8]{0,1:T(8,128)(2,1)} %param.8) | copy-start | bytes 6148
  2.8 65.1 %all-to-all-start = ((bf16[16,128,256]{1,2,0:T(8,128)(2,1)}), bf16[16,128,256]{1,2,0:T(8,128)(2,1)S(1)}, u32[]{:S(2)}, u32[]{:S(2)}) async-start(bf16[16,128,256]{1,2,0:T(8,128)(2,1)} %broadcast_in_dim.133), calls=%async_computation | async-start | bytes 2097152 | tf_op jit(solution)/shard_map/all_to_all | solution.py:44
  72.3 30.3 %all-to-all-start.1 = ((bf16[16,16,4224]{2,1,0:T(8,128)(2,1)}), bf16[16,16,4224]{2,1,0:T(8,128)(2,1)S(1)}, u32[]{:S(2)}, u32[]{:S(2)}) async-start(bf16[16,16,4224]{2,1,0:T(8,128)(2,1)} %bitcast.75), calls=%async_computation.1 | async-start | bytes 4325376 | tf_op jit(solution)/shard_map/all_to_all | solution.py:88
  102.9 7.5 %copy-start.3 = (bf16[1,192,2048]{2,1,0:T(8,128)(2,1)S(1)}, bf16[1,192,2048]{2,1,0:T(8,128)(2,1)}, u32[]{:S(2)}) copy-start(bf16[1,192,2048]{2,1,0:T(8,128)(2,1)} %param.11) | copy-start | bytes 2359300
  110.3 2.7 %copy-start.1 = (bf16[2,16,16,4224]{3,2,1,0:T(8,128)(2,1)}, bf16[2,16,16,4224]{3,2,1,0:T(8,128)(2,1)S(1)}, u32[]{:S(2)}) copy-start(bf16[2,16,16,4224]{3,2,1,0:T(8,128)(2,1)S(1)} %all_to_all.36) | copy-start | bytes 12976132
  110.4 1.7 copy-start.2
  114.0 6.7 %copy-start.6 = (bf16[512,192]{0,1:T(8,128)(2,1)}, bf16[512,192]{0,1:T(8,128)(2,1)S(1)}, u32[]{:S(2)}) copy-start(bf16[512,192]{0,1:T(8,128)(2,1)S(1)} %get-tuple-element.27) | copy-start | bytes 589828
  123.9 10.1 %all-to-all-start.3 = ((bf16[2,256,4096]{2,1,0:T(8,128)(2,1)}), bf16[2,256,4096]{2,1,0:T(8,128)(2,1)}, u32[]{:S(2)}, u32[]{:S(2)}) async-start(bf16[2,256,4096]{2,1,0:T(8,128)(2,1)} %bitcast.74), calls=%async_computation.3 | async-start | bytes 8388608 | tf_op jit(solution)/shard_map/all_to_all | solution.py:124
  138.8 37.1 %all-to-all-start.5 = ((bf16[16,16,4224]{2,1,0:T(8,128)(2,1)}), bf16[16,16,4224]{2,1,0:T(8,128)(2,1)S(1)}, u32[]{:S(2)}, u32[]{:S(2)}) async-start(bf16[16,16,4224]{2,1,0:T(8,128)(2,1)} %pad_maximum_fusion.1), calls=%async_computation.5 | async-start | bytes 4325376 | tf_op jit(solution)/shard_map/all_to_all | solution.py:134
  184.4 65.1 %all-to-all-start.6 = ((bf16[16,129,256]{2,1,0:T(8,128)(2,1)}), bf16[16,129,256]{2,1,0:T(8,128)(2,1)S(1)}, u32[]{:S(2)}, u32[]{:S(2)}) async-start(bf16[16,129,256]{2,1,0:T(8,128)(2,1)} %copy.56), calls=%async_computation.6 | async-start | bytes 2228224 | tf_op jit(solution)/shard_map/all_to_all | solution.py:166
  200.9 3.1 %copy-start.7 = (bf16[512,192]{0,1:T(8,128)(2,1)S(1)}, bf16[512,192]{0,1:T(8,128)(2,1)}, u32[]{:S(2)}) copy-start(bf16[512,192]{0,1:T(8,128)(2,1)} %copy-done.6) | copy-start | bytes 589828

commit v5 on v2

--- a/solution.py
+++ b/solution.py
@@ -40,12 +40,15 @@
     tok_local, topk_count = expert_ids.shape
     capacity = min(tok_local, 2 * tok_local * topk_count // (exp_local * groups))
     part_width = tokens.shape[1]
-    both = jnp.concatenate([tokens, grad_output], axis=1)
-    gathered = lax.all_gather(both, "expert", axis=0, tiled=False)
-    gathered = gathered.reshape(groups, tok_local, 2, part_width)
-    full_both = jnp.transpose(gathered, (1, 2, 0, 3)).reshape(tok_local, 2 * groups * part_width)
     feature_width = groups * part_width
-    row_width = 2 * feature_width + PAD
+
+    def gather_features(block):
+        spread_out = jnp.broadcast_to(block[None], (groups,) + block.shape)
+        got = lax.all_to_all(spread_out, "expert", split_axis=0, concat_axis=0, tiled=True)
+        return jnp.transpose(got, (1, 0, 2)).reshape(tok_local, feature_width)
+
+    full_x = gather_features(tokens)
+    full_dy = gather_features(grad_output)
     gate_piece = gate_weight[0]
     up_piece = up_weight[0]
     down_piece = down_weight[0]
@@ -76,29 +79,62 @@
             (chips, capacity) + trailing
         )
 
-    send_buf = jnp.concatenate(
-        [full_both[token_of] * keep_mask, column_block(slot_weight, tokens.dtype)], axis=1
-    )
-    half_buf = lax.all_to_all(spread(send_buf), "dpc", split_axis=0, concat_axis=0, tiled=True)
-    recv_buf = lax.all_to_all(
-        jnp.broadcast_to(half_buf[None], (cores,) + half_buf.shape),
-        "core",
-        split_axis=0,
-        concat_axis=0,
-        tiled=True,
-    ).reshape(-1, row_width)
-    slot_rows = recv_buf[:, :feature_width]
-    slot_grads = recv_buf[:, feature_width : 2 * feature_width]
-    slot_scale = recv_buf[:, 2 * feature_width]
+    def dispatch(send_buf):
+        width = send_buf.shape[1]
+        half_buf = lax.all_to_all(spread(send_buf), "dpc", split_axis=0, concat_axis=0, tiled=True)
+        return lax.all_to_all(
+            jnp.broadcast_to(half_buf[None], (cores,) + half_buf.shape),
+            "core",
+            split_axis=0,
+            concat_axis=0,
+            tiled=True,
+        ).reshape(-1, width)
+
+    def pair_sum(values):
+        pair = lax.all_to_all(
+            values.reshape((cores, -1) + values.shape[1:]), "core", split_axis=0, concat_axis=0, tiled=True
+        )
+        return jnp.sum(pair.astype(jnp.float32), axis=0).astype(jnp.bfloat16)
+
+    def send_back(values):
+        width = values.shape[1]
+        return lax.all_to_all(
+            values.reshape(chips, capacity, width), "dpc", split_axis=0, concat_axis=0, tiled=True
+        ).reshape(-1, width)
+
+    wide_token = spread(token_of).reshape(-1)
+    wide_live = spread(slot_live).reshape(-1)
+    wide_row = spread(row_of).reshape(-1)
+    token_place = (
+        (wide_token[None, :] == jnp.arange(tok_local, dtype=jnp.int32)[:, None])
+        & (wide_live[None, :] > 0)
+    ).astype(jnp.bfloat16)
+
+    def combine(rows, extra):
+        total = jnp.dot(token_place, rows, preferred_element_type=jnp.float32)
+        planes = jnp.transpose(total.reshape(tok_local, groups, part_width), (1, 0, 2))
+        if extra is not None:
+            planes = jnp.concatenate([planes, extra[:, None]], axis=1)
+        received = lax.all_to_all(
+            planes.astype(jnp.bfloat16), "expert", split_axis=0, concat_axis=0, tiled=True
+        )
+        return jnp.sum(received.astype(jnp.float32), axis=0)
+
+    recv_x = dispatch(
+        jnp.concatenate([full_x[token_of] * keep_mask, column_block(slot_weight, tokens.dtype)], axis=1)
+    )
+    slot_rows = recv_x[:, :feature_width]
+    slot_scale = recv_x[:, feature_width]
     weight_wide = slot_scale.astype(jnp.float32)[:, None]
-
     gate_act = contract_last(slot_rows, gate_piece)
     up_act = contract_last(slot_rows, up_piece)
     active, silu_slope = silu_parts(gate_act)
     hidden = (active * up_act).astype(jnp.bfloat16)
     partial_out = jnp.dot(hidden, down_piece, preferred_element_type=jnp.float32)
     scaled = (weight_wide * partial_out).astype(jnp.bfloat16)
-
+    mixed_part = combine(send_back(pair_sum(scaled)), None)
+
+    slot_grads = dispatch(full_dy[token_of] * keep_mask)
     into_hidden = contract_last(slot_grads, down_piece)
     route_terms = jnp.sum(into_hidden * hidden.astype(jnp.float32), axis=1).astype(jnp.bfloat16)
     hidden_grad = weight_wide * into_hidden
@@ -113,54 +149,27 @@
     grad_up = contract_first(up_grad, slot_rows).astype(jnp.bfloat16)[None]
     grad_down = contract_first(hidden, scaled_grad).astype(jnp.bfloat16)[None]
 
-    core_index = lax.axis_index("core")
-    piece_buf = jnp.concatenate([scaled, row_grad], axis=1).reshape(cores, -1, 2 * feature_width)
-    pair = lax.all_to_all(piece_buf, "core", split_axis=0, concat_axis=0, tiled=True)
     pair_terms = lax.all_to_all(
         route_terms.reshape(cores, -1), "core", split_axis=0, concat_axis=0, tiled=True
     )
-    pair_sum = jnp.sum(pair.astype(jnp.float32), axis=0).astype(jnp.bfloat16)
     lane = jnp.arange(PAD, dtype=jnp.int32)[None, :]
     term_block = jnp.zeros((pair_terms.shape[1], PAD), jnp.bfloat16)
     for k in range(cores):
         term_block = jnp.where(lane == k, pair_terms[k][:, None], term_block)
-    back_buf = jnp.concatenate([pair_sum, term_block], axis=1)
-    back = lax.all_to_all(
-        back_buf.reshape(chips, capacity, row_width),
-        "dpc",
-        split_axis=0,
-        concat_axis=0,
-        tiled=True,
-    ).reshape(-1, row_width)
-
-    wide_token = spread(token_of).reshape(-1)
-    wide_live = spread(slot_live).reshape(-1)
-    wide_row = spread(row_of).reshape(-1)
-    token_place = (
-        (wide_token[None, :] == jnp.arange(tok_local, dtype=jnp.int32)[:, None])
-        & (wide_live[None, :] > 0)
-    ).astype(jnp.bfloat16)
-    both_sum = jnp.dot(
-        token_place, back[:, : 2 * feature_width], preferred_element_type=jnp.float32
-    )
+    back = send_back(jnp.concatenate([pair_sum(row_grad), term_block], axis=1))
     row_place = (
         (wide_row[None, :] == jnp.arange(row_count, dtype=jnp.int32)[:, None])
         & (wide_live[None, :] > 0)
     ).astype(jnp.bfloat16)
     route_sum = jnp.dot(
         row_place,
-        back[:, 2 * feature_width : 2 * feature_width + cores],
+        back[:, feature_width : feature_width + cores],
         preferred_element_type=jnp.float32,
     ).sum(axis=1)
-    planes = jnp.transpose(
-        both_sum.reshape(tok_local, 2, groups, part_width), (0, 2, 1, 3)
-    ).reshape(tok_local, groups, 2 * part_width)
-    route_row = jnp.pad(route_sum.reshape(groups, -1), ((0, 0), (0, 2 * part_width - row_count // groups)))
-    packed = jnp.concatenate([planes, route_row[None]], axis=0).reshape(tok_local + 1, -1)
-    reduced = lax.psum_scatter(packed, "expert", scatter_dimension=1, tiled=True)
-    mixed_part = reduced[:tok_local, :part_width]
-    token_part = reduced[:tok_local, part_width:]
-    route_part = reduced[tok_local, : row_count // groups].reshape(-1, topk_count)
+    route_row = jnp.pad(route_sum.reshape(groups, -1), ((0, 0), (0, part_width - row_count // groups)))
+    token_total = combine(back[:, :feature_width], route_row)
+    token_part = token_total[:tok_local]
+    route_part = token_total[tok_local, : row_count // groups].reshape(-1, topk_count)
     return (
         mixed_part.astype(jnp.bfloat16),
         token_part.astype(jnp.bfloat16),

time: 279 us -> 290 us (1.039)
  the two profiles are of different devices: /device:TPU:2 before, /device:TPU:32 now
where the time goes in v5:
time: 290 us; the launch traced here: 288 us
  waiting for transfers between devices  126 us (43%)
  starting transfers between devices  72.7 us (25%)
  blocking collectives  29.3 us (10%)
  local copies, waits for them, and re-layouts  24.6 us (8%)
  matrix products  20.5 us (7%)
  other arithmetic  14 us (5%)
    all_to_all x2, waiting for transfers between devices, combine(): lax.all_to_all(planes.astype(jnp.bfloat16), 'expert', split_axis=0, conca...  43.8 us
    all_to_all x2, waiting for transfers between devices, gather_features(): lax.all_to_all(spread_out, 'expert', split_axis=0, concat_axis=0, tiled=T...  41.4 us
    all_to_all x2, waiting for transfers between devices, send_back(): lax.all_to_all(values.reshape(chips, capacity, width), 'dpc', split_axis=...  27.7 us
    all_to_all x2, starting transfers between devices, combine(): lax.all_to_all(planes.astype(jnp.bfloat16), 'expert', split_axis=0, conca...  22.1 us
    all_to_all x2, starting transfers between devices, gather_features(): lax.all_to_all(spread_out, 'expert', split_axis=0, concat_axis=0, tiled=T...  22.1 us
    all_to_all x1, blocking collectives, dispatch(): lax.all_to_all(spread(send_buf), 'dpc', split_axis=0, concat_axis=0, tile...  16.6 us
    all_to_all x1, waiting for transfers between devices, dispatch(): lax.all_to_all(spread(send_buf), 'dpc', split_axis=0, concat_axis=0, tile...  11.9 us
    all_to_all x2, starting transfers between devices, send_back(): lax.all_to_all(values.reshape(chips, capacity, width), 'dpc', split_axis=...  8.34 us
  transfers between devices with their start and end apart: 10, of which 8 were waited for; matrix products, arithmetic and copies ran while one was open for 15% of the time, Pallas kernels for 0%

profile of v5, /device:TPU:32, one launch (start us, length us, event | category | flops | bytes accessed | tf_op | source)
XLA Modules:
  0.0 288.1 jit_solution(12798066105029507640)
XLA Ops:
  0.7 1.7 broadcast_in_dim.161
  2.4 15.2 %all-to-all-start.6 = ((bf16[16,128,128]{2,1,0:T(8,128)(2,1)}), bf16[16,128,128]{2,1,0:T(8,128)(2,1)S(1)}, u32[]{:S(2)}, u32[]{:S(2)}) async-start(bf16[16,128,128]{2,1,0:T(8,128)(2,1)} %broadcast_in_dim.161), calls=%async_computation.6 | async-start | bytes 1048576 | tf_op jit(solution)/shard_map/all_to_all | solution.py:47
  17.6 0.8 copy.33
  18.7 2.3 reduce-window.6
  21.6 24.5 %all-to-all-done.6 = bf16[16,128,128]{2,1,0:T(8,128)(2,1)S(1)} async-done(((bf16[16,128,128]{2,1,0:T(8,128)(2,1)}), bf16[16,128,128]{2,1,0:T(8,128)(2,1)S(1)}, u32[]{:S(2)}, u32[]{:S(2)}) %all-to-all-start.6) | async-done | bytes 524320 | tf_op jit(solution)/shard_map/all_to_all | solution.py:47
  46.1 0.9 broadcast_in_dim.151
  47.0 6.9 %all-to-all-start = ((bf16[16,128,128]{2,1,0:T(8,128)(2,1)}), bf16[16,128,128]{2,1,0:T(8,128)(2,1)S(1)}, u32[]{:S(2)}, u32[]{:S(2)}) async-start(bf16[16,128,128]{2,1,0:T(8,128)(2,1)} %broadcast_in_dim.151), calls=%async_computation | async-start | bytes 1048576 | tf_op jit(solution)/shard_map/all_to_all | solution.py:47
  54.2 4.3 %scatter_custom_fusion.1 = s32[128]{0:T(128)S(1)} fusion(s32[1024]{0:T(1024)S(1)} %bitcast.111, s32[1024]{0:T(1024)S(1)} %ne.90, s32[]{:T(128)} %constant.61.clone.1), kind=kCustom, calls=%fused_computation.118 | custom fusion | bytes 516 | tf_op jit(solution)/shard_map/scatter | solution.py:69
  58.5 4.3 %scatter_custom_fusion = s32[128]{0:T(128)S(1)} fusion(s32[1024]{0:T(1024)S(1)} %bitcast.112, s32[1024]{0:T(1024)S(1)} %iota.30, s32[]{:T(128)} %constant.61.clone.1), kind=kCustom, calls=%fused_computation.120 | custom fusion | bytes 516 | tf_op jit(solution)/shard_map/scatter | solution.py:67
  62.9 1.3 gather_fusion.1
  64.5 0.9 gather_fusion.2
  65.5 16.9 %all-to-all-done = bf16[16,128,128]{2,1,0:T(8,128)(2,1)S(1)} async-done(((bf16[16,128,128]{2,1,0:T(8,128)(2,1)}), bf16[16,128,128]{2,1,0:T(8,128)(2,1)S(1)}, u32[]{:S(2)}, u32[]{:S(2)}) %all-to-all-start) | async-done | bytes 524320 | tf_op jit(solution)/shard_map/all_to_all | solution.py:47
  82.4 1.1 broadcast_in_dim.162
  83.5 7.0 %all-to-all-start.7 = ((bf16[16,16,2048]{2,1,0:T(8,128)(2,1)}), bf16[16,16,2048]{2,1,0:T(8,128)(2,1)S(1)}, u32[]{:S(2)}, u32[]{:S(2)}) async-start(bf16[16,16,2048]{2,1,0:T(8,128)(2,1)} %bitcast.20), calls=%async_computation.7 | async-start | bytes 2097152 | tf_op jit(solution)/shard_map/all_to_all | solution.py:84
  90.7 0.9 gather_fusion
  91.8 11.9 %all-to-all-done.7 = bf16[16,16,2048]{2,1,0:T(8,128)(2,1)S(1)} async-done(((bf16[16,16,2048]{2,1,0:T(8,128)(2,1)}), bf16[16,16,2048]{2,1,0:T(8,128)(2,1)S(1)}, u32[]{:S(2)}, u32[]{:S(2)}) %all-to-all-start.7) | async-done | bytes 1048608 | tf_op jit(solution)/shard_map/all_to_all | solution.py:84
  103.7 16.6 %all_to_all.66 = bf16[16,16,2176]{2,1,0:T(8,128)(2,1)S(1)} all-to-all(bf16[16,16,2176]{2,1,0:T(8,128)(2,1)S(1)} %bitcast.95), channel_id=1, replica_groups=mesh['dpc'=16,'core'=2,'expert'=16] {'dpc'}, dimensions={0} | all-to-all | bytes 2228224 | tf_op jit(solution)/shard_map/all_to_all | solution.py:84
  120.5 6.4 %all_to_all.67 = bf16[2,16,16,2176]{3,2,1,0:T(8,128)(2,1)} all-to-all(bf16[2,16,16,2176]{3,2,1,0:T(8,128)(2,1)S(1)} %broadcast_in_dim.160), channel_id=1, replica_groups=mesh['dpc'=16,'core'=2,'expert'=16] {'core'}, dimensions={0} | all-to-all | bytes 4456448 | tf_op jit(solution)/shard_map/all_to_all | solution.py:85
  126.9 1.6 broadcast_in_dim.163
  128.5 4.9 %all-to-all-start.8 = ((bf16[2,16,16,2048]{3,2,1,0:T(8,128)(2,1)}), bf16[2,16,16,2048]{3,2,1,0:T(8,128)(2,1)}, u32[]{:S(2)}, u32[]{:S(2)}) async-start(bf16[2,16,16,2048]{3,2,1,0:T(8,128)(2,1)} %broadcast_in_dim.163), calls=%async_computation.8 | async-start | bytes 4194304 | tf_op jit(solution)/shard_map/all_to_all | solution.py:85
  133.6 2.8 fusion.6
  136.3 1.6 fusion.8
  137.9 2.7 multiply_reduce_fusion
  142.5 2.1 multiply_convert_fusion.1
  144.6 4.9 %all-to-all-start.3 = ((bf16[2,256,2048]{2,1,0:T(8,128)(2,1)}), bf16[2,256,2048]{2,1,0:T(8,128)(2,1)}, u32[]{:S(2)}, u32[]{:S(2)}) async-start(bf16[2,256,2048]{2,1,0:T(8,128)(2,1)} %bitcast.12), calls=%async_computation.3 | async-start | bytes 4194304 | tf_op jit(solution)/shard_map/all_to_all | solution.py:94
  149.6 0.7 fusion.20
  150.7 0.8 add_convert_fusion
  151.5 1.1 all-to-all-done.3
  152.6 3.2 %all-to-all-start.10 = ((bf16[2,2,128]{2,1,0:T(2,128)(2,1)}), bf16[2,2,128]{2,1,0:T(2,128)(2,1)S(1)}, u32[]{:S(2)}, u32[]{:S(2)}) async-start(bf16[2,2,128]{2,1,0:T(2,128)(2,1)} %reshape.435), calls=%async_computation.10 | async-start | bytes 2048 | tf_op jit(solution)/shard_map/all_to_all | solution.py:152
  155.8 3.3 %reduce_sum.76 = bf16[256,2048]{1,0:T(8,128)(2,1)} reduce(bf16[2,256,2048]{2,1,0:T(8,128)(2,1)} %all-to-all-done.3, bf16[]{:T(256)} %constant.71.clone.1), dimensions={0}, to_apply=%region_5.6 | reduce | flops 524288 | bytes 3145730 | tf_op jit(solution)/shard_map/reduce_sum | solution.py:97
  159.1 6.3 %all_to_all.68 = bf16[2,256,2048]{2,1,0:T(8,128)(2,1)} all-to-all(bf16[2,256,2048]{2,1,0:T(8,128)(2,1)S(1)} %bitcast.94), channel_id=1, replica_groups=mesh['dpc'=16,'core'=2,'expert'=16] {'core'}, dimensions={0} | all-to-all | bytes 4194304 | tf_op jit(solution)/shard_map/all_to_all | solution.py:94
  165.4 4.6 %all-to-all-start.4 = ((bf16[16,16,2048]{2,1,0:T(8,128)(2,1)}), bf16[16,16,2048]{2,1,0:T(8,128)(2,1)}, u32[]{:S(2)}, u32[]{:S(2)}) async-start(bf16[16,16,2048]{2,1,0:T(8,128)(2,1)} %bitcast.98), calls=%async_computation.4 | async-start | bytes 2097152 | tf_op jit(solution)/shard_map/all_to_all | solution.py:101
  170.3 1.8 reduce_sum.78
  172.3 2.3 pad_maximum_fusion
  174.6 13.7 %all-to-all-done.4 = bf16[16,16,2048]{2,1,0:T(8,128)(2,1)} async-done(((bf16[16,16,2048]{2,1,0:T(8,128)(2,1)}), bf16[16,16,2048]{2,1,0:T(8,128)(2,1)}, u32[]{:S(2)}, u32[]{:S(2)}) %all-to-all-start.4) | async-done | bytes 1048608 | tf_op jit(solution)/shard_map/all_to_all | solution.py:101
  188.3 3.7 %all-to-all-start.11 = ((bf16[16,16,2176]{2,1,0:T(8,128)(2,1)}), bf16[16,16,2176]{2,1,0:T(8,128)(2,1)S(1)}, u32[]{:S(2)}, u32[]{:S(2)}) async-start(bf16[16,16,2176]{2,1,0:T(8,128)(2,1)} %pad_maximum_fusion), calls=%async_computation.11 | async-start | bytes 2228224 | tf_op jit(solution)/shard_map/all_to_all | solution.py:101
  192.4 1.5 copy.38
  193.9 1.3 fusion.10
  195.2 14.0 %all-to-all-done.11 = bf16[16,16,2176]{2,1,0:T(8,128)(2,1)S(1)} async-done(((bf16[16,16,2176]{2,1,0:T(8,128)(2,1)}), bf16[16,16,2176]{2,1,0:T(8,128)(2,1)S(1)}, u32[]{:S(2)}, u32[]{:S(2)}) %all-to-all-start.11) | async-done | bytes 1114144 | tf_op jit(solution)/shard_map/all_to_all | solution.py:101
  209.1 14.6 %all-to-all-start.5 = ((bf16[16,128,128]{2,1,0:T(8,128)(2,1)}), bf16[16,128,128]{2,1,0:T(8,128)(2,1)S(1)}, u32[]{:S(2)}, u32[]{:S(2)}) async-start(bf16[16,128,128]{2,1,0:T(8,128)(2,1)} %fusion.10), calls=%async_computation.5 | async-start | bytes 1048576 | tf_op jit(solution)/shard_map/all_to_all | solution.py:118
  224.8 0.9 pad_maximum_fusion.1
  225.7 23.4 %all-to-all-done.5 = bf16[16,128,128]{2,1,0:T(8,128)(2,1)S(1)} async-done(((bf16[16,128,128]{2,1,0:T(8,128)(2,1)}), bf16[16,128,128]{2,1,0:T(8,128)(2,1)S(1)}, u32[]{:S(2)}, u32[]{:S(2)}) %all-to-all-start.5) | async-done | bytes 524320 | tf_op jit(solution)/shard_map/all_to_all | solution.py:118
  249.1 7.5 %all-to-all-start.12 = ((bf16[16,129,128]{2,1,0:T(8,128)(2,1)}), bf16[16,129,128]{2,1,0:T(8,128)(2,1)}, u32[]{:S(2)}, u32[]{:S(2)}) async-start(bf16[16,129,128]{2,1,0:T(8,128)(2,1)} %pad_maximum_fusion.1), calls=%async_computation.12 | async-start | bytes 1114112 | tf_op jit(solution)/shard_map/all_to_all | solution.py:118
  256.7 3.2 %fusion = bf16[1,192,2048]{2,1,0:T(8,128)(2,1)} fusion(bf16[512,192]{0,1:T(8,128)(2,1)} %copy-done.7, bf16[512,2176]{1,0:T(8,128)(2,1)} %bitcast.101), kind=kOutput, calls=%fused_computation.11 | convolution fusion | flops 403046400 | bytes 3080192 | tf_op jit(solution)/shard_map/dot_general | solution.py:17
  259.9 1.5 fusion.1
  261.4 3.2 %fusion.2 = bf16[1,192,2048]{2,1,0:T(8,128)(2,1)} fusion(bf16[512,192]{0,1:T(8,128)(2,1)S(1)} %copy-done.13, bf16[512,2048]{1,0:T(8,128)(2,1)} %bitcast.21, f32[512]{0:T(512)S(1)} %convert_reduce_fusion.1), kind=kOutput, calls=%fused_computation.13 | convolution fusion | flops 406192128 | bytes 3082240 | tf_op jit(solution)/shard_map/dot_general | solution.py:17
  265.2 20.4 %all-to-all-done.12 = bf16[16,129,128]{2,1,0:T(8,128)(2,1)} async-done(((bf16[16,129,128]{2,1,0:T(8,128)(2,1)}), bf16[16,129,128]{2,1,0:T(8,128)(2,1)}, u32[]{:S(2)}, u32[]{:S(2)}) %all-to-all-start.12) | async-done | bytes 528416 | tf_op jit(solution)/shard_map/all_to_all | solution.py:118
  285.6 1.1 convert_reduce_fusion
  (94 shorter events, 8.2 us)
Async XLA Ops:
  0.6 137.3 %copy-start = (bf16[1,192,2048]{2,1,0:T(8,128)(2,1)S(1)}, bf16[1,192,2048]{2,1,0:T(8,128)(2,1)}, u32[]{:S(2)}) copy-start(bf16[1,192,2048]{2,1,0:T(8,128)(2,1)} %param.12) | copy-start | bytes 2359300
  0.6 45.5 %copy-start.10 = (bf16[128,128]{1,0:T(8,128)(2,1)S(1)}, bf16[128,128]{1,0:T(8,128)(2,1)}, u32[]{:S(2)}) copy-start(bf16[128,128]{1,0:T(8,128)(2,1)} %param.7) | copy-start | bytes 98308
  0.7 53.3 %copy-start.11 = (bf16[128,8]{0,1:T(8,128)(2,1)S(1)}, bf16[128,8]{0,1:T(8,128)(2,1)}, u32[]{:S(2)}) copy-start(bf16[128,8]{0,1:T(8,128)(2,1)} %param.8) | copy-start | bytes 6148
  2.4 43.7 %all-to-all-start.6 = ((bf16[16,128,128]{2,1,0:T(8,128)(2,1)}), bf16[16,128,128]{2,1,0:T(8,128)(2,1)S(1)}, u32[]{:S(2)}, u32[]{:S(2)}) async-start(bf16[16,128,128]{2,1,0:T(8,128)(2,1)} %broadcast_in_dim.161), calls=%async_computation.6 | async-start | bytes 1048576 | tf_op jit(solution)/shard_map/all_to_all | solution.py:47
  47.0 35.4 %all-to-all-start = ((bf16[16,128,128]{2,1,0:T(8,128)(2,1)}), bf16[16,128,128]{2,1,0:T(8,128)(2,1)S(1)}, u32[]{:S(2)}, u32[]{:S(2)}) async-start(bf16[16,128,128]{2,1,0:T(8,128)(2,1)} %broadcast_in_dim.151), calls=%async_computation | async-start | bytes 1048576 | tf_op jit(solution)/shard_map/all_to_all | solution.py:47
  83.5 20.1 %all-to-all-start.7 = ((bf16[16,16,2048]{2,1,0:T(8,128)(2,1)}), bf16[16,16,2048]{2,1,0:T(8,128)(2,1)S(1)}, u32[]{:S(2)}, u32[]{:S(2)}) async-start(bf16[16,16,2048]{2,1,0:T(8,128)(2,1)} %bitcast.20), calls=%async_computation.7 | async-start | bytes 2097152 | tf_op jit(solution)/shard_map/all_to_all | solution.py:84
  128.5 5.0 %copy-start.2 = (bf16[2,16,16,2176]{3,2,1,0:T(8,128)(2,1)S(1)}, bf16[2,16,16,2176]{3,2,1,0:T(8,128)(2,1)}, u32[]{:S(2)}) copy-start(bf16[2,16,16,2176]{3,2,1,0:T(8,128)(2,1)} %all_to_all.67) | copy-start | bytes 6684676
  128.5 9.5 %all-to-all-start.8 = ((bf16[2,16,16,2048]{3,2,1,0:T(8,128)(2,1)}), bf16[2,16,16,2048]{3,2,1,0:T(8,128)(2,1)}, u32[]{:S(2)}, u32[]{:S(2)}) async-start(bf16[2,16,16,2048]{3,2,1,0:T(8,128)(2,1)} %broadcast_in_dim.163), calls=%async_computation.8 | async-start | bytes 4194304 | tf_op jit(solution)/shard_map/all_to_all | solution.py:85
  133.5 2.8 copy-start.4
  140.7 4.0 %copy-start.12 = (bf16[512,192]{0,1:T(8,128)(2,1)}, bf16[512,192]{0,1:T(8,128)(2,1)S(1)}, u32[]{:S(2)}) copy-start(bf16[512,192]{0,1:T(8,128)(2,1)S(1)} %get-tuple-element.9) | copy-start | bytes 589828
  140.7 8.9 %copy-start.7 = (bf16[512,192]{0,1:T(8,128)(2,1)}, bf16[512,192]{0,1:T(8,128)(2,1)S(1)}, u32[]{:S(2)}) copy-start(bf16[512,192]{0,1:T(8,128)(2,1)S(1)} %get-tuple-element.12) | copy-start | bytes 589828
  140.7 9.7 %copy-start.8 = (bf16[512,192]{0,1:T(8,128)(2,1)}, bf16[512,192]{0,1:T(8,128)(2,1)S(1)}, u32[]{:S(2)}) copy-start(bf16[512,192]{0,1:T(8,128)(2,1)S(1)} %get-tuple-element.13) | copy-start | bytes 589828
  144.6 5.0 %copy-start.5 = (bf16[1,192,2048]{2,1,0:T(8,128)(2,1)S(1)}, bf16[1,192,2048]{2,1,0:T(8,128)(2,1)}, u32[]{:S(2)}) copy-start(bf16[1,192,2048]{2,1,0:T(8,128)(2,1)} %param.10) | copy-start | bytes 2359300
  144.6 7.9 %all-to-all-start.3 = ((bf16[2,256,2048]{2,1,0:T(8,128)(2,1)}), bf16[2,256,2048]{2,1,0:T(8,128)(2,1)}, u32[]{:S(2)}, u32[]{:S(2)}) async-start(bf16[2,256,2048]{2,1,0:T(8,128)(2,1)} %bitcast.12), calls=%async_computation.3 | async-start | bytes 4194304 | tf_op jit(solution)/shard_map/all_to_all | solution.py:94
  149.6 1.1 copy-start.6
  152.6 6.5 %all-to-all-start.10 = ((bf16[2,2,128]{2,1,0:T(2,128)(2,1)}), bf16[2,2,128]{2,1,0:T(2,128)(2,1)S(1)}, u32[]{:S(2)}, u32[]{:S(2)}) async-start(bf16[2,2,128]{2,1,0:T(2,128)(2,1)} %reshape.435), calls=%async_computation.10 | async-start | bytes 2048 | tf_op jit(solution)/shard_map/all_to_all | solution.py:152
  165.4 4.9 %copy-start.1 = (bf16[2,256,2048]{2,1,0:T(8,128)(2,1)S(1)}, bf16[2,256,2048]{2,1,0:T(8,128)(2,1)}, u32[]{:S(2)}) copy-start(bf16[2,256,2048]{2,1,0:T(8,128)(2,1)} %all_to_all.68) | copy-start | bytes 6291460
  165.4 22.9 %all-to-all-start.4 = ((bf16[16,16,2048]{2,1,0:T(8,128)(2,1)}), bf16[16,16,2048]{2,1,0:T(8,128)(2,1)}, u32[]{:S(2)}, u32[]{:S(2)}) async-start(bf16[16,16,2048]{2,1,0:T(8,128)(2,1)} %bitcast.98), calls=%async_computation.4 | async-start | bytes 2097152 | tf_op jit(solution)/shard_map/all_to_all | solution.py:101
  188.3 20.8 %all-to-all-start.11 = ((bf16[16,16,2176]{2,1,0:T(8,128)(2,1)}), bf16[16,16,2176]{2,1,0:T(8,128)(2,1)S(1)}, u32[]{:S(2)}, u32[]{:S(2)}) async-start(bf16[16,16,2176]{2,1,0:T(8,128)(2,1)} %pad_maximum_fusion), calls=%async_computation.11 | async-start | bytes 2228224 | tf_op jit(solution)/shard_map/all_to_all | solution.py:101
  209.1 40.0 %all-to-all-start.5 = ((bf16[16,128,128]{2,1,0:T(8,128)(2,1)}), bf16[16,128,128]{2,1,0:T(8,128)(2,1)S(1)}, u32[]{:S(2)}, u32[]{:S(2)}) async-start(bf16[16,128,128]{2,1,0:T(8,128)(2,1)} %fusion.10), calls=%async_computation.5 | async-start | bytes 1048576 | tf_op jit(solution)/shard_map/all_to_all | solution.py:118
  225.7 34.2 %copy-start.3 = (bf16[2,16,16,2176]{3,2,1,0:T(8,128)(2,1)S(1)}, bf16[2,16,16,2176]{3,2,1,0:T(8,128)(2,1)}, u32[]{:S(2)}) copy-start(bf16[2,16,16,2176]{3,2,1,0:T(8,128)(2,1)} %all_to_all.67) | copy-start | bytes 6684676
  249.1 36.5 %all-to-all-start.12 = ((bf16[16,129,128]{2,1,0:T(8,128)(2,1)}), bf16[16,129,128]{2,1,0:T(8,128)(2,1)}, u32[]{:S(2)}, u32[]{:S(2)}) async-start(bf16[16,129,128]{2,1,0:T(8,128)(2,1)} %pad_maximum_fusion.1), calls=%async_computation.12 | async-start | bytes 1114112 | tf_op jit(solution)/shard_map/all_to_all | solution.py:118
  256.7 3.2 %copy-start.9 = (bf16[512,192]{0,1:T(8,128)(2,1)S(1)}, bf16[512,192]{0,1:T(8,128)(2,1)}, u32[]{:S(2)}) copy-start(bf16[512,192]{0,1:T(8,128)(2,1)} %copy-done.8) | copy-start | bytes 589828
  259.9 1.5 copy-start.13

commit v6 on v4

--- a/solution.py
+++ b/solution.py
@@ -119,17 +119,15 @@
     grad_up = contract_first(up_grad, slot_rows).astype(jnp.bfloat16)[None]
     grad_down = contract_first(hidden, scaled_grad).astype(jnp.bfloat16)[None]
 
-    core_index = lax.axis_index("core")
-    piece_buf = jnp.concatenate([scaled, row_grad], axis=1).reshape(cores, -1, 2 * feature_width)
+    piece_buf = jnp.concatenate(
+        [scaled, row_grad, column_block(route_terms, jnp.bfloat16)], axis=1
+    ).reshape(cores, -1, row_width)
     pair = lax.all_to_all(piece_buf, "core", split_axis=0, concat_axis=0, tiled=True)
-    pair_terms = lax.all_to_all(
-        route_terms.reshape(cores, -1), "core", split_axis=0, concat_axis=0, tiled=True
-    )
-    pair_sum = jnp.sum(pair.astype(jnp.float32), axis=0).astype(jnp.bfloat16)
+    pair_sum = jnp.sum(pair[:, :, : 2 * feature_width].astype(jnp.float32), axis=0).astype(jnp.bfloat16)
     lane = jnp.arange(PAD, dtype=jnp.int32)[None, :]
-    term_block = jnp.zeros((pair_terms.shape[1], PAD), jnp.bfloat16)
+    term_block = jnp.zeros((pair.shape[1], PAD), jnp.bfloat16)
     for k in range(cores):
-        term_block = jnp.where(lane == k, pair_terms[k][:, None], term_block)
+        term_block = jnp.where(lane == k, pair[k, :, 2 * feature_width : 2 * feature_width + 1], term_block)
     back_buf = jnp.concatenate([pair_sum, term_block], axis=1)
     back = lax.all_to_all(
         back_buf.reshape(chips, capacity, row_width),

time: 253 us -> 258 us (1.020)
  local copies, waits for them, and re-layouts: 26.9 us -> 38.3 us
  starting transfers between devices: 48.8 us -> 43.4 us
  blocking collectives: 11 us -> 15.9 us
  waiting for transfers between devices: 135 us -> 131 us
    reshape x0 -> x1, local copies, waits for them, and re-layouts: none -> 6.47 us  [on_device(): piece_buf = jnp.concatenate([scaled, row_grad, column_block(route_terms,...]
    all_to_all x1 -> x0, starting transfers between devices: 5.77 us -> none  [on_device(): lax.all_to_all(piece_buf, 'core', split_axis=0, concat_axis=0, tiled=True)]
    all_to_all x1, blocking collectives: 3.69 us -> 8.59 us  [on_device(): lax.all_to_all(piece_buf, 'core', split_axis=0, concat_axis=0, tiled=True)]
    all_to_all x1 -> x0, waiting for transfers between devices: 4.16 us -> none  [on_device(): lax.all_to_all(piece_buf, 'core', split_axis=0, concat_axis=0, tiled=True)]
    reduce_sum x0 -> x1, local copies, waits for them, and re-layouts: none -> 2.87 us  [on_device(): jnp.sum(pair[:, :, :2 * feature_width].astype(jnp.float32), axis=0)]
  transfers between devices with their start and end apart: 5 -> 4, of which waited for: 5 -> 4; matrix products, arithmetic and copies ran while one was open for 9% -> 9% of each run, Pallas kernels for 0% -> 0%
where the time goes in v6:
time: 258 us; the launch traced here: 257 us
  waiting for transfers between devices  131 us (51%)
  starting transfers between devices  43.4 us (17%)
  local copies, waits for them, and re-layouts  38.3 us (15%)
  blocking collectives  15.9 us (6%)
  matrix products  15 us (6%)
  other arithmetic  12.8 us (5%)
    all_to_all x1, waiting for transfers between devices, on_device(): lax.all_to_all(packed, 'expert', split_axis=0, concat_axis=0, tiled=True)  42.3 us
    all_to_all x1, waiting for transfers between devices, on_device(): lax.all_to_all(jnp.broadcast_to(both[None], (groups,) + both.shape), 'exp...  36.1 us
    all_to_all x1, waiting for transfers between devices, on_device(): lax.all_to_all(back_buf.reshape(chips, capacity, row_width), 'dpc', split...  29.3 us
    all_to_all x1, waiting for transfers between devices, on_device(): lax.all_to_all(spread(send_buf), 'dpc', split_axis=0, concat_axis=0, tile...  23 us
    all_to_all x1, starting transfers between devices, on_device(): lax.all_to_all(jnp.broadcast_to(both[None], (groups,) + both.shape), 'exp...  15.2 us
    all_to_all x1, starting transfers between devices, on_device(): lax.all_to_all(packed, 'expert', split_axis=0, concat_axis=0, tiled=True)  13.8 us
    dot_general x3, matrix products, contract_first(): lax.dot_general(left_side, right_side, (((0,), (0,)), ((), ())), preferre...  9.33 us
    all_to_all x1, blocking collectives, on_device(): lax.all_to_all(piece_buf, 'core', split_axis=0, concat_axis=0, tiled=True)  8.59 us
  transfers between devices with their start and end apart: 4, of which 4 were waited for; matrix products, arithmetic and copies ran while one was open for 9% of the time, Pallas kernels for 0%

profile of v6, /device:TPU:16, one launch (start us, length us, event | category | flops | bytes accessed | tf_op | source)
XLA Modules:
  0.0 257.2 jit_solution(15656955419486601688)
XLA Ops:
  0.7 0.9 pad_maximum_fusion.3
  1.6 1.2 broadcast_in_dim.155
  2.8 15.2 %all-to-all-start = ((bf16[16,128,256]{1,2,0:T(8,128)(2,1)}), bf16[16,128,256]{1,2,0:T(8,128)(2,1)S(1)}, u32[]{:S(2)}, u32[]{:S(2)}) async-start(bf16[16,128,256]{1,2,0:T(8,128)(2,1)} %broadcast_in_dim.155), calls=%async_computation | async-start | bytes 2097152 | tf_op jit(solution)/shard_map/all_to_all | solution.py:44
  18.7 2.3 reduce-window.6
  21.6 4.3 %scatter_custom_fusion.1 = s32[128]{0:T(128)S(1)} fusion(s32[1024]{0:T(1024)S(1)} %bitcast.93, s32[1024]{0:T(1024)S(1)} %ne.90, s32[]{:T(128)} %constant.59.clone.1), kind=kCustom, calls=%fused_computation.114 | custom fusion | bytes 516 | tf_op jit(solution)/shard_map/scatter | solution.py:72
  26.0 4.3 %scatter_custom_fusion = s32[128]{0:T(128)S(1)} fusion(s32[1024]{0:T(1024)S(1)} %bitcast.94, s32[1024]{0:T(1024)S(1)} %iota.33, s32[]{:T(128)} %constant.59.clone.1), kind=kCustom, calls=%fused_computation.116 | custom fusion | bytes 516 | tf_op jit(solution)/shard_map/scatter | solution.py:70
  30.4 1.3 gather_fusion.1
  31.9 36.1 %all-to-all-done = bf16[16,128,256]{1,2,0:T(8,128)(2,1)S(1)} async-done(((bf16[16,128,256]{1,2,0:T(8,128)(2,1)}), bf16[16,128,256]{1,2,0:T(8,128)(2,1)S(1)}, u32[]{:S(2)}, u32[]{:S(2)}) %all-to-all-start) | async-done | bytes 1048608 | tf_op jit(solution)/shard_map/all_to_all | solution.py:44
  68.0 1.0 copy.53
  69.0 0.5 copy.71
  69.4 1.2 gather_fusion
  70.8 1.5 broadcast_in_dim.163
  72.3 7.3 %all-to-all-start.1 = ((bf16[16,16,4224]{2,1,0:T(8,128)(2,1)}), bf16[16,16,4224]{2,1,0:T(8,128)(2,1)S(1)}, u32[]{:S(2)}, u32[]{:S(2)}) async-start(bf16[16,16,4224]{2,1,0:T(8,128)(2,1)} %bitcast.75), calls=%async_computation.1 | async-start | bytes 4325376 | tf_op jit(solution)/shard_map/all_to_all | solution.py:88
  79.6 23.0 %all-to-all-done.1 = bf16[16,16,4224]{2,1,0:T(8,128)(2,1)S(1)} async-done(((bf16[16,16,4224]{2,1,0:T(8,128)(2,1)}), bf16[16,16,4224]{2,1,0:T(8,128)(2,1)S(1)}, u32[]{:S(2)}, u32[]{:S(2)}) %all-to-all-start.1) | async-done | bytes 2162720 | tf_op jit(solution)/shard_map/all_to_all | solution.py:88
  102.6 0.3 broadcast_in_dim.164
  102.9 7.3 %all_to_all.30 = bf16[2,16,16,4224]{3,2,1,0:T(8,128)(2,1)S(1)} all-to-all(bf16[2,16,16,4224]{3,2,1,0:T(8,128)(2,1)S(1)} %broadcast_in_dim.164), channel_id=1, replica_groups=mesh['dpc'=16,'core'=2,'expert'=16] {'core'}, dimensions={0} | all-to-all | bytes 8650752 | tf_op jit(solution)/shard_map/all_to_all | solution.py:89
  110.4 0.8 fusion.13
  111.3 0.9 copy-done.3
  112.1 0.8 fusion.15
  113.0 1.0 multiply_reduce_fusion
  114.1 0.7 multiply_convert_fusion.1
  114.9 0.7 fusion.23
  115.6 0.8 add_convert_fusion
  116.4 2.2 pad_maximum_fusion
  118.6 6.5 %copy.55 = bf16[2,256,4224]{1,2,0:T(8,128)(2,1)} copy(bf16[2,256,4224]{2,1,0:T(8,128)(2,1)} %bitcast.74) | data formatting | bytes 8650752 | tf_op jit(solution)/shard_map/reshape | solution.py:124
  125.1 8.6 %all_to_all.31 = bf16[2,256,4224]{1,2,0:T(8,128)(2,1)S(1)} all-to-all(bf16[2,256,4224]{1,2,0:T(8,128)(2,1)} %copy.55), channel_id=1, replica_groups=mesh['dpc'=16,'core'=2,'expert'=16] {'core'}, dimensions={0} | all-to-all | bytes 8650752 | tf_op jit(solution)/shard_map/all_to_all | solution.py:125
  133.7 2.0 copy-done.1
  135.7 0.7 slice_reduce_fusion
  136.4 2.9 %copy.56 = bf16[256,4096]{1,0:T(8,128)(2,1)} copy(bf16[256,4096]{0,1:T(8,128)(2,1)S(1)} %slice_reduce_fusion) | data formatting | bytes 4194304 | tf_op jit(solution)/shard_map/reduce_sum | solution.py:126
  139.3 0.7 slice_reduce_fusion.4
  140.3 3.1 %pad_maximum_fusion.1 = bf16[16,16,4224]{2,1,0:T(8,128)(2,1)} fusion(bf16[16,16,128]{2,1,0:T(8,128)(2,1)S(1)} %select_select_fusion, bf16[16,16,4096]{2,1,0:T(8,128)(2,1)} %bitcast.78), kind=kLoop, calls=%fused_computation.16 | loop fusion | flops 4325376 | bytes 4325376 | tf_op jit(solution)/shard_map/concatenate | solution.py:131
  143.4 7.1 %all-to-all-start.4 = ((bf16[16,16,4224]{2,1,0:T(8,128)(2,1)}), bf16[16,16,4224]{2,1,0:T(8,128)(2,1)S(1)}, u32[]{:S(2)}, u32[]{:S(2)}) async-start(bf16[16,16,4224]{2,1,0:T(8,128)(2,1)} %pad_maximum_fusion.1), calls=%async_computation.4 | async-start | bytes 4325376 | tf_op jit(solution)/shard_map/all_to_all | solution.py:132
  151.0 29.3 %all-to-all-done.4 = bf16[16,16,4224]{2,1,0:T(8,128)(2,1)S(1)} async-done(((bf16[16,16,4224]{2,1,0:T(8,128)(2,1)}), bf16[16,16,4224]{2,1,0:T(8,128)(2,1)S(1)}, u32[]{:S(2)}, u32[]{:S(2)}) %all-to-all-start.4) | async-done | bytes 2162720 | tf_op jit(solution)/shard_map/all_to_all | solution.py:132
  180.3 0.3 convolution_reduce_fusion
  180.6 0.5 fusion.8
  181.3 1.8 copy.57
  183.2 1.4 copy.58
  184.6 2.0 pad_maximum_fusion.2
  186.6 2.2 copy.59
  188.8 13.8 %all-to-all-start.5 = ((bf16[16,129,256]{2,1,0:T(8,128)(2,1)}), bf16[16,129,256]{2,1,0:T(8,128)(2,1)S(1)}, u32[]{:S(2)}, u32[]{:S(2)}) async-start(bf16[16,129,256]{2,1,0:T(8,128)(2,1)} %copy.59), calls=%async_computation.5 | async-start | bytes 2228224 | tf_op jit(solution)/shard_map/all_to_all | solution.py:164
  202.6 3.1 %fusion = bf16[1,192,2048]{2,1,0:T(8,128)(2,1)} fusion(bf16[512,192]{0,1:T(8,128)(2,1)S(1)} %get-tuple-element.30, bf16[512,4224]{1,0:T(8,128)(2,1)} %bitcast.83), kind=kOutput, calls=%fused_computation.13 | convolution fusion | flops 403046400 | bytes 3080192 | tf_op jit(solution)/shard_map/dot_general | solution.py:17
  205.7 3.1 %fusion.1 = bf16[1,192,2048]{2,1,0:T(8,128)(2,1)} fusion(bf16[512,192]{0,1:T(8,128)(2,1)S(1)} %get-tuple-element.31, bf16[512,4224]{1,0:T(8,128)(2,1)} %bitcast.84), kind=kOutput, calls=%fused_computation.14 | convolution fusion | flops 403046400 | bytes 3080192 | tf_op jit(solution)/shard_map/dot_general | solution.py:17
  208.8 3.2 %fusion.2 = bf16[1,192,2048]{2,1,0:T(8,128)(2,1)} fusion(bf16[512,192]{0,1:T(8,128)(2,1)S(1)} %copy-done.8, f32[512]{0:T(512)S(1)} %convert_reduce_fusion.1, bf16[512,4224]{1,0:T(8,128)(2,1)} %bitcast.85), kind=kOutput, calls=%fused_computation.15 | convolution fusion | flops 406192128 | bytes 3082240 | tf_op jit(solution)/shard_map/dot_general | solution.py:17
  211.9 42.3 %all-to-all-done.5 = bf16[16,129,256]{2,1,0:T(8,128)(2,1)S(1)} async-done(((bf16[16,129,256]{2,1,0:T(8,128)(2,1)}), bf16[16,129,256]{2,1,0:T(8,128)(2,1)S(1)}, u32[]{:S(2)}, u32[]{:S(2)}) %all-to-all-start.5) | async-done | bytes 1056800 | tf_op jit(solution)/shard_map/all_to_all | solution.py:164
  254.2 0.5 convert_reduce_fusion
  255.0 0.7 copy.63
  255.8 0.7 reshape_squeeze.3
  256.4 0.7 copy.62
  (68 shorter events, 3.6 us)
Async XLA Ops:
  0.6 112.3 %copy-start = (bf16[1,192,2048]{2,1,0:T(8,128)(2,1)S(1)}, bf16[1,192,2048]{2,1,0:T(8,128)(2,1)}, u32[]{:S(2)}) copy-start(bf16[1,192,2048]{2,1,0:T(8,128)(2,1)} %param.12) | copy-start | bytes 2359300
  0.6 17.4 %copy-start.5 = (s32[128,8]{0,1:T(8,128)S(1)}, s32[128,8]{0,1:T(8,128)}, u32[]{:S(2)}) copy-start(s32[128,8]{0,1:T(8,128)} %param.9) | copy-start | bytes 12292
  0.7 17.8 %copy-start.6 = (bf16[128,8]{0,1:T(8,128)(2,1)S(1)}, bf16[128,8]{0,1:T(8,128)(2,1)}, u32[]{:S(2)}) copy-start(bf16[128,8]{0,1:T(8,128)(2,1)} %param.8) | copy-start | bytes 6148
  2.8 65.1 %all-to-all-start = ((bf16[16,128,256]{1,2,0:T(8,128)(2,1)}), bf16[16,128,256]{1,2,0:T(8,128)(2,1)S(1)}, u32[]{:S(2)}, u32[]{:S(2)}) async-start(bf16[16,128,256]{1,2,0:T(8,128)(2,1)} %broadcast_in_dim.155), calls=%async_computation | async-start | bytes 2097152 | tf_op jit(solution)/shard_map/all_to_all | solution.py:44
  72.3 30.3 %all-to-all-start.1 = ((bf16[16,16,4224]{2,1,0:T(8,128)(2,1)}), bf16[16,16,4224]{2,1,0:T(8,128)(2,1)S(1)}, u32[]{:S(2)}, u32[]{:S(2)}) async-start(bf16[16,16,4224]{2,1,0:T(8,128)(2,1)} %bitcast.75), calls=%async_computation.1 | async-start | bytes 4325376 | tf_op jit(solution)/shard_map/all_to_all | solution.py:88
  102.9 7.5 %copy-start.4 = (bf16[1,192,2048]{2,1,0:T(8,128)(2,1)S(1)}, bf16[1,192,2048]{2,1,0:T(8,128)(2,1)}, u32[]{:S(2)}) copy-start(bf16[1,192,2048]{2,1,0:T(8,128)(2,1)} %param.11) | copy-start | bytes 2359300
  110.3 2.7 %copy-start.2 = (bf16[2,16,16,4224]{3,2,1,0:T(8,128)(2,1)}, bf16[2,16,16,4224]{3,2,1,0:T(8,128)(2,1)S(1)}, u32[]{:S(2)}) copy-start(bf16[2,16,16,4224]{3,2,1,0:T(8,128)(2,1)S(1)} %all_to_all.30) | copy-start | bytes 12976132
  110.4 1.7 copy-start.3
  114.0 1.6 copy-start.7
  133.7 2.0 copy-start.1
  143.4 36.9 %all-to-all-start.4 = ((bf16[16,16,4224]{2,1,0:T(8,128)(2,1)}), bf16[16,16,4224]{2,1,0:T(8,128)(2,1)S(1)}, u32[]{:S(2)}, u32[]{:S(2)}) async-start(bf16[16,16,4224]{2,1,0:T(8,128)(2,1)} %pad_maximum_fusion.1), calls=%async_computation.4 | async-start | bytes 4325376 | tf_op jit(solution)/shard_map/all_to_all | solution.py:132
  188.8 65.5 %all-to-all-start.5 = ((bf16[16,129,256]{2,1,0:T(8,128)(2,1)}), bf16[16,129,256]{2,1,0:T(8,128)(2,1)S(1)}, u32[]{:S(2)}, u32[]{:S(2)}) async-start(bf16[16,129,256]{2,1,0:T(8,128)(2,1)} %copy.59), calls=%async_computation.5 | async-start | bytes 2228224 | tf_op jit(solution)/shard_map/all_to_all | solution.py:164
  205.7 3.1 %copy-start.8 = (bf16[512,192]{0,1:T(8,128)(2,1)S(1)}, bf16[512,192]{0,1:T(8,128)(2,1)}, u32[]{:S(2)}) copy-start(bf16[512,192]{0,1:T(8,128)(2,1)} %copy-done.7) | copy-start | bytes 589828

commit v7 on v4

--- a/solution.py
+++ b/solution.py
@@ -86,12 +86,10 @@
         [full_both[token_of] * keep_mask, column_block(slot_weight, tokens.dtype)], axis=1
     )
     half_buf = lax.all_to_all(spread(send_buf), "dpc", split_axis=0, concat_axis=0, tiled=True)
-    recv_buf = lax.all_to_all(
-        jnp.broadcast_to(half_buf[None], (cores,) + half_buf.shape),
-        "core",
-        split_axis=0,
-        concat_axis=0,
-        tiled=True,
+    other_buf = lax.ppermute(half_buf, "core", [(k, (k + 1) % cores) for k in range(cores)])
+    first = lax.axis_index("core") == 0
+    recv_buf = jnp.where(
+        first, jnp.stack([half_buf, other_buf]), jnp.stack([other_buf, half_buf])
     ).reshape(-1, row_width)
     slot_rows = recv_buf[:, :feature_width]
     slot_grads = recv_buf[:, feature_width : 2 * feature_width]

time: 253 us -> 251 us (level)
  blocking collectives: 11 us -> 32.6 us
  waiting for transfers between devices: 135 us -> 117 us
  starting transfers between devices: 48.8 us -> 42.1 us
  other arithmetic: 14.5 us -> 17.5 us
    all_to_all x1 -> x0, waiting for transfers between devices: 23 us -> none  [on_device(): lax.all_to_all(spread(send_buf), 'dpc', split_axis=0, concat_axis=0, tile...]
    all_to_all x1, blocking collectives: 7.34 us -> 28.9 us  [on_device(): lax.all_to_all(spread(send_buf), 'dpc', split_axis=0, concat_axis=0, tile...]
    all_to_all x1 -> x0, starting transfers between devices: 7.28 us -> none  [on_device(): lax.all_to_all(spread(send_buf), 'dpc', split_axis=0, concat_axis=0, tile...]
    ppermute x0 -> x1, waiting for transfers between devices: none -> 4.33 us  [on_device(): lax.ppermute(half_buf, 'core', [(k, (k + 1) % cores) for k in range(cores)])]
    select_n x0 -> x1, other arithmetic: none -> 2.94 us  [on_device(): jnp.where(first, jnp.stack([half_buf, other_buf]), jnp.stack([other_buf,...]
where the time goes in v7:
time: 251 us
  waiting for transfers between devices  117 us (47%)
  starting transfers between devices  42.1 us (17%)
  blocking collectives  32.6 us (13%)
  local copies, waits for them, and re-layouts  25.7 us (10%)
  other arithmetic  17.5 us (7%)
  matrix products  15 us (6%)
    all_to_all x1, waiting for transfers between devices, on_device(): lax.all_to_all(packed, 'expert', split_axis=0, concat_axis=0, tiled=True)  42.3 us
    all_to_all x1, waiting for transfers between devices, on_device(): lax.all_to_all(jnp.broadcast_to(both[None], (groups,) + both.shape), 'exp...  36.1 us
    all_to_all x1, waiting for transfers between devices, on_device(): lax.all_to_all(back_buf.reshape(chips, capacity, row_width), 'dpc', split...  29.8 us
    all_to_all x1, blocking collectives, on_device(): lax.all_to_all(spread(send_buf), 'dpc', split_axis=0, concat_axis=0, tile...  28.9 us
    all_to_all x1, starting transfers between devices, on_device(): lax.all_to_all(jnp.broadcast_to(both[None], (groups,) + both.shape), 'exp...  15.2 us
    all_to_all x1, starting transfers between devices, on_device(): lax.all_to_all(packed, 'expert', split_axis=0, concat_axis=0, tiled=True)  13.6 us
    dot_general x3, matrix products, contract_first(): lax.dot_general(left_side, right_side, (((0,), (0,)), ((), ())), preferre...  9.32 us
    all_to_all x1, starting transfers between devices, on_device(): lax.all_to_all(piece_buf, 'core', split_axis=0, concat_axis=0, tiled=True)  5.77 us
  transfers between devices with their start and end apart: 5, of which 5 were waited for; matrix products, arithmetic and copies ran while one was open for 9% of the time, Pallas kernels for 0%

profile of v7, /device:TPU:16, one launch (start us, length us, event | category | flops | bytes accessed | tf_op | source)
XLA Modules:
  0.0 250.7 jit_solution(8837860964764238762)
XLA Ops:
  0.7 0.9 pad_maximum_fusion.3
  1.6 1.2 broadcast_in_dim.127
  2.8 15.2 %all-to-all-start = ((bf16[16,128,256]{1,2,0:T(8,128)(2,1)}), bf16[16,128,256]{1,2,0:T(8,128)(2,1)S(1)}, u32[]{:S(2)}, u32[]{:S(2)}) async-start(bf16[16,128,256]{1,2,0:T(8,128)(2,1)} %broadcast_in_dim.127), calls=%async_computation | async-start | bytes 2097152 | tf_op jit(solution)/shard_map/all_to_all | solution.py:44
  18.7 2.3 reduce-window.6
  21.6 4.3 %scatter_custom_fusion.1 = s32[128]{0:T(128)S(1)} fusion(s32[1024]{0:T(1024)S(1)} %bitcast.96, s32[1024]{0:T(1024)S(1)} %ne.90, s32[]{:T(128)} %constant.62.clone.1), kind=kCustom, calls=%fused_computation.113 | custom fusion | bytes 516 | tf_op jit(solution)/shard_map/scatter | solution.py:72
  26.0 4.3 %scatter_custom_fusion = s32[128]{0:T(128)S(1)} fusion(s32[1024]{0:T(1024)S(1)} %bitcast.97, s32[1024]{0:T(1024)S(1)} %iota.30, s32[]{:T(128)} %constant.62.clone.1), kind=kCustom, calls=%fused_computation.115 | custom fusion | bytes 516 | tf_op jit(solution)/shard_map/scatter | solution.py:70
  30.4 1.3 gather_fusion.1
  31.9 36.1 %all-to-all-done = bf16[16,128,256]{1,2,0:T(8,128)(2,1)S(1)} async-done(((bf16[16,128,256]{1,2,0:T(8,128)(2,1)}), bf16[16,128,256]{1,2,0:T(8,128)(2,1)S(1)}, u32[]{:S(2)}, u32[]{:S(2)}) %all-to-all-start) | async-done | bytes 1048608 | tf_op jit(solution)/shard_map/all_to_all | solution.py:44
  68.0 1.0 copy.51
  69.0 0.5 copy.68
  69.4 1.2 gather_fusion
  71.0 28.9 %all_to_all.31 = bf16[16,16,4224]{2,1,0:T(8,128)(2,1)S(1)} all-to-all(bf16[16,16,4224]{2,1,0:T(8,128)(2,1)S(1)} %bitcast.78), channel_id=1, replica_groups=mesh['dpc'=16,'core'=2,'expert'=16] {'dpc'}, dimensions={0} | all-to-all | bytes 4325376 | tf_op jit(solution)/shard_map/all_to_all | solution.py:88
  99.9 1.9 collective-permute-start
  101.8 4.3 %collective-permute-done = bf16[16,16,4224]{2,1,0:T(8,128)(2,1)} collective-permute-done((bf16[16,16,4224]{2,1,0:T(8,128)(2,1)S(1)}, bf16[16,16,4224]{2,1,0:T(8,128)(2,1)}, u32[]{:S(2)}, u32[]{:S(2)}) %collective-permute-start) | collective-permute-done | bytes 2162720 | tf_op jit(solution)/shard_map/ppermute | solution.py:89
  106.2 2.9 %maximum_select_fusion = bf16[2,16,16,4224]{3,2,1,0:T(8,128)(2,1)S(1)} fusion(bf16[1,16,16,4224]{3,2,1,0:T(8,128)(2,1)} %bitcast.9, bf16[1,16,16,4224]{3,2,1,0:T(8,128)(2,1)S(1)} %bitcast.77, pred[]{:T(512)S(6)} %eq.117), kind=kLoop, calls=%fused_computation.5 | loop fusion | flops 6488064 | bytes 8650753 | tf_op jit(solution)/shard_map/jit(_where)/select_n | solution.py:91
  109.2 0.8 fusion.13
  110.1 0.9 copy-done.2
  111.0 0.8 fusion.15
  111.8 1.0 multiply_reduce_fusion
  112.8 0.5 broadcast.342
  113.4 0.7 reduce.11
  114.1 3.7 %all_to_all.32 = bf16[2,2,128]{2,1,0:T(2,128)(2,1)S(1)} all-to-all(bf16[2,2,128]{2,1,0:T(2,128)(2,1)S(1)} %reshape.388), channel_id=1, replica_groups=mesh['dpc'=16,'core'=2,'expert'=16] {'core'}, dimensions={0} | all-to-all | bytes 2048 | tf_op jit(solution)/shard_map/all_to_all | solution.py:123
  118.0 0.8 multiply_convert_fusion.1
  118.7 0.7 fusion.23
  119.5 0.4 copy-done.4
  119.9 0.7 add_convert_fusion
  120.6 2.5 pad_maximum_fusion
  123.1 5.8 %all-to-all-start.2 = ((bf16[2,256,4096]{2,1,0:T(8,128)(2,1)}), bf16[2,256,4096]{2,1,0:T(8,128)(2,1)}, u32[]{:S(2)}, u32[]{:S(2)}) async-start(bf16[2,256,4096]{2,1,0:T(8,128)(2,1)} %bitcast.76), calls=%async_computation.2 | async-start | bytes 8388608 | tf_op jit(solution)/shard_map/all_to_all | solution.py:122
  129.0 4.2 %all-to-all-done.2 = bf16[2,256,4096]{2,1,0:T(8,128)(2,1)} async-done(((bf16[2,256,4096]{2,1,0:T(8,128)(2,1)}), bf16[2,256,4096]{2,1,0:T(8,128)(2,1)}, u32[]{:S(2)}, u32[]{:S(2)}) %all-to-all-start.2) | async-done | bytes 4194336 | tf_op jit(solution)/shard_map/all_to_all | solution.py:122
  133.2 3.3 %reduce_sum.52 = bf16[256,4096]{1,0:T(8,128)(2,1)S(1)} reduce(bf16[2,256,4096]{2,1,0:T(8,128)(2,1)} %all-to-all-done.2, bf16[]{:T(256)} %constant.74.clone.1), dimensions={0}, to_apply=%region_5.6 | reduce | flops 1048576 | bytes 6291458 | tf_op jit(solution)/shard_map/reduce_sum | solution.py:126
  136.5 1.5 pad_maximum_fusion.1
  138.0 5.7 %all-to-all-start.4 = ((bf16[16,16,4224]{2,1,0:T(8,128)(2,1)}), bf16[16,16,4224]{2,1,0:T(8,128)(2,1)S(1)}, u32[]{:S(2)}, u32[]{:S(2)}) async-start(bf16[16,16,4224]{2,1,0:T(8,128)(2,1)} %pad_maximum_fusion.1), calls=%async_computation.4 | async-start | bytes 4325376 | tf_op jit(solution)/shard_map/all_to_all | solution.py:132
  144.2 29.8 %all-to-all-done.4 = bf16[16,16,4224]{2,1,0:T(8,128)(2,1)S(1)} async-done(((bf16[16,16,4224]{2,1,0:T(8,128)(2,1)}), bf16[16,16,4224]{2,1,0:T(8,128)(2,1)S(1)}, u32[]{:S(2)}, u32[]{:S(2)}) %all-to-all-start.4) | async-done | bytes 2162720 | tf_op jit(solution)/shard_map/all_to_all | solution.py:132
  174.1 0.3 convolution_reduce_fusion
  174.4 0.5 fusion.8
  175.1 1.8 copy.54
  177.0 1.4 copy.55
  178.4 2.0 pad_maximum_fusion.2
  180.4 2.2 copy.56
  182.6 13.6 %all-to-all-start.5 = ((bf16[16,129,256]{2,1,0:T(8,128)(2,1)}), bf16[16,129,256]{2,1,0:T(8,128)(2,1)S(1)}, u32[]{:S(2)}, u32[]{:S(2)}) async-start(bf16[16,129,256]{2,1,0:T(8,128)(2,1)} %copy.56), calls=%async_computation.5 | async-start | bytes 2228224 | tf_op jit(solution)/shard_map/all_to_all | solution.py:164
  196.1 3.1 %fusion = bf16[1,192,2048]{2,1,0:T(8,128)(2,1)} fusion(bf16[512,192]{0,1:T(8,128)(2,1)S(1)} %get-tuple-element.30, bf16[512,4224]{1,0:T(8,128)(2,1)} %bitcast.86), kind=kOutput, calls=%fused_computation.13 | convolution fusion | flops 403046400 | bytes 3080192 | tf_op jit(solution)/shard_map/dot_general | solution.py:17
  199.2 3.1 %fusion.1 = bf16[1,192,2048]{2,1,0:T(8,128)(2,1)} fusion(bf16[512,192]{0,1:T(8,128)(2,1)S(1)} %get-tuple-element.31, bf16[512,4224]{1,0:T(8,128)(2,1)} %bitcast.87), kind=kOutput, calls=%fused_computation.14 | convolution fusion | flops 403046400 | bytes 3080192 | tf_op jit(solution)/shard_map/dot_general | solution.py:17
  202.3 3.2 %fusion.2 = bf16[1,192,2048]{2,1,0:T(8,128)(2,1)} fusion(bf16[512,192]{0,1:T(8,128)(2,1)S(1)} %copy-done.8, f32[512]{0:T(512)S(1)} %convert_reduce_fusion.1, bf16[512,4224]{1,0:T(8,128)(2,1)} %bitcast.88), kind=kOutput, calls=%fused_computation.15 | convolution fusion | flops 406192128 | bytes 3082240 | tf_op jit(solution)/shard_map/dot_general | solution.py:17
  205.5 42.3 %all-to-all-done.5 = bf16[16,129,256]{2,1,0:T(8,128)(2,1)S(1)} async-done(((bf16[16,129,256]{2,1,0:T(8,128)(2,1)}), bf16[16,129,256]{2,1,0:T(8,128)(2,1)S(1)}, u32[]{:S(2)}, u32[]{:S(2)}) %all-to-all-start.5) | async-done | bytes 1056800 | tf_op jit(solution)/shard_map/all_to_all | solution.py:164
  247.8 0.5 convert_reduce_fusion
  248.6 0.7 copy.60
  249.3 0.7 reshape_squeeze.3
  250.0 0.7 copy.59
  (72 shorter events, 3.7 us)
Async XLA Ops:
  0.6 111.2 %copy-start = (bf16[1,192,2048]{2,1,0:T(8,128)(2,1)S(1)}, bf16[1,192,2048]{2,1,0:T(8,128)(2,1)}, u32[]{:S(2)}) copy-start(bf16[1,192,2048]{2,1,0:T(8,128)(2,1)} %param.12) | copy-start | bytes 2359300
  0.6 17.4 %copy-start.5 = (s32[128,8]{0,1:T(8,128)S(1)}, s32[128,8]{0,1:T(8,128)}, u32[]{:S(2)}) copy-start(s32[128,8]{0,1:T(8,128)} %param.9) | copy-start | bytes 12292
  0.7 17.8 %copy-start.6 = (bf16[128,8]{0,1:T(8,128)(2,1)S(1)}, bf16[128,8]{0,1:T(8,128)(2,1)}, u32[]{:S(2)}) copy-start(bf16[128,8]{0,1:T(8,128)(2,1)} %param.8) | copy-start | bytes 6148
  2.8 65.1 %all-to-all-start = ((bf16[16,128,256]{1,2,0:T(8,128)(2,1)}), bf16[16,128,256]{1,2,0:T(8,128)(2,1)S(1)}, u32[]{:S(2)}, u32[]{:S(2)}) async-start(bf16[16,128,256]{1,2,0:T(8,128)(2,1)} %broadcast_in_dim.127), calls=%async_computation | async-start | bytes 2097152 | tf_op jit(solution)/shard_map/all_to_all | solution.py:44
  99.9 6.3 %collective-permute-start = (bf16[16,16,4224]{2,1,0:T(8,128)(2,1)S(1)}, bf16[16,16,4224]{2,1,0:T(8,128)(2,1)}, u32[]{:S(2)}, u32[]{:S(2)}) collective-permute-start(bf16[16,16,4224]{2,1,0:T(8,128)(2,1)S(1)} %all_to_all.31), channel_id=1, source_target_pairs={{0,16},{16,0},{1,17},{17,1},{2,18},{18,2},{3,19},{19,3},{4,20},{20... | collective-permute-start | bytes 6488072 | tf_op jit(solution)/shard_map/ppermute | solution.py:89
  106.2 3.1 %copy-start.3 = (bf16[1,192,2048]{2,1,0:T(8,128)(2,1)S(1)}, bf16[1,192,2048]{2,1,0:T(8,128)(2,1)}, u32[]{:S(2)}) copy-start(bf16[1,192,2048]{2,1,0:T(8,128)(2,1)} %param.11) | copy-start | bytes 2359300
  109.1 2.7 %copy-start.1 = (bf16[2,16,16,4224]{3,2,1,0:T(8,128)(2,1)}, bf16[2,16,16,4224]{3,2,1,0:T(8,128)(2,1)S(1)}, u32[]{:S(2)}) copy-start(bf16[2,16,16,4224]{3,2,1,0:T(8,128)(2,1)S(1)} %maximum_select_fusion) | copy-start | bytes 12976132
  109.2 1.7 copy-start.2
  112.8 6.7 %copy-start.7 = (bf16[512,192]{0,1:T(8,128)(2,1)}, bf16[512,192]{0,1:T(8,128)(2,1)S(1)}, u32[]{:S(2)}) copy-start(bf16[512,192]{0,1:T(8,128)(2,1)S(1)} %get-tuple-element.27) | copy-start | bytes 589828
  118.7 1.1 copy-start.4
  123.1 10.1 %all-to-all-start.2 = ((bf16[2,256,4096]{2,1,0:T(8,128)(2,1)}), bf16[2,256,4096]{2,1,0:T(8,128)(2,1)}, u32[]{:S(2)}, u32[]{:S(2)}) async-start(bf16[2,256,4096]{2,1,0:T(8,128)(2,1)} %bitcast.76), calls=%async_computation.2 | async-start | bytes 8388608 | tf_op jit(solution)/shard_map/all_to_all | solution.py:122
  138.0 36.1 %all-to-all-start.4 = ((bf16[16,16,4224]{2,1,0:T(8,128)(2,1)}), bf16[16,16,4224]{2,1,0:T(8,128)(2,1)S(1)}, u32[]{:S(2)}, u32[]{:S(2)}) async-start(bf16[16,16,4224]{2,1,0:T(8,128)(2,1)} %pad_maximum_fusion.1), calls=%async_computation.4 | async-start | bytes 4325376 | tf_op jit(solution)/shard_map/all_to_all | solution.py:132
  182.6 65.2 %all-to-all-start.5 = ((bf16[16,129,256]{2,1,0:T(8,128)(2,1)}), bf16[16,129,256]{2,1,0:T(8,128)(2,1)S(1)}, u32[]{:S(2)}, u32[]{:S(2)}) async-start(bf16[16,129,256]{2,1,0:T(8,128)(2,1)} %copy.56), calls=%async_computation.5 | async-start | bytes 2228224 | tf_op jit(solution)/shard_map/all_to_all | solution.py:164
  199.2 3.1 %copy-start.8 = (bf16[512,192]{0,1:T(8,128)(2,1)S(1)}, bf16[512,192]{0,1:T(8,128)(2,1)}, u32[]{:S(2)}) copy-start(bf16[512,192]{0,1:T(8,128)(2,1)} %copy-done.7) | copy-start | bytes 589828

commit v8 on v7

--- a/solution.py
+++ b/solution.py
@@ -117,17 +117,25 @@
     grad_up = contract_first(up_grad, slot_rows).astype(jnp.bfloat16)[None]
     grad_down = contract_first(hidden, scaled_grad).astype(jnp.bfloat16)[None]
 
-    core_index = lax.axis_index("core")
-    piece_buf = jnp.concatenate([scaled, row_grad], axis=1).reshape(cores, -1, 2 * feature_width)
-    pair = lax.all_to_all(piece_buf, "core", split_axis=0, concat_axis=0, tiled=True)
-    pair_terms = lax.all_to_all(
-        route_terms.reshape(cores, -1), "core", split_axis=0, concat_axis=0, tiled=True
-    )
-    pair_sum = jnp.sum(pair.astype(jnp.float32), axis=0).astype(jnp.bfloat16)
+    piece_buf = jnp.concatenate(
+        [scaled, row_grad, column_block(route_terms, jnp.bfloat16)], axis=1
+    ).reshape(cores, -1, row_width)
+    mine = jnp.where(first, piece_buf[0], piece_buf[1])
+    got = lax.ppermute(
+        jnp.where(first, piece_buf[1], piece_buf[0]),
+        "core",
+        [(k, (k + 1) % cores) for k in range(cores)],
+    )
+    pair_sum = (
+        mine[:, : 2 * feature_width].astype(jnp.float32) + got[:, : 2 * feature_width].astype(jnp.float32)
+    ).astype(jnp.bfloat16)
     lane = jnp.arange(PAD, dtype=jnp.int32)[None, :]
-    term_block = jnp.zeros((pair_terms.shape[1], PAD), jnp.bfloat16)
-    for k in range(cores):
-        term_block = jnp.where(lane == k, pair_terms[k][:, None], term_block)
+    term_col = 2 * feature_width
+    term_block = jnp.where(
+        lane == 0,
+        mine[:, term_col : term_col + 1],
+        jnp.where(lane == 1, got[:, term_col : term_col + 1], jnp.zeros((), jnp.bfloat16)),
+    )
     back_buf = jnp.concatenate([pair_sum, term_block], axis=1)
     back = lax.all_to_all(
         back_buf.reshape(chips, capacity, row_width),

time: 251 us -> 238 us (0.948)
  other arithmetic: 17.5 us -> 12.6 us
  blocking collectives: 32.6 us -> 28.9 us
  starting transfers between devices: 42.1 us -> 38.6 us
    all_to_all x1 -> x0, starting transfers between devices: 5.77 us -> none  [on_device(): lax.all_to_all(piece_buf, 'core', split_axis=0, concat_axis=0, tiled=True)]
    all_to_all x1 -> x0, waiting for transfers between devices: 4.16 us -> none  [on_device(): lax.all_to_all(piece_buf, 'core', split_axis=0, concat_axis=0, tiled=True)]
    ppermute x0 -> x1, waiting for transfers between devices: none -> 3.98 us  [on_device(): lax.ppermute(jnp.where(first, piece_buf[1], piece_buf[0]), 'core', [(k, (...]
    all_to_all x1 -> x0, blocking collectives: 3.69 us -> none  [on_device(): lax.all_to_all(route_terms.reshape(cores, -1), 'core', split_axis=0, conc...]
    reduce_sum x1 -> x0, other arithmetic: 3.31 us -> none  [on_device(): pair_sum = jnp.sum(pair.astype(jnp.float32), axis=0).astype(jnp.bfloat16)]
  transfers between devices with their start and end apart: 5 -> 5, of which waited for: 5 -> 5; matrix products, arithmetic and copies ran while one was open for 9% -> 10% of each run, Pallas kernels for 0% -> 0%
where the time goes in v8:
time: 238 us; the launch traced here: 237 us
  waiting for transfers between devices  117 us (49%)
  starting transfers between devices  38.6 us (16%)
  blocking collectives  28.9 us (12%)
  local copies, waits for them, and re-layouts  24.7 us (10%)
  matrix products  15 us (6%)
  other arithmetic  12.6 us (5%)
    all_to_all x1, waiting for transfers between devices, on_device(): lax.all_to_all(packed, 'expert', split_axis=0, concat_axis=0, tiled=True)  42.3 us
    all_to_all x1, waiting for transfers between devices, on_device(): lax.all_to_all(jnp.broadcast_to(both[None], (groups,) + both.shape), 'exp...  36.1 us
    all_to_all x1, waiting for transfers between devices, on_device(): lax.all_to_all(back_buf.reshape(chips, capacity, row_width), 'dpc', split...  29.8 us
    all_to_all x1, blocking collectives, on_device(): lax.all_to_all(spread(send_buf), 'dpc', split_axis=0, concat_axis=0, tile...  28.9 us
    all_to_all x1, starting transfers between devices, on_device(): lax.all_to_all(jnp.broadcast_to(both[None], (groups,) + both.shape), 'exp...  15.2 us
    all_to_all x1, starting transfers between devices, on_device(): lax.all_to_all(packed, 'expert', split_axis=0, concat_axis=0, tiled=True)  13.6 us
    dot_general x3, matrix products, contract_first(): lax.dot_general(left_side, right_side, (((0,), (0,)), ((), ())), preferre...  9.32 us
    all_to_all x1, starting transfers between devices, on_device(): lax.all_to_all(back_buf.reshape(chips, capacity, row_width), 'dpc', split...  5.83 us
  transfers between devices with their start and end apart: 5, of which 5 were waited for; matrix products, arithmetic and copies ran while one was open for 10% of the time, Pallas kernels for 0%

profile of v8, /device:TPU:16, one launch (start us, length us, event | category | flops | bytes accessed | tf_op | source)
XLA Modules:
  0.0 237.4 jit_solution(4120544441259280671)
XLA Ops:
  0.7 0.9 pad_maximum_fusion.3
  1.6 1.2 broadcast_in_dim.156
  2.8 15.2 %all-to-all-start = ((bf16[16,128,256]{1,2,0:T(8,128)(2,1)}), bf16[16,128,256]{1,2,0:T(8,128)(2,1)S(1)}, u32[]{:S(2)}, u32[]{:S(2)}) async-start(bf16[16,128,256]{1,2,0:T(8,128)(2,1)} %broadcast_in_dim.156), calls=%async_computation | async-start | bytes 2097152 | tf_op jit(solution)/shard_map/all_to_all | solution.py:44
  18.7 2.3 reduce-window.6
  21.0 0.3 slice_reduce_fusion.3
  21.3 0.2 reduce-window.9
  21.6 4.3 %scatter_custom_fusion.1 = s32[128]{0:T(128)S(1)} fusion(s32[1024]{0:T(1024)S(1)} %bitcast.93, s32[1024]{0:T(1024)S(1)} %ne.90, s32[]{:T(128)} %constant.60.clone.1), kind=kCustom, calls=%fused_computation.117 | custom fusion | bytes 516 | tf_op jit(solution)/shard_map/scatter | solution.py:72
  26.0 4.3 %scatter_custom_fusion = s32[128]{0:T(128)S(1)} fusion(s32[1024]{0:T(1024)S(1)} %bitcast.94, s32[1024]{0:T(1024)S(1)} %iota.33, s32[]{:T(128)} %constant.60.clone.1), kind=kCustom, calls=%fused_computation.119 | custom fusion | bytes 516 | tf_op jit(solution)/shard_map/scatter | solution.py:70
  30.4 1.3 gather_fusion.1
  31.9 36.1 %all-to-all-done = bf16[16,128,256]{1,2,0:T(8,128)(2,1)S(1)} async-done(((bf16[16,128,256]{1,2,0:T(8,128)(2,1)}), bf16[16,128,256]{1,2,0:T(8,128)(2,1)S(1)}, u32[]{:S(2)}, u32[]{:S(2)}) %all-to-all-start) | async-done | bytes 1048608 | tf_op jit(solution)/shard_map/all_to_all | solution.py:44
  68.0 1.0 copy.49
  69.0 0.5 copy.65
  69.4 1.2 gather_fusion
  71.0 28.9 %all_to_all.20 = bf16[16,16,4224]{2,1,0:T(8,128)(2,1)S(1)} all-to-all(bf16[16,16,4224]{2,1,0:T(8,128)(2,1)S(1)} %bitcast.76), channel_id=1, replica_groups=mesh['dpc'=16,'core'=2,'expert'=16] {'dpc'}, dimensions={0} | all-to-all | bytes 4325376 | tf_op jit(solution)/shard_map/all_to_all | solution.py:88
  99.9 1.9 collective-permute-start
  101.8 4.3 %collective-permute-done = bf16[16,16,4224]{2,1,0:T(8,128)(2,1)} collective-permute-done((bf16[16,16,4224]{2,1,0:T(8,128)(2,1)S(1)}, bf16[16,16,4224]{2,1,0:T(8,128)(2,1)}, u32[]{:S(2)}, u32[]{:S(2)}) %collective-permute-start) | collective-permute-done | bytes 2162720 | tf_op jit(solution)/shard_map/ppermute | solution.py:89
  106.2 2.9 %maximum_select_fusion = bf16[2,16,16,4224]{3,2,1,0:T(8,128)(2,1)S(1)} fusion(bf16[1,16,16,4224]{3,2,1,0:T(8,128)(2,1)} %bitcast.9, bf16[1,16,16,4224]{3,2,1,0:T(8,128)(2,1)S(1)} %bitcast.75, pred[]{:T(512)S(6)} %eq.120), kind=kLoop, calls=%fused_computation.5 | loop fusion | flops 6488064 | bytes 8650753 | tf_op jit(solution)/shard_map/jit(_where)/select_n | solution.py:91
  109.2 0.8 fusion.13
  110.1 0.9 copy-done.2
  111.0 0.8 fusion.15
  111.8 1.0 multiply_reduce_fusion
  113.0 0.8 multiply_convert_fusion.1
  113.7 0.8 fusion.23
  114.5 0.8 add_convert_fusion.1
  115.3 0.4 pad_maximum_fusion
  115.7 0.4 broadcast_select_fusion.1
  116.1 2.0 collective-permute-start.1
  118.2 4.0 %collective-permute-done.1 = bf16[256,4224]{1,0:T(8,128)(2,1)S(1)} collective-permute-done((bf16[256,4224]{1,0:T(8,128)(2,1)S(1)}, bf16[256,4224]{1,0:T(8,128)(2,1)S(1)}, u32[]{:S(2)}, u32[]{:S(2)}) %collective-permute-start.1) | collective-permute-done | bytes 2162720 | tf_op jit(solution)/shard_map/ppermute | solution.py:124
  122.5 0.6 add_convert_fusion
  123.1 1.5 pad_maximum_fusion.1
  124.6 5.8 %all-to-all-start.2 = ((bf16[16,16,4224]{2,1,0:T(8,128)(2,1)}), bf16[16,16,4224]{2,1,0:T(8,128)(2,1)S(1)}, u32[]{:S(2)}, u32[]{:S(2)}) async-start(bf16[16,16,4224]{2,1,0:T(8,128)(2,1)} %bitcast.14), calls=%async_computation.2 | async-start | bytes 4325376 | tf_op jit(solution)/shard_map/all_to_all | solution.py:140
  131.0 29.8 %all-to-all-done.2 = bf16[16,16,4224]{2,1,0:T(8,128)(2,1)S(1)} async-done(((bf16[16,16,4224]{2,1,0:T(8,128)(2,1)}), bf16[16,16,4224]{2,1,0:T(8,128)(2,1)S(1)}, u32[]{:S(2)}, u32[]{:S(2)}) %all-to-all-start.2) | async-done | bytes 2162720 | tf_op jit(solution)/shard_map/all_to_all | solution.py:140
  160.8 0.3 convolution_reduce_fusion
  161.1 0.5 fusion.8
  161.6 0.2 copy.61
  161.9 1.8 copy.51
  163.8 1.4 copy.52
  165.1 2.0 pad_maximum_fusion.2
  167.1 2.2 copy.53
  169.3 13.6 %all-to-all-start.3 = ((bf16[16,129,256]{2,1,0:T(8,128)(2,1)}), bf16[16,129,256]{2,1,0:T(8,128)(2,1)S(1)}, u32[]{:S(2)}, u32[]{:S(2)}) async-start(bf16[16,129,256]{2,1,0:T(8,128)(2,1)} %copy.53), calls=%async_computation.3 | async-start | bytes 2228224 | tf_op jit(solution)/shard_map/all_to_all | solution.py:172
  182.9 3.1 %fusion = bf16[1,192,2048]{2,1,0:T(8,128)(2,1)} fusion(bf16[512,192]{0,1:T(8,128)(2,1)S(1)} %get-tuple-element.30, bf16[512,4224]{1,0:T(8,128)(2,1)} %bitcast.83), kind=kOutput, calls=%fused_computation.14 | convolution fusion | flops 403046400 | bytes 3080192 | tf_op jit(solution)/shard_map/dot_general | solution.py:17
  186.0 3.1 %fusion.1 = bf16[1,192,2048]{2,1,0:T(8,128)(2,1)} fusion(bf16[512,192]{0,1:T(8,128)(2,1)S(1)} %get-tuple-element.31, bf16[512,4224]{1,0:T(8,128)(2,1)} %bitcast.84), kind=kOutput, calls=%fused_computation.15 | convolution fusion | flops 403046400 | bytes 3080192 | tf_op jit(solution)/shard_map/dot_general | solution.py:17
  189.0 3.2 %fusion.2 = bf16[1,192,2048]{2,1,0:T(8,128)(2,1)} fusion(bf16[512,192]{0,1:T(8,128)(2,1)S(1)} %copy-done.7, f32[512]{0:T(512)S(1)} %convert_reduce_fusion.1, bf16[512,4224]{1,0:T(8,128)(2,1)} %bitcast.85), kind=kOutput, calls=%fused_computation.16 | convolution fusion | flops 406192128 | bytes 3082240 | tf_op jit(solution)/shard_map/dot_general | solution.py:17
  192.2 42.3 %all-to-all-done.3 = bf16[16,129,256]{2,1,0:T(8,128)(2,1)S(1)} async-done(((bf16[16,129,256]{2,1,0:T(8,128)(2,1)}), bf16[16,129,256]{2,1,0:T(8,128)(2,1)S(1)}, u32[]{:S(2)}, u32[]{:S(2)}) %all-to-all-start.3) | async-done | bytes 1056800 | tf_op jit(solution)/shard_map/all_to_all | solution.py:172
  234.5 0.5 convert_reduce_fusion
  235.3 0.7 copy.57
  236.0 0.7 reshape_squeeze.3
  236.7 0.7 copy.56
  (65 shorter events, 3.1 us)
Async XLA Ops:
  0.6 111.2 %copy-start = (bf16[1,192,2048]{2,1,0:T(8,128)(2,1)S(1)}, bf16[1,192,2048]{2,1,0:T(8,128)(2,1)}, u32[]{:S(2)}) copy-start(bf16[1,192,2048]{2,1,0:T(8,128)(2,1)} %param.12) | copy-start | bytes 2359300
  0.6 17.4 %copy-start.4 = (s32[128,8]{0,1:T(8,128)S(1)}, s32[128,8]{0,1:T(8,128)}, u32[]{:S(2)}) copy-start(s32[128,8]{0,1:T(8,128)} %param.9) | copy-start | bytes 12292
  0.7 17.8 %copy-start.5 = (bf16[128,8]{0,1:T(8,128)(2,1)S(1)}, bf16[128,8]{0,1:T(8,128)(2,1)}, u32[]{:S(2)}) copy-start(bf16[128,8]{0,1:T(8,128)(2,1)} %param.8) | copy-start | bytes 6148
  2.8 65.1 %all-to-all-start = ((bf16[16,128,256]{1,2,0:T(8,128)(2,1)}), bf16[16,128,256]{1,2,0:T(8,128)(2,1)S(1)}, u32[]{:S(2)}, u32[]{:S(2)}) async-start(bf16[16,128,256]{1,2,0:T(8,128)(2,1)} %broadcast_in_dim.156), calls=%async_computation | async-start | bytes 2097152 | tf_op jit(solution)/shard_map/all_to_all | solution.py:44
  99.9 6.3 %collective-permute-start = (bf16[16,16,4224]{2,1,0:T(8,128)(2,1)S(1)}, bf16[16,16,4224]{2,1,0:T(8,128)(2,1)}, u32[]{:S(2)}, u32[]{:S(2)}) collective-permute-start(bf16[16,16,4224]{2,1,0:T(8,128)(2,1)S(1)} %all_to_all.20), channel_id=1, source_target_pairs={{0,16},{16,0},{1,17},{17,1},{2,18},{18,2},{3,19},{19,3},{4,20},{20... | collective-permute-start | bytes 6488072 | tf_op jit(solution)/shard_map/ppermute | solution.py:89
  106.2 3.1 %copy-start.3 = (bf16[1,192,2048]{2,1,0:T(8,128)(2,1)S(1)}, bf16[1,192,2048]{2,1,0:T(8,128)(2,1)}, u32[]{:S(2)}) copy-start(bf16[1,192,2048]{2,1,0:T(8,128)(2,1)} %param.11) | copy-start | bytes 2359300
  109.1 2.7 %copy-start.1 = (bf16[2,16,16,4224]{3,2,1,0:T(8,128)(2,1)}, bf16[2,16,16,4224]{3,2,1,0:T(8,128)(2,1)S(1)}, u32[]{:S(2)}) copy-start(bf16[2,16,16,4224]{3,2,1,0:T(8,128)(2,1)S(1)} %maximum_select_fusion) | copy-start | bytes 12976132
  109.2 1.7 copy-start.2
  112.8 1.7 copy-start.6
  116.1 6.1 %collective-permute-start.1 = (bf16[256,4224]{1,0:T(8,128)(2,1)S(1)}, bf16[256,4224]{1,0:T(8,128)(2,1)S(1)}, u32[]{:S(2)}, u32[]{:S(2)}) collective-permute-start(bf16[256,4224]{1,0:T(8,128)(2,1)S(1)} %get-tuple-element.29), channel_id=1, source_target_pairs={{0,16},{16,0},{1,17},{17,1},{2,18},{18,2},{3,19},{19,3},{4,20},{20... | collective-permute-start | bytes 6488072 | tf_op jit(solution)/shard_map/ppermute | solution.py:124
  124.6 36.2 %all-to-all-start.2 = ((bf16[16,16,4224]{2,1,0:T(8,128)(2,1)}), bf16[16,16,4224]{2,1,0:T(8,128)(2,1)S(1)}, u32[]{:S(2)}, u32[]{:S(2)}) async-start(bf16[16,16,4224]{2,1,0:T(8,128)(2,1)} %bitcast.14), calls=%async_computation.2 | async-start | bytes 4325376 | tf_op jit(solution)/shard_map/all_to_all | solution.py:140
  169.3 65.2 %all-to-all-start.3 = ((bf16[16,129,256]{2,1,0:T(8,128)(2,1)}), bf16[16,129,256]{2,1,0:T(8,128)(2,1)S(1)}, u32[]{:S(2)}, u32[]{:S(2)}) async-start(bf16[16,129,256]{2,1,0:T(8,128)(2,1)} %copy.53), calls=%async_computation.3 | async-start | bytes 2228224 | tf_op jit(solution)/shard_map/all_to_all | solution.py:172
  185.9 3.1 %copy-start.7 = (bf16[512,192]{0,1:T(8,128)(2,1)S(1)}, bf16[512,192]{0,1:T(8,128)(2,1)}, u32[]{:S(2)}) copy-start(bf16[512,192]{0,1:T(8,128)(2,1)} %copy-done.6) | copy-start | bytes 589828

commit v9 on v8

--- a/solution.py
+++ b/solution.py
@@ -87,10 +87,7 @@
     )
     half_buf = lax.all_to_all(spread(send_buf), "dpc", split_axis=0, concat_axis=0, tiled=True)
     other_buf = lax.ppermute(half_buf, "core", [(k, (k + 1) % cores) for k in range(cores)])
-    first = lax.axis_index("core") == 0
-    recv_buf = jnp.where(
-        first, jnp.stack([half_buf, other_buf]), jnp.stack([other_buf, half_buf])
-    ).reshape(-1, row_width)
+    recv_buf = jnp.stack([half_buf, other_buf]).reshape(-1, row_width)
     slot_rows = recv_buf[:, :feature_width]
     slot_grads = recv_buf[:, feature_width : 2 * feature_width]
     slot_scale = recv_buf[:, 2 * feature_width]
@@ -120,9 +117,9 @@
     piece_buf = jnp.concatenate(
         [scaled, row_grad, column_block(route_terms, jnp.bfloat16)], axis=1
     ).reshape(cores, -1, row_width)
-    mine = jnp.where(first, piece_buf[0], piece_buf[1])
+    mine = piece_buf[0]
     got = lax.ppermute(
-        jnp.where(first, piece_buf[1], piece_buf[0]),
+        piece_buf[1],
         "core",
         [(k, (k + 1) % cores) for k in range(cores)],
     )

time: 238 us -> 235 us (0.987)
  other arithmetic: 12.6 us -> 9.45 us
    select_n x2 -> x0, other arithmetic: 3.33 us -> none  [the longest x1 2.94 us: on_device(): jnp.where(first, jnp.stack([half_buf, other_buf]), jnp.stack([other_buf,...]
where the time goes in v9:
time: 235 us
  waiting for transfers between devices  116 us (49%)
  starting transfers between devices  38.6 us (16%)
  blocking collectives  28.9 us (12%)
  local copies, waits for them, and re-layouts  25.3 us (11%)
  matrix products  15.1 us (6%)
  other arithmetic  9.45 us (4%)
    all_to_all x1, waiting for transfers between devices, on_device(): lax.all_to_all(packed, 'expert', split_axis=0, concat_axis=0, tiled=True)  42.3 us
    all_to_all x1, waiting for transfers between devices, on_device(): lax.all_to_all(jnp.broadcast_to(both[None], (groups,) + both.shape), 'exp...  36.1 us
    all_to_all x1, waiting for transfers between devices, on_device(): lax.all_to_all(back_buf.reshape(chips, capacity, row_width), 'dpc', split...  29.8 us
    all_to_all x1, blocking collectives, on_device(): lax.all_to_all(spread(send_buf), 'dpc', split_axis=0, concat_axis=0, tile...  28.9 us
    all_to_all x1, starting transfers between devices, on_device(): lax.all_to_all(jnp.broadcast_to(both[None], (groups,) + both.shape), 'exp...  15.2 us
    all_to_all x1, starting transfers between devices, on_device(): lax.all_to_all(packed, 'expert', split_axis=0, concat_axis=0, tiled=True)  13.6 us
    dot_general x3, matrix products, contract_first(): lax.dot_general(left_side, right_side, (((0,), (0,)), ((), ())), preferre...  9.33 us
    all_to_all x1, starting transfers between devices, on_device(): lax.all_to_all(back_buf.reshape(chips, capacity, row_width), 'dpc', split...  5.83 us
  transfers between devices with their start and end apart: 5, of which 5 were waited for; matrix products, arithmetic and copies ran while one was open for 10% of the time, Pallas kernels for 0%

profile of v9, /device:TPU:16, one launch (start us, length us, event | category | flops | bytes accessed | tf_op | source)
XLA Modules:
  0.0 234.7 jit_solution(11381738354026656189)
XLA Ops:
  0.7 0.9 pad_maximum_fusion.6
  1.6 1.2 broadcast_in_dim.156
  2.8 15.2 %all-to-all-start = ((bf16[16,128,256]{1,2,0:T(8,128)(2,1)}), bf16[16,128,256]{1,2,0:T(8,128)(2,1)S(1)}, u32[]{:S(2)}, u32[]{:S(2)}) async-start(bf16[16,128,256]{1,2,0:T(8,128)(2,1)} %broadcast_in_dim.156), calls=%async_computation | async-start | bytes 2097152 | tf_op jit(solution)/shard_map/all_to_all | solution.py:44
  18.7 2.3 reduce-window.6
  21.0 0.3 slice_reduce_fusion.3
  21.3 0.2 reduce-window.9
  21.6 4.3 %scatter_custom_fusion.1 = s32[128]{0:T(128)S(1)} fusion(s32[1024]{0:T(1024)S(1)} %bitcast.94, s32[1024]{0:T(1024)S(1)} %ne.90, s32[]{:T(128)} %constant.57.clone.1), kind=kCustom, calls=%fused_computation.117 | custom fusion | bytes 516 | tf_op jit(solution)/shard_map/scatter | solution.py:72
  26.0 4.3 %scatter_custom_fusion = s32[128]{0:T(128)S(1)} fusion(s32[1024]{0:T(1024)S(1)} %bitcast.95, s32[1024]{0:T(1024)S(1)} %iota.33, s32[]{:T(128)} %constant.57.clone.1), kind=kCustom, calls=%fused_computation.119 | custom fusion | bytes 516 | tf_op jit(solution)/shard_map/scatter | solution.py:70
  30.4 1.3 gather_fusion.1
  31.9 36.1 %all-to-all-done = bf16[16,128,256]{1,2,0:T(8,128)(2,1)S(1)} async-done(((bf16[16,128,256]{1,2,0:T(8,128)(2,1)}), bf16[16,128,256]{1,2,0:T(8,128)(2,1)S(1)}, u32[]{:S(2)}, u32[]{:S(2)}) %all-to-all-start) | async-done | bytes 1048608 | tf_op jit(solution)/shard_map/all_to_all | solution.py:44
  68.0 1.0 copy.49
  69.0 0.5 copy.65
  69.4 1.2 gather_fusion
  71.0 28.9 %all_to_all.20 = bf16[16,16,4224]{2,1,0:T(8,128)(2,1)S(1)} all-to-all(bf16[16,16,4224]{2,1,0:T(8,128)(2,1)S(1)} %bitcast.76), channel_id=1, replica_groups=mesh['dpc'=16,'core'=2,'expert'=16] {'dpc'}, dimensions={0} | all-to-all | bytes 4325376 | tf_op jit(solution)/shard_map/all_to_all | solution.py:88
  99.9 1.9 collective-permute-start
  101.8 4.2 %collective-permute-done = bf16[16,16,4224]{2,1,0:T(8,128)(2,1)S(1)} collective-permute-done((bf16[16,16,4224]{2,1,0:T(8,128)(2,1)S(1)}, bf16[16,16,4224]{2,1,0:T(8,128)(2,1)S(1)}, u32[]{:S(2)}, u32[]{:S(2)}) %collective-permute-start) | collective-permute-done | bytes 2162720 | tf_op jit(solution)/shard_map/ppermute | solution.py:89
  106.0 0.4 pad_maximum_fusion
  106.6 0.6 copy-done.3
  107.2 0.8 fusion.13
  108.0 0.9 copy-done.2
  108.9 0.8 fusion.15
  109.7 1.0 multiply_reduce_fusion
  110.9 0.8 multiply_convert_fusion.1
  111.6 0.8 fusion.23
  112.4 0.8 add_convert_fusion.1
  113.2 0.2 pad_maximum_fusion.1
  113.4 2.0 collective-permute-start.1
  115.5 4.0 %collective-permute-done.1 = bf16[256,4224]{1,0:T(8,128)(2,1)S(1)} collective-permute-done((bf16[256,4224]{1,0:T(8,128)(2,1)S(1)}, bf16[256,4224]{1,0:T(8,128)(2,1)S(1)}, u32[]{:S(2)}, u32[]{:S(2)}) %collective-permute-start.1) | collective-permute-done | bytes 2162720 | tf_op jit(solution)/shard_map/ppermute | solution.py:121
  119.8 0.6 add_convert_fusion
  120.4 1.5 pad_maximum_fusion.3
  121.9 5.8 %all-to-all-start.2 = ((bf16[16,16,4224]{2,1,0:T(8,128)(2,1)}), bf16[16,16,4224]{2,1,0:T(8,128)(2,1)S(1)}, u32[]{:S(2)}, u32[]{:S(2)}) async-start(bf16[16,16,4224]{2,1,0:T(8,128)(2,1)} %bitcast.14), calls=%async_computation.2 | async-start | bytes 4325376 | tf_op jit(solution)/shard_map/all_to_all | solution.py:137
  128.3 29.8 %all-to-all-done.2 = bf16[16,16,4224]{2,1,0:T(8,128)(2,1)S(1)} async-done(((bf16[16,16,4224]{2,1,0:T(8,128)(2,1)}), bf16[16,16,4224]{2,1,0:T(8,128)(2,1)S(1)}, u32[]{:S(2)}, u32[]{:S(2)}) %all-to-all-start.2) | async-done | bytes 2162720 | tf_op jit(solution)/shard_map/all_to_all | solution.py:137
  158.1 0.3 convolution_reduce_fusion
  158.4 0.5 fusion.8
  158.9 0.2 copy.61
  159.1 1.8 copy.51
  161.0 1.4 copy.52
  162.4 2.0 pad_maximum_fusion.5
  164.4 2.2 copy.53
  166.6 13.6 %all-to-all-start.3 = ((bf16[16,129,256]{2,1,0:T(8,128)(2,1)}), bf16[16,129,256]{2,1,0:T(8,128)(2,1)S(1)}, u32[]{:S(2)}, u32[]{:S(2)}) async-start(bf16[16,129,256]{2,1,0:T(8,128)(2,1)} %copy.53), calls=%async_computation.3 | async-start | bytes 2228224 | tf_op jit(solution)/shard_map/all_to_all | solution.py:169
  180.2 3.1 %fusion = bf16[1,192,2048]{2,1,0:T(8,128)(2,1)} fusion(bf16[512,192]{0,1:T(8,128)(2,1)S(1)} %get-tuple-element.28, bf16[512,4224]{1,0:T(8,128)(2,1)} %bitcast.83), kind=kOutput, calls=%fused_computation.13 | convolution fusion | flops 403046400 | bytes 3080192 | tf_op jit(solution)/shard_map/dot_general | solution.py:17
  183.2 3.1 %fusion.1 = bf16[1,192,2048]{2,1,0:T(8,128)(2,1)} fusion(bf16[512,192]{0,1:T(8,128)(2,1)S(1)} %get-tuple-element.29, bf16[512,4224]{1,0:T(8,128)(2,1)} %bitcast.84), kind=kOutput, calls=%fused_computation.14 | convolution fusion | flops 403046400 | bytes 3080192 | tf_op jit(solution)/shard_map/dot_general | solution.py:17
  186.3 3.2 %fusion.2 = bf16[1,192,2048]{2,1,0:T(8,128)(2,1)} fusion(bf16[512,192]{0,1:T(8,128)(2,1)S(1)} %copy-done.7, f32[512]{0:T(512)S(1)} %convert_reduce_fusion.1, bf16[512,4224]{1,0:T(8,128)(2,1)} %bitcast.85), kind=kOutput, calls=%fused_computation.15 | convolution fusion | flops 406192128 | bytes 3082240 | tf_op jit(solution)/shard_map/dot_general | solution.py:17
  189.5 42.3 %all-to-all-done.3 = bf16[16,129,256]{2,1,0:T(8,128)(2,1)S(1)} async-done(((bf16[16,129,256]{2,1,0:T(8,128)(2,1)}), bf16[16,129,256]{2,1,0:T(8,128)(2,1)S(1)}, u32[]{:S(2)}, u32[]{:S(2)}) %all-to-all-start.3) | async-done | bytes 1056800 | tf_op jit(solution)/shard_map/all_to_all | solution.py:169
  231.8 0.5 convert_reduce_fusion
  232.6 0.7 copy.57
  233.3 0.7 reshape_squeeze.3
  234.0 0.7 copy.56
  (64 shorter events, 3.1 us)
Async XLA Ops:
  0.6 109.1 %copy-start = (bf16[1,192,2048]{2,1,0:T(8,128)(2,1)S(1)}, bf16[1,192,2048]{2,1,0:T(8,128)(2,1)}, u32[]{:S(2)}) copy-start(bf16[1,192,2048]{2,1,0:T(8,128)(2,1)} %param.12) | copy-start | bytes 2359300
  0.6 17.4 %copy-start.4 = (s32[128,8]{0,1:T(8,128)S(1)}, s32[128,8]{0,1:T(8,128)}, u32[]{:S(2)}) copy-start(s32[128,8]{0,1:T(8,128)} %param.9) | copy-start | bytes 12292
  0.7 17.8 %copy-start.5 = (bf16[128,8]{0,1:T(8,128)(2,1)S(1)}, bf16[128,8]{0,1:T(8,128)(2,1)}, u32[]{:S(2)}) copy-start(bf16[128,8]{0,1:T(8,128)(2,1)} %param.8) | copy-start | bytes 6148
  2.8 65.1 %all-to-all-start = ((bf16[16,128,256]{1,2,0:T(8,128)(2,1)}), bf16[16,128,256]{1,2,0:T(8,128)(2,1)S(1)}, u32[]{:S(2)}, u32[]{:S(2)}) async-start(bf16[16,128,256]{1,2,0:T(8,128)(2,1)} %broadcast_in_dim.156), calls=%async_computation | async-start | bytes 2097152 | tf_op jit(solution)/shard_map/all_to_all | solution.py:44
  99.9 6.1 %collective-permute-start = (bf16[16,16,4224]{2,1,0:T(8,128)(2,1)S(1)}, bf16[16,16,4224]{2,1,0:T(8,128)(2,1)S(1)}, u32[]{:S(2)}, u32[]{:S(2)}) collective-permute-start(bf16[16,16,4224]{2,1,0:T(8,128)(2,1)S(1)} %all_to_all.20), channel_id=1, source_target_pairs={{0,16},{16,0},{1,17},{17,1},{2,18},{18,2},{3,19},{19,3},{4,20},{20... | collective-permute-start | bytes 6488072 | tf_op jit(solution)/shard_map/ppermute | solution.py:89
  106.0 1.1 copy-start.3
  106.5 3.3 %copy-start.1 = (bf16[2,16,16,4224]{3,2,1,0:T(8,128)(2,1)}, bf16[2,16,16,4224]{3,2,1,0:T(8,128)(2,1)S(1)}, u32[]{:S(2)}) copy-start(bf16[2,16,16,4224]{3,2,1,0:T(8,128)(2,1)S(1)} %pad_maximum_fusion) | copy-start | bytes 12976132
  107.2 1.7 copy-start.2
  110.7 1.7 copy-start.6
  113.4 6.1 %collective-permute-start.1 = (bf16[256,4224]{1,0:T(8,128)(2,1)S(1)}, bf16[256,4224]{1,0:T(8,128)(2,1)S(1)}, u32[]{:S(2)}, u32[]{:S(2)}) collective-permute-start(bf16[256,4224]{1,0:T(8,128)(2,1)S(1)} %pad_maximum_fusion.1), channel_id=1, source_target_pairs={{0,16},{16,0},{1,17},{17,1},{2,18},{18,2},{3,19},{19,3},{4,20},{20... | collective-permute-start | bytes 6488072 | tf_op jit(solution)/shard_map/ppermute | solution.py:121
  121.9 36.2 %all-to-all-start.2 = ((bf16[16,16,4224]{2,1,0:T(8,128)(2,1)}), bf16[16,16,4224]{2,1,0:T(8,128)(2,1)S(1)}, u32[]{:S(2)}, u32[]{:S(2)}) async-start(bf16[16,16,4224]{2,1,0:T(8,128)(2,1)} %bitcast.14), calls=%async_computation.2 | async-start | bytes 4325376 | tf_op jit(solution)/shard_map/all_to_all | solution.py:137
  166.6 65.2 %all-to-all-start.3 = ((bf16[16,129,256]{2,1,0:T(8,128)(2,1)}), bf16[16,129,256]{2,1,0:T(8,128)(2,1)S(1)}, u32[]{:S(2)}, u32[]{:S(2)}) async-start(bf16[16,129,256]{2,1,0:T(8,128)(2,1)} %copy.53), calls=%async_computation.3 | async-start | bytes 2228224 | tf_op jit(solution)/shard_map/all_to_all | solution.py:169
  183.2 3.1 %copy-start.7 = (bf16[512,192]{0,1:T(8,128)(2,1)S(1)}, bf16[512,192]{0,1:T(8,128)(2,1)}, u32[]{:S(2)}) copy-start(bf16[512,192]{0,1:T(8,128)(2,1)} %copy-done.6) | copy-start | bytes 589828
